TPU v7x, 256 devices: a whole 4x4x8 slice. The times are simulated.
256 devices in a mesh: expert: 128 (over z, x, y), dp: 2 (over core).
Axes of the slice: x: 4, y: 4, z: 8, core: 2. Of those that a mesh axis runs over, the one named last changes fastest.
Arguments:
- hidden: bfloat16 [32768, 8, 1024], P(('expert', 'dp')), may hold values from -8 to 8
- routes: int32 [32768, 8], P(('expert', 'dp')), may hold values from 0 to 127, as said below
- slots: int32 [32768, 8], P(('expert', 'dp')), may hold values from 0 to 15, as said below
- down_weight: bfloat16 [128, 1024, 7168], P('expert', None, 'dp'), may hold values from -0.1875 to 0.1875
- omega: bfloat16 [128, 1024, 256], P('expert'), may hold values from -0.1875 to 0.1875
Outputs:
- whitening: float32 [128, 1024, 1024], P('expert', 'dp')
- basis: float32 [2, 3584, 256], P('dp', 'expert')
Inputs may be any that keep to these rules, and one draw needn't show every extreme that they name: `routes`: each token names 8 different experts. Among the tokens of one device no expert is named more than 16 times, and one expert is named exactly 16 times by the tokens of every device. Among the tokens of one device, the pairs that name one expert have different slots.
All inputs are finite; a program needn't handle non-finite values.
Results may differ from a plain program's by a relative error of at most 0.0032.
Values may be sent and summed in bfloat16 or wider, within the bound.
No kernel may reach another device: no remote copies, remote signals or barrier semaphores. Data moves between devices by JAX's collectives and lax.ppermute only.
A program may use at most 128 MiB of HBM per device.

v0:
```python
import math

import jax
import jax.numpy as jnp
from jax import lax
from jax.sharding import PartitionSpec as P

damping = 0.1
jitter = 1e-06


def contract(left, right):
    return lax.dot_general(
        left, right, (((0,), (0,)), ((), ())), preferred_element_type=jnp.float32
    )


def local(hidden, routes, slots, down_weight, omega):
    n_exp = lax.axis_size("expert")
    n_dp = lax.axis_size("dp")
    tok_rows, n_route, hid_width = hidden.shape
    capacity = 2 * tok_rows * n_route // n_exp
    n_slot = n_exp * n_dp * capacity
    slot_index = (routes * capacity + slots).reshape(-1)
    outgoing = jnp.zeros((n_exp * capacity, hid_width), jnp.bfloat16)
    outgoing = (
        outgoing.at[slot_index]
        .set(hidden.reshape(-1, hid_width))
        .reshape(n_exp, capacity, hid_width)
    )
    received = lax.all_to_all(outgoing, "expert", split_axis=0, concat_axis=0, tiled=True).reshape(
        n_exp * capacity, hid_width
    )
    gram_mat = lax.psum(contract(received, received), "dp") / n_slot
    identity_mat = jnp.eye(hid_width, dtype=jnp.float32)
    damped = gram_mat + (damping * jnp.mean(jnp.diagonal(gram_mat)) + jitter) * identity_mat
    whitening = jnp.linalg.cholesky(damped)
    test_mat = jnp.dot(
        whitening, omega[0].astype(jnp.float32), precision=lax.Precision.HIGHEST
    ).astype(jnp.bfloat16)
    down_half = down_weight[0]
    half_cols = down_half.shape[1]
    row_share = half_cols // n_exp
    whole_half = lax.psum(contract(down_half, test_mat), "expert")
    small_gram = lax.psum(jnp.dot(whole_half.T, whole_half, precision=lax.Precision.HIGHEST), "dp")
    sketch = lax.dynamic_slice_in_dim(
        whole_half, lax.axis_index("expert") * row_share, row_share, 0
    )
    qr_factor = jnp.linalg.cholesky(small_gram)
    basis_rows = jax.scipy.linalg.solve_triangular(qr_factor, sketch.T, lower=True).T * math.sqrt(
        half_cols * n_dp
    )
    own_rows = lax.dynamic_slice_in_dim(
        whitening, lax.axis_index("dp") * (hid_width // n_dp), hid_width // n_dp, 0
    )
    return (own_rows[None], basis_rows[None])


def solution(mesh):
    placed = (
        P(("expert", "dp"), None, None),
        P(("expert", "dp"), None),
        P(("expert", "dp"), None),
        P("expert", None, "dp"),
        P("expert", None, None),
    )
    return jax.shard_map(
        local,
        mesh=mesh,
        in_specs=placed,
        out_specs=(P("expert", "dp", None), P("dp", "expert", None)),
        check_vma=False,
    )
```

profile of v0, /device:TPU:1, one launch (start us, length us, event | category | flops | bytes accessed | tf_op | source)
XLA Modules:
  0.0 775.2 jit_solution(16030494886946830001)
XLA Ops:
  8.8 7.9 %scatter_custom_fusion = bf16[2048,1024]{1,0:T(8,128)(2,1)} fusion(s32[1024]{0:T(1024)S(1)} %bitcast.111, bf16[128,8,1024]{2,1,0:T(8,128)(2,1)S(1)} %copy-done, bf16[]{:T(256)} %constant.347.clone.1), kind=kCustom, calls=%fused_computation.14 | custom fusion | bytes 6291458 | tf_op jit(solution)/shard_map/scatter | solution.py:28
  16.7 110.1 %all_to_all.5 = bf16[128,16,1024]{2,1,0:T(8,128)(2,1)S(1)} all-to-all(bf16[128,16,1024]{2,1,0:T(8,128)(2,1)} %bitcast.109), channel_id=1, replica_groups=mesh['expert'=128,'dp'=2] {'expert'}, dimensions={0} | all-to-all | bytes 8388608 | tf_op jit(solution)/shard_map/all_to_all | solution.py:31
  126.7 6.2 convolution_bitcast_fusion
  133.0 38.1 %all-reduce.6.cloned.1.call-done = f32[1024,1024]{0,1:T(8,128)} async-done(((f32[1024,1024]{0,1:T(8,128)}), f32[1024,1024]{0,1:T(8,128)}) %all-reduce.6.cloned.1.call-update) | async-done | bytes 4194320 | tf_op jit(solution)/shard_map/psum | solution.py:34
  171.2 5.0 broadcast_multiply_fusion
  176.2 16.8 %gather_fusion = f32[1024]{0:T(1024)S(1)} fusion(f32[1024,1024]{0,1:T(8,128)} %broadcast_multiply_fusion, s32[1024]{0:T(1024)S(1)} %bitcast.108), kind=kCustom, calls=%fused_computation | custom fusion | bytes 16384 | tf_op jit(solution)/shard_map/jit(diagonal)/cond/branch_0_fun/gather | solution.py:36
  194.3 5.0 select_add_fusion
  199.3 5.5 copy.56
  204.8 4.5 fusion.5
  211.2 11.7 %cholesky.249 = f32[128,128]{1,0:T(8,128)S(1)} custom-call(f32[128,128]{1,0:T(8,128)S(1)} %cholesky.650), custom_call_target="Cholesky" | custom-call | tf_op jit(solution)/shard_map/jit(cholesky)/cholesky | solution.py:37
  223.0 9.8 %custom-call.67 = f32[1,128,128]{1,2,0:T(8,128)S(1)} custom-call(f32[1,128,128]{2,1,0:T(8,128)S(1)} %get-tuple-element.44), custom_call_target="InvertDiagBlocksLowerTriangular" | custom-call | tf_op jit(solution)/shard_map/jit(cholesky)/cholesky | solution.py:37
  236.2 11.7 %cholesky.274 = f32[128,128]{1,0:T(8,128)S(1)} custom-call(f32[128,128]{1,0:T(8,128)S(1)} %cholesky.654), custom_call_target="Cholesky" | custom-call | tf_op jit(solution)/shard_map/jit(cholesky)/cholesky | solution.py:37
  250.7 9.8 %custom-call.68 = f32[1,128,128]{1,2,0:T(8,128)S(1)} custom-call(f32[1,128,128]{2,1,0:T(8,128)S(1)} %get-tuple-element.42), custom_call_target="InvertDiagBlocksLowerTriangular" | custom-call | tf_op jit(solution)/shard_map/jit(cholesky)/cholesky | solution.py:37
  266.0 11.7 %cholesky.299 = f32[128,128]{1,0:T(8,128)S(1)} custom-call(f32[128,128]{1,0:T(8,128)S(1)} %cholesky.659), custom_call_target="Cholesky" | custom-call | tf_op jit(solution)/shard_map/jit(cholesky)/cholesky | solution.py:37
  278.5 9.8 %custom-call.69 = f32[1,128,128]{1,2,0:T(8,128)S(1)} custom-call(f32[1,128,128]{2,1,0:T(8,128)S(1)} %get-tuple-element.40), custom_call_target="InvertDiagBlocksLowerTriangular" | custom-call | tf_op jit(solution)/shard_map/jit(cholesky)/cholesky | solution.py:37
  293.1 11.7 %cholesky.539 = f32[128,128]{1,0:T(8,128)S(1)} custom-call(f32[128,128]{1,0:T(8,128)S(1)} %cholesky.664), custom_call_target="Cholesky" | custom-call | tf_op jit(solution)/shard_map/jit(cholesky)/cholesky | solution.py:37
  305.6 9.8 %custom-call.70 = f32[1,128,128]{1,2,0:T(8,128)S(1)} custom-call(f32[1,128,128]{2,1,0:T(8,128)S(1)} %get-tuple-element.38), custom_call_target="InvertDiagBlocksLowerTriangular" | custom-call | tf_op jit(solution)/shard_map/jit(cholesky)/cholesky | solution.py:37
  319.7 11.8 %cholesky.558 = f32[128,128]{1,0:T(8,128)S(1)} custom-call(f32[128,128]{1,0:T(8,128)S(1)} %cholesky.669), custom_call_target="Cholesky" | custom-call | tf_op jit(solution)/shard_map/jit(cholesky)/cholesky | solution.py:37
  332.3 9.8 %custom-call.71 = f32[1,128,128]{1,2,0:T(8,128)S(1)} custom-call(f32[1,128,128]{2,1,0:T(8,128)S(1)} %get-tuple-element.36), custom_call_target="InvertDiagBlocksLowerTriangular" | custom-call | tf_op jit(solution)/shard_map/jit(cholesky)/cholesky | solution.py:37
  346.4 11.7 %cholesky.578 = f32[128,128]{1,0:T(8,128)S(1)} custom-call(f32[128,128]{1,0:T(8,128)S(1)} %cholesky.674), custom_call_target="Cholesky" | custom-call | tf_op jit(solution)/shard_map/jit(cholesky)/cholesky | solution.py:37
  358.8 9.8 %custom-call.72 = f32[1,128,128]{1,2,0:T(8,128)S(1)} custom-call(f32[1,128,128]{2,1,0:T(8,128)S(1)} %get-tuple-element.34), custom_call_target="InvertDiagBlocksLowerTriangular" | custom-call | tf_op jit(solution)/shard_map/jit(cholesky)/cholesky | solution.py:37
  372.5 11.7 %cholesky.598 = f32[128,128]{1,0:T(8,128)S(1)} custom-call(f32[128,128]{1,0:T(8,128)S(1)} %cholesky.679), custom_call_target="Cholesky" | custom-call | tf_op jit(solution)/shard_map/jit(cholesky)/cholesky | solution.py:37
  385.0 9.8 %custom-call.77 = f32[1,128,128]{1,2,0:T(8,128)S(1)} custom-call(f32[1,128,128]{2,1,0:T(8,128)S(1)} %get-tuple-element.32), custom_call_target="InvertDiagBlocksLowerTriangular" | custom-call | tf_op jit(solution)/shard_map/jit(cholesky)/cholesky/custom-call.17 | solution.py:37
  397.9 11.7 %cholesky.612 = f32[128,128]{1,0:T(8,128)S(1)} custom-call(f32[128,128]{1,0:T(8,128)S(1)} %convolution_subtract_fusion.8), custom_call_target="Cholesky" | custom-call | tf_op jit(solution)/shard_map/jit(cholesky)/cholesky | solution.py:37
  428.6 7.1 fusion.2
  435.8 229.8 %all-reduce.8.cloned.1.call-done = f32[3584,256]{0,1:T(8,128)} async-done(((f32[3584,256]{0,1:T(8,128)}), f32[3584,256]{0,1:T(8,128)}) %all-reduce.8.cloned.1.call-update) | async-done | bytes 3670032 | tf_op jit(solution)/shard_map/psum | solution.py:44
  665.6 7.0 fusion.47
  680.0 24.5 %all-reduce.10.cloned.1.call-done = f32[256,256]{0,1:T(8,128)} async-done(((f32[256,256]{0,1:T(8,128)}), f32[256,256]{0,1:T(8,128)}) %all-reduce.10.cloned.1.call-update) | async-done | bytes 262160 | tf_op jit(solution)/shard_map/psum | solution.py:45
  706.6 11.7 %cholesky.625 = f32[128,128]{1,0:T(8,128)S(1)} custom-call(f32[128,128]{1,0:T(8,128)S(1)} %cholesky.683), custom_call_target="Cholesky" | custom-call | tf_op jit(solution)/shard_map/jit(cholesky)/cholesky | solution.py:49
  718.4 9.8 %custom-call.78 = f32[1,128,128]{1,2,0:T(8,128)S(1)} custom-call(f32[1,128,128]{2,1,0:T(8,128)S(1)} %get-tuple-element.30), custom_call_target="InvertDiagBlocksLowerTriangular" | custom-call | tf_op jit(solution)/shard_map/jit(cholesky)/cholesky/custom-call.17 | solution.py:49
  728.7 11.7 %cholesky.634 = f32[128,128]{1,0:T(8,128)S(1)} custom-call(f32[128,128]{1,0:T(8,128)S(1)} %convolution_subtract_fusion.7), custom_call_target="Cholesky" | custom-call | tf_op jit(solution)/shard_map/jit(cholesky)/cholesky | solution.py:49
  747.2 19.9 %custom-call.73 = f32[2,128,128]{1,2,0:T(8,128)S(1)} custom-call(f32[2,128,128]{2,1,0:T(8,128)S(1)} %get-tuple-element.10), custom_call_target="InvertDiagBlocksLowerTriangular" | custom-call | tf_op jit(solution)/shard_map/jit(_solve_triangular)/triangular_solve | solution.py:50
  (107 shorter events, 74.8 us)
Async XLA Ops:
  7.2 1.6 copy-start
  7.2 164.0 %all-reduce.6.cloned.1.call-start = ((), (), s32[]{:S(2)}) async-start(), calls=%async_computation.1 | async-start | bytes 8388608 | tf_op jit(solution)/shard_map/psum | solution.py:34
  133.0 532.6 %all-reduce.8.cloned.1.call-start = ((), (), s32[]{:S(2)}) async-start(), calls=%async_computation.2 | async-start | bytes 7340032 | tf_op jit(solution)/shard_map/psum | solution.py:44
  209.3 1.9 copy-start.3
  420.0 4.7 copy-start.4
  422.8 1.9 copy-start.2
  435.7 268.8 %all-reduce.10.cloned.1.call-start = ((), (), s32[]{:S(2)}) async-start(), calls=%async_computation.3 | async-start | bytes 524288 | tf_op jit(solution)/shard_map/psum | solution.py:45
  672.6 95.9 %copy-start.1 = (bf16[128,8,1024]{2,1,0:T(8,128)(2,1)S(1)}, bf16[128,8,1024]{2,1,0:T(8,128)(2,1)}, u32[]{:S(2)}) copy-start(bf16[128,8,1024]{2,1,0:T(8,128)(2,1)} %param.7) | copy-start | bytes 6291460
Sparse Core Ops, SparseCore 0:
  133.1 38.0 all-reduce.5
  435.8 229.7 all-reduce.7
  672.7 31.7 all-reduce.9
where the time goes:
time: 784 us; the launch traced here: 775 us
  waiting for transfers between devices  293 us (37%)
  other arithmetic  242 us (31%)
  blocking collectives  110 us (14%)
  local copies, waits for them, and re-layouts  57 us (7%)
  matrix products  52.5 us (7%)
  between operations  21.4 us (3%)
    psum x1, waiting for transfers between devices, local(): whole_half = lax.psum(contract(down_half, test_mat), 'expert')  230 us
    another operation x30, other arithmetic, local(): whitening = jnp.linalg.cholesky(damped)  167 us
    all_to_all x1, blocking collectives, local(): lax.all_to_all(outgoing, 'expert', split_axis=0, concat_axis=0, tiled=True)  110 us
    psum x1, waiting for transfers between devices, local(): gram_mat = lax.psum(contract(received, received), 'dp') / n_slot  38.1 us
    another operation x7, other arithmetic, local(): qr_factor = jnp.linalg.cholesky(small_gram)  34.6 us
    another operation x14, matrix products, local(): whitening = jnp.linalg.cholesky(damped)  27.2 us
    psum x1, waiting for transfers between devices, local(): lax.psum(jnp.dot(whole_half.T, whole_half, precision=lax.Precision.HIGHES...  24.5 us
    another operation x3, other arithmetic, local(): jax.scipy.linalg.solve_triangular(qr_factor, sketch.T, lower=True)  19.9 us
  transfers between devices with their start and end apart: 3, of which 3 were waited for; matrix products, arithmetic and copies ran while one was open for 1% of the time, Pallas kernels for 0%

commit v1 on v0

--- a/solution.py
+++ b/solution.py
@@ -31,20 +31,23 @@
     received = lax.all_to_all(outgoing, "expert", split_axis=0, concat_axis=0, tiled=True).reshape(
         n_exp * capacity, hid_width
     )
-    gram_mat = lax.psum(contract(received, received), "dp") / n_slot
-    identity_mat = jnp.eye(hid_width, dtype=jnp.float32)
-    damped = gram_mat + (damping * jnp.mean(jnp.diagonal(gram_mat)) + jitter) * identity_mat
+    partner = lax.ppermute(received, "dp", [(0, 1), (1, 0)])
+    gram_mat = (contract(received, received) + contract(partner, partner)) / n_slot
+    on_diag = lax.broadcasted_iota(jnp.int32, gram_mat.shape, 0) == lax.broadcasted_iota(
+        jnp.int32, gram_mat.shape, 1
+    )
+    diag_mean = jnp.sum(jnp.where(on_diag, gram_mat, 0.0)) / hid_width
+    damped = jnp.where(on_diag, gram_mat + (damping * diag_mean + jitter), gram_mat)
     whitening = jnp.linalg.cholesky(damped)
     test_mat = jnp.dot(
         whitening, omega[0].astype(jnp.float32), precision=lax.Precision.HIGHEST
     ).astype(jnp.bfloat16)
     down_half = down_weight[0]
     half_cols = down_half.shape[1]
-    row_share = half_cols // n_exp
-    whole_half = lax.psum(contract(down_half, test_mat), "expert")
-    small_gram = lax.psum(jnp.dot(whole_half.T, whole_half, precision=lax.Precision.HIGHEST), "dp")
-    sketch = lax.dynamic_slice_in_dim(
-        whole_half, lax.axis_index("expert") * row_share, row_share, 0
+    term = contract(down_half, test_mat).reshape(n_exp, half_cols // n_exp, -1)
+    sketch = lax.psum_scatter(term, "expert", scatter_dimension=0, tiled=True)[0]
+    small_gram = lax.psum(
+        jnp.dot(sketch.T, sketch, precision=lax.Precision.HIGHEST), ("expert", "dp")
     )
     qr_factor = jnp.linalg.cholesky(small_gram)
     basis_rows = jax.scipy.linalg.solve_triangular(qr_factor, sketch.T, lower=True).T * math.sqrt(

time: 784 us -> 1420 us (1.81)
  waiting for transfers between devices: 293 us -> 953 us
  local copies, waits for them, and re-layouts: 57 us -> 39.5 us
    reduce_scatter x0 -> x1, waiting for transfers between devices: none -> 605 us  [local(): lax.psum_scatter(term, 'expert', scatter_dimension=0, tiled=True)[0]]
    psum x3 -> x1, waiting for transfers between devices: 292 us -> 346 us  [local(): lax.psum(jnp.dot(sketch.T, sketch, precision=lax.Precision.HIGHEST), ('ex...]
    gather x1 -> x0, local copies, waits for them, and re-layouts: 16.8 us -> none  [local(): jnp.diagonal(gram_mat)]
where the time goes in v1:
time: 1420 us; the launch traced here: 1410 us
  waiting for transfers between devices  953 us (67%)
  other arithmetic  236 us (17%)
  blocking collectives  110 us (8%)
  matrix products  46.8 us (3%)
  local copies, waits for them, and re-layouts  39.5 us (3%)
  between operations  21.4 us (2%)
    reduce_scatter x1, waiting for transfers between devices, local(): lax.psum_scatter(term, 'expert', scatter_dimension=0, tiled=True)[0]  605 us
    psum x1, waiting for transfers between devices, local(): lax.psum(jnp.dot(sketch.T, sketch, precision=lax.Precision.HIGHEST), ('ex...  346 us
    another operation x30, other arithmetic, local(): whitening = jnp.linalg.cholesky(damped)  172 us
    all_to_all x1, blocking collectives, local(): lax.all_to_all(outgoing, 'expert', split_axis=0, concat_axis=0, tiled=True)  110 us
    another operation x7, other arithmetic, local(): qr_factor = jnp.linalg.cholesky(small_gram)  34.6 us
  transfers between devices with their start and end apart: 3, of which 3 were waited for; matrix products, arithmetic and copies ran while one was open for 1% of the time, Pallas kernels for 0%

profile of v1, /device:TPU:1, one launch (start us, length us, event | category | flops | bytes accessed | tf_op | source)
XLA Modules:
  0.0 1410.6 jit_solution(1682598114201949649)
XLA Ops:
  8.8 7.9 scatter_custom_fusion
  16.7 110.1 %all_to_all.5 = bf16[128,16,1024]{2,1,0:T(8,128)(2,1)S(1)} all-to-all(bf16[128,16,1024]{2,1,0:T(8,128)(2,1)} %bitcast.114), channel_id=1, replica_groups=mesh['expert'=128,'dp'=2] {'expert'}, dimensions={0} | all-to-all | bytes 8388608 | tf_op jit(solution)/shard_map/all_to_all | solution.py:31
  126.7 3.6 collective-permute-start
  130.4 4.6 fusion.68
  137.2 7.2 select_reduce_fusion
  144.3 5.5 copy.28
  150.5 4.4 fusion.6
  156.9 11.7 cholesky.249
  168.6 9.8 custom-call.67
  184.9 11.9 cholesky.274
  197.4 9.8 custom-call.68
  210.6 11.7 cholesky.299
  223.5 9.8 custom-call.69
  236.9 12.1 cholesky.539
  250.3 9.8 custom-call.70
  263.5 11.7 cholesky.558
  276.5 10.0 custom-call.71
  289.8 11.7 cholesky.578
  302.8 9.8 custom-call.72
  315.6 11.9 cholesky.598
  328.8 9.8 custom-call.75
  341.2 11.7 cholesky.612
  366.5 7.0 fusion.2
  373.5 5.1 copy.30
  378.7 4.8 reshape.116
  383.9 604.7 %reduce-scatter.2.cloned.1.call-done = f32[1,28,256]{2,1,0:T(8,128)} async-done(((f32[128,28,256]{2,1,0:T(8,128)}), f32[1,28,256]{2,1,0:T(8,128)}) %reduce-scatter.2.cloned.1.call-update) | async-done | bytes 28688 | tf_op jit(solution)/shard_map/reduce_scatter | solution.py:48
  993.9 345.9 %all-reduce.4.cloned.1.call-done = f32[256,256]{0,1:T(8,128)} async-done(((f32[256,256]{0,1:T(8,128)}), f32[256,256]{0,1:T(8,128)}) %all-reduce.4.cloned.1.call-update) | async-done | bytes 262160 | tf_op jit(solution)/shard_map/psum | solution.py:49
  1341.9 11.7 cholesky.625
  1353.7 9.8 custom-call.76
  1364.0 11.7 cholesky.634
  1378.5 4.2 while.1
  1382.7 19.7 %custom-call.73 = f32[2,128,128]{1,2,0:T(8,128)S(1)} custom-call(f32[2,128,128]{2,1,0:T(8,128)S(1)} %get-tuple-element.10), custom_call_target="InvertDiagBlocksLowerTriangular" | custom-call | tf_op jit(solution)/shard_map/jit(_solve_triangular)/triangular_solve | solution.py:53
  (87 shorter events, 62.1 us)
Async XLA Ops:
  7.2 1.6 copy-start
  7.2 981.4 %reduce-scatter.2.cloned.1.call-start = ((), (), s32[]{:S(2)}) async-start(), calls=%async_computation.2 | async-start | bytes 4227072 | tf_op jit(solution)/shard_map/reduce_scatter | solution.py:48
  126.7 10.4 collective-permute-start
  154.9 1.9 copy-start.3
  359.8 4.7 copy-start.4
  362.6 1.9 copy-start.2
  383.4 956.4 %all-reduce.4.cloned.1.call-start = ((), (), s32[]{:S(2)}) async-start(), calls=%async_computation.3 | async-start | bytes 524288 | tf_op jit(solution)/shard_map/psum | solution.py:49
  990.6 411.8 %copy-start.5 = (f32[1,28,256]{2,1,0:T(8,128)S(1)}, f32[1,28,256]{2,1,0:T(8,128)}, u32[]{:S(2)}) copy-start(f32[1,28,256]{2,1,0:T(8,128)} %reduce-scatter.2.cloned.1.call-done) | copy-start | bytes 86020
  990.6 413.0 %copy-start.1 = (bf16[128,8,1024]{2,1,0:T(8,128)(2,1)S(1)}, bf16[128,8,1024]{2,1,0:T(8,128)(2,1)}, u32[]{:S(2)}) copy-start(bf16[128,8,1024]{2,1,0:T(8,128)(2,1)} %param.7) | copy-start | bytes 6291460
Sparse Core Ops, SparseCore 0:
  383.6 605.0 reduce-scatter.1
  994.1 345.7 all-reduce.3

commit v2 on v1

--- a/solution.py
+++ b/solution.py
@@ -13,6 +13,53 @@
     return lax.dot_general(
         left, right, (((0,), (0,)), ((), ())), preferred_element_type=jnp.float32
     )
+
+
+def xor_pairs(n, mask):
+    return [(i, i ^ mask) for i in range(n)]
+
+
+def scatter_sum(term, orders):
+    n_exp, rows, cols = term.shape
+    n_bits = n_exp.bit_length() - 1
+    me = lax.axis_index("expert")
+    width = cols // len(orders)
+    outs = []
+    for s, order in enumerate(orders):
+        part = term[:, :, s * width:(s + 1) * width].reshape([2] * n_bits + [rows, width])
+        perm = [n_bits - 1 - b for b in order] + [n_bits, n_bits + 1]
+        part = part.transpose(perm).reshape(n_exp, rows, width)
+        for b in order:
+            half = part.shape[0] // 2
+            v = (me >> b) & 1
+            keep = lax.dynamic_slice_in_dim(part, v * half, half, 0)
+            send = lax.dynamic_slice_in_dim(part, (1 - v) * half, half, 0)
+            part = keep + lax.ppermute(send, "expert", xor_pairs(n_exp, 1 << b))
+        outs.append(part[0])
+    return jnp.concatenate(outs, axis=-1)
+
+
+def all_sum(x, order):
+    n_exp = lax.axis_size("expert")
+    for b in order:
+        x = x + lax.ppermute(x, "expert", xor_pairs(n_exp, 1 << b))
+    return x + lax.ppermute(x, "dp", [(0, 1), (1, 0)])
+
+
+def bit_orders(n_exp, n_streams):
+    n_bits = n_exp.bit_length() - 1
+    if n_bits >= 5:
+        axes = [[0, 1], [2, 3], list(range(4, n_bits))]
+    else:
+        axes = [list(range(n_bits))]
+    orders = []
+    for s in range(n_streams):
+        turn = axes[s % len(axes):] + axes[:s % len(axes)]
+        order = []
+        for level in range(max(len(a) for a in turn)):
+            order += [a[level] for a in turn if level < len(a)]
+        orders.append(order)
+    return orders
 
 
 def local(hidden, routes, slots, down_weight, omega):
@@ -45,10 +92,9 @@
     down_half = down_weight[0]
     half_cols = down_half.shape[1]
     term = contract(down_half, test_mat).reshape(n_exp, half_cols // n_exp, -1)
-    sketch = lax.psum_scatter(term, "expert", scatter_dimension=0, tiled=True)[0]
-    small_gram = lax.psum(
-        jnp.dot(sketch.T, sketch, precision=lax.Precision.HIGHEST), ("expert", "dp")
-    )
+    orders = bit_orders(n_exp, 2)
+    sketch = scatter_sum(term, orders)
+    small_gram = all_sum(jnp.dot(sketch.T, sketch, precision=lax.Precision.HIGHEST), orders[0])
     qr_factor = jnp.linalg.cholesky(small_gram)
     basis_rows = jax.scipy.linalg.solve_triangular(qr_factor, sketch.T, lower=True).T * math.sqrt(
         half_cols * n_dp

time: 1420 us -> 602 us (0.42)
  waiting for transfers between devices: 953 us -> 181 us
  blocking collectives: 110 us -> 0 us
  starting transfers between devices: 4.13 us -> 65.5 us
    reduce_scatter x1 -> x0, waiting for transfers between devices: 605 us -> none  [local(): lax.psum_scatter(term, 'expert', scatter_dimension=0, tiled=True)[0]]
    psum x1 -> x0, waiting for transfers between devices: 346 us -> none  [local(): lax.psum(jnp.dot(sketch.T, sketch, precision=lax.Precision.HIGHEST), ('ex...]
    all_to_all x1 -> x0, blocking collectives: 110 us -> none  [local(): lax.all_to_all(outgoing, 'expert', split_axis=0, concat_axis=0, tiled=True)]
    all_to_all x0 -> x1, waiting for transfers between devices: none -> 93.3 us  [local(): lax.all_to_all(outgoing, 'expert', split_axis=0, concat_axis=0, tiled=True)]
    ppermute x0 -> x22, waiting for transfers between devices: none -> 87.3 us  [the longest x14 45.1 us: scatter_sum(): part = keep + lax.ppermute(send, 'expert', xor_pairs(n_exp, 1 << b))]
    ppermute x0 -> x22, starting transfers between devices: none -> 45.5 us  [the longest x14 17.7 us: scatter_sum(): part = keep + lax.ppermute(send, 'expert', xor_pairs(n_exp, 1 << b))]
    all_to_all x0 -> x1, starting transfers between devices: none -> 16.9 us  [local(): lax.all_to_all(outgoing, 'expert', split_axis=0, concat_axis=0, tiled=True)]
  transfers between devices with their start and end apart: 3 -> 24, of which waited for: 3 -> 19; matrix products, arithmetic and copies ran while one was open for 1% -> 3% of each run, Pallas kernels for 0% -> 0%
where the time goes in v2:
time: 602 us; the launch traced here: 593 us
  other arithmetic  240 us (40%)
  waiting for transfers between devices  181 us (30%)
  starting transfers between devices  65.5 us (11%)
  local copies, waits for them, and re-layouts  49.5 us (8%)
  matrix products  48.3 us (8%)
  between operations  8.61 us (1%)
    another operation x30, other arithmetic, local(): whitening = jnp.linalg.cholesky(damped)  172 us
    all_to_all x1, waiting for transfers between devices, local(): lax.all_to_all(outgoing, 'expert', split_axis=0, concat_axis=0, tiled=True)  93.3 us
    ppermute x14, waiting for transfers between devices, scatter_sum(): part = keep + lax.ppermute(send, 'expert', xor_pairs(n_exp, 1 << b))  45.1 us
    ppermute x7, waiting for transfers between devices, all_sum(): x = x + lax.ppermute(x, 'expert', xor_pairs(n_exp, 1 << b))  42.2 us
    another operation x7, other arithmetic, local(): qr_factor = jnp.linalg.cholesky(small_gram)  34.7 us
    another operation x14, matrix products, local(): whitening = jnp.linalg.cholesky(damped)  23.1 us
    dot_general x3, matrix products, contract(): lax.dot_general(left, right, (((0,), (0,)), ((), ())), preferred_element_...  21.8 us
    another operation x3, other arithmetic, local(): jax.scipy.linalg.solve_triangular(qr_factor, sketch.T, lower=True)  19.7 us
  transfers between devices with their start and end apart: 24, of which 19 were waited for; matrix products, arithmetic and copies ran while one was open for 3% of the time, Pallas kernels for 0%

profile of v2, /device:TPU:1, one launch (start us, length us, event | category | flops | bytes accessed | tf_op | source)
XLA Modules:
  0.0 592.7 jit_solution(8064766923309068767)
XLA Ops:
  2.3 7.9 %scatter_custom_fusion = bf16[2048,1024]{1,0:T(8,128)(2,1)} fusion(s32[1024]{0:T(1024)S(1)} %bitcast.128, bf16[128,8,1024]{2,1,0:T(8,128)(2,1)S(1)} %copy-done, bf16[]{:T(256)} %constant.351.clone.1), kind=kCustom, calls=%fused_computation.17 | custom fusion | bytes 6291458 | tf_op jit(solution)/shard_map/scatter | solution.py:75
  10.2 16.9 %all-to-all-start = ((bf16[128,16,1024]{2,1,0:T(8,128)(2,1)}), bf16[128,16,1024]{2,1,0:T(8,128)(2,1)}, u32[]{:S(2)}, u32[]{:S(2)}) async-start(bf16[128,16,1024]{2,1,0:T(8,128)(2,1)} %bitcast.123), calls=%async_computation | async-start | bytes 8388608 | tf_op jit(solution)/shard_map/all_to_all | solution.py:78
  27.1 93.3 %all-to-all-done = bf16[128,16,1024]{2,1,0:T(8,128)(2,1)} async-done(((bf16[128,16,1024]{2,1,0:T(8,128)(2,1)}), bf16[128,16,1024]{2,1,0:T(8,128)(2,1)}, u32[]{:S(2)}, u32[]{:S(2)}) %all-to-all-start) | async-done | bytes 4194336 | tf_op jit(solution)/shard_map/all_to_all | solution.py:78
  123.5 7.6 %fusion.70 = f32[1024,1024,1]{1,0,2:T(8,128)S(1)} fusion(bf16[128,16,1024]{2,1,0:T(8,128)(2,1)} %all-to-all-done), kind=kOutput, calls=%fused_computation.167 | convolution fusion | flops 4294967296 | bytes 8388608 | tf_op jit(solution)/shard_map/dot_general | solution.py:13
  131.1 7.2 %select_reduce_fusion = (f32[]{:T(128)}, f32[1024,1024]{1,0:T(8,128)}) fusion(bf16[2048,1024]{1,0:T(8,128)(2,1)S(1)} %collective-permute-done, f32[1024,1024,1]{1,0,2:T(8,128)S(1)} %fusion.70), kind=kOutput, calls=%fused_computation.14 | convolution fusion | flops 4300210176 | bytes 12582916 | tf_op jit(solution)/shard_map/dot_general | solution.py:13
  138.3 5.5 copy.49
  150.9 11.7 %cholesky.249 = f32[128,128]{1,0:T(8,128)S(1)} custom-call(f32[128,128]{1,0:T(8,128)S(1)} %cholesky.650), custom_call_target="Cholesky" | custom-call | tf_op jit(solution)/shard_map/jit(cholesky)/cholesky | solution.py:88
  162.6 9.8 %custom-call.67 = f32[1,128,128]{1,2,0:T(8,128)S(1)} custom-call(f32[1,128,128]{2,1,0:T(8,128)S(1)} %get-tuple-element.60), custom_call_target="InvertDiagBlocksLowerTriangular" | custom-call | tf_op jit(solution)/shard_map/jit(cholesky)/cholesky | solution.py:88
  178.9 12.1 %cholesky.274 = f32[128,128]{1,0:T(8,128)S(1)} custom-call(f32[128,128]{1,0:T(8,128)S(1)} %cholesky.654), custom_call_target="Cholesky" | custom-call | tf_op jit(solution)/shard_map/jit(cholesky)/cholesky | solution.py:88
  191.6 9.8 %custom-call.68 = f32[1,128,128]{1,2,0:T(8,128)S(1)} custom-call(f32[1,128,128]{2,1,0:T(8,128)S(1)} %get-tuple-element.57), custom_call_target="InvertDiagBlocksLowerTriangular" | custom-call | tf_op jit(solution)/shard_map/jit(cholesky)/cholesky | solution.py:88
  204.8 11.7 %cholesky.299 = f32[128,128]{1,0:T(8,128)S(1)} custom-call(f32[128,128]{1,0:T(8,128)S(1)} %cholesky.659), custom_call_target="Cholesky" | custom-call | tf_op jit(solution)/shard_map/jit(cholesky)/cholesky | solution.py:88
  217.7 9.8 %custom-call.69 = f32[1,128,128]{1,2,0:T(8,128)S(1)} custom-call(f32[1,128,128]{2,1,0:T(8,128)S(1)} %get-tuple-element.54), custom_call_target="InvertDiagBlocksLowerTriangular" | custom-call | tf_op jit(solution)/shard_map/jit(cholesky)/cholesky | solution.py:88
  231.1 11.9 %cholesky.539 = f32[128,128]{1,0:T(8,128)S(1)} custom-call(f32[128,128]{1,0:T(8,128)S(1)} %cholesky.664), custom_call_target="Cholesky" | custom-call | tf_op jit(solution)/shard_map/jit(cholesky)/cholesky | solution.py:88
  244.2 9.8 %custom-call.70 = f32[1,128,128]{1,2,0:T(8,128)S(1)} custom-call(f32[1,128,128]{2,1,0:T(8,128)S(1)} %get-tuple-element.51), custom_call_target="InvertDiagBlocksLowerTriangular" | custom-call | tf_op jit(solution)/shard_map/jit(cholesky)/cholesky | solution.py:88
  257.5 11.7 %cholesky.558 = f32[128,128]{1,0:T(8,128)S(1)} custom-call(f32[128,128]{1,0:T(8,128)S(1)} %cholesky.669), custom_call_target="Cholesky" | custom-call | tf_op jit(solution)/shard_map/jit(cholesky)/cholesky | solution.py:88
  270.5 10.0 %custom-call.71 = f32[1,128,128]{1,2,0:T(8,128)S(1)} custom-call(f32[1,128,128]{2,1,0:T(8,128)S(1)} %get-tuple-element.48), custom_call_target="InvertDiagBlocksLowerTriangular" | custom-call | tf_op jit(solution)/shard_map/jit(cholesky)/cholesky | solution.py:88
  283.8 11.7 %cholesky.578 = f32[128,128]{1,0:T(8,128)S(1)} custom-call(f32[128,128]{1,0:T(8,128)S(1)} %cholesky.674), custom_call_target="Cholesky" | custom-call | tf_op jit(solution)/shard_map/jit(cholesky)/cholesky | solution.py:88
  296.8 9.8 %custom-call.72 = f32[1,128,128]{1,2,0:T(8,128)S(1)} custom-call(f32[1,128,128]{2,1,0:T(8,128)S(1)} %get-tuple-element.45), custom_call_target="InvertDiagBlocksLowerTriangular" | custom-call | tf_op jit(solution)/shard_map/jit(cholesky)/cholesky | solution.py:88
  309.6 12.1 %cholesky.598 = f32[128,128]{1,0:T(8,128)S(1)} custom-call(f32[128,128]{1,0:T(8,128)S(1)} %cholesky.679), custom_call_target="Cholesky" | custom-call | tf_op jit(solution)/shard_map/jit(cholesky)/cholesky | solution.py:88
  323.0 9.8 %custom-call.75 = f32[1,128,128]{1,2,0:T(8,128)S(1)} custom-call(f32[1,128,128]{2,1,0:T(8,128)S(1)} %get-tuple-element.42), custom_call_target="InvertDiagBlocksLowerTriangular" | custom-call | tf_op jit(solution)/shard_map/jit(cholesky)/cholesky/custom-call.17 | solution.py:88
  335.4 11.7 %cholesky.612 = f32[128,128]{1,0:T(8,128)S(1)} custom-call(f32[128,128]{1,0:T(8,128)S(1)} %slice_subtract_fusion.7), custom_call_target="Cholesky" | custom-call | tf_op jit(solution)/shard_map/jit(cholesky)/cholesky | solution.py:88
  360.7 7.0 %fusion.2 = f32[3584,256]{0,1:T(8,128)} fusion(bf16[1024,256]{1,0:T(8,128)(2,1)S(1)} %convolution_convert_fusion, bf16[1,1024,3584]{2,1,0:T(8,128)(2,1)} %param.10), kind=kOutput, calls=%fused_computation.7 | convolution fusion | flops 1879048192 | bytes 11534336 | tf_op jit(solution)/shard_map/dot_general | solution.py:13
  386.9 18.3 %collective-permute-done.1 = f32[64,28,128]{2,0,1:T(8,128)} collective-permute-done((f32[64,28,128]{2,0,1:T(8,128)}, f32[64,28,128]{2,0,1:T(8,128)}, u32[]{:S(2)}, u32[]{:S(2)}) %collective-permute-start.1) | collective-permute-done | bytes 917536 | tf_op jit(solution)/shard_map/ppermute | solution.py:37
  414.2 6.8 %collective-permute-done.2 = f32[32,28,128]{2,1,0:T(8,128)S(1)} collective-permute-done((f32[32,28,128]{2,1,0:T(8,128)}, f32[32,28,128]{2,1,0:T(8,128)S(1)}, u32[]{:S(2)}, u32[]{:S(2)}) %collective-permute-start.2) | collective-permute-done | bytes 458784 | tf_op jit(solution)/shard_map/ppermute | solution.py:37
  426.0 5.1 collective-permute-done.3
  489.9 6.9 %collective-permute-done.20 = f32[256,256]{0,1:T(8,128)S(1)} collective-permute-done((f32[256,256]{0,1:T(8,128)S(1)}, f32[256,256]{0,1:T(8,128)S(1)}, u32[]{:S(2)}, u32[]{:S(2)}) %collective-permute-start.20) | collective-permute-done | bytes 262176 | tf_op jit(solution)/shard_map/ppermute | solution.py:45
  500.0 11.6 %collective-permute-done.21 = f32[256,256]{0,1:T(8,128)S(1)} collective-permute-done((f32[256,256]{0,1:T(8,128)S(1)}, f32[256,256]{0,1:T(8,128)S(1)}, u32[]{:S(2)}, u32[]{:S(2)}) %collective-permute-start.21) | collective-permute-done | bytes 262176 | tf_op jit(solution)/shard_map/ppermute | solution.py:45
  511.7 15.2 %collective-permute-start.22 = (f32[256,256]{0,1:T(8,128)S(1)}, f32[256,256]{0,1:T(8,128)S(1)}, u32[]{:S(2)}, u32[]{:S(2)}) collective-permute-start(f32[256,256]{0,1:T(8,128)S(1)} %add.329), channel_id=1, source_target_pairs={{0,1},{1,0},{2,3},{3,2},{4,5},{5,4},{6,7},{7,6},{8,9},{9,8},{10,11... | collective-permute-start | bytes 786440 | tf_op jit(solution)/shard_map/ppermute | solution.py:46
  530.3 11.7 %cholesky.625 = f32[128,128]{1,0:T(8,128)S(1)} custom-call(f32[128,128]{1,0:T(8,128)S(1)} %cholesky.683), custom_call_target="Cholesky" | custom-call | tf_op jit(solution)/shard_map/jit(cholesky)/cholesky | solution.py:98
  542.1 9.8 %custom-call.76 = f32[1,128,128]{1,2,0:T(8,128)S(1)} custom-call(f32[1,128,128]{2,1,0:T(8,128)S(1)} %get-tuple-element.38), custom_call_target="InvertDiagBlocksLowerTriangular" | custom-call | tf_op jit(solution)/shard_map/jit(cholesky)/cholesky/custom-call.17 | solution.py:98
  552.4 11.7 %cholesky.634 = f32[128,128]{1,0:T(8,128)S(1)} custom-call(f32[128,128]{1,0:T(8,128)S(1)} %slice_subtract_fusion.6), custom_call_target="Cholesky" | custom-call | tf_op jit(solution)/shard_map/jit(cholesky)/cholesky | solution.py:98
  571.3 19.7 %custom-call.73 = f32[2,128,128]{1,2,0:T(8,128)S(1)} custom-call(f32[2,128,128]{2,1,0:T(8,128)S(1)} %get-tuple-element.10), custom_call_target="InvertDiagBlocksLowerTriangular" | custom-call | tf_op jit(solution)/shard_map/jit(_solve_triangular)/triangular_solve | solution.py:99
  (168 shorter events, 162.5 us)
Async XLA Ops:
  0.6 1.6 copy-start
  10.2 110.2 %all-to-all-start = ((bf16[128,16,1024]{2,1,0:T(8,128)(2,1)}), bf16[128,16,1024]{2,1,0:T(8,128)(2,1)}, u32[]{:S(2)}, u32[]{:S(2)}) async-start(bf16[128,16,1024]{2,1,0:T(8,128)(2,1)} %bitcast.123), calls=%async_computation | async-start | bytes 8388608 | tf_op jit(solution)/shard_map/all_to_all | solution.py:78
  120.4 10.7 %collective-permute-start = (bf16[2048,1024]{1,0:T(8,128)(2,1)}, bf16[2048,1024]{1,0:T(8,128)(2,1)S(1)}, u32[]{:S(2)}, u32[]{:S(2)}) collective-permute-start(bf16[2048,1024]{1,0:T(8,128)(2,1)} %bitcast.4), channel_id=1, source_target_pairs={{0,1},{1,0},{2,3},{3,2},{4,5},{5,4},{6,7},{7,6},{8,9},{9,8},{10,11... | collective-permute-start | bytes 12582920 | tf_op jit(solution)/shard_map/ppermute | solution.py:81
  148.9 1.9 copy-start.3
  354.0 4.7 copy-start.6
  356.7 1.9 copy-start.2
  383.0 22.2 %collective-permute-start.1 = (f32[64,28,128]{2,0,1:T(8,128)}, f32[64,28,128]{2,0,1:T(8,128)}, u32[]{:S(2)}, u32[]{:S(2)}) collective-permute-start(f32[64,28,128]{2,0,1:T(8,128)} %get-tuple-element.31), channel_id=1, source_target_pairs={{0,2},{2,0},{4,6},{6,4},{8,10},{10,8},{12,14},{14,12},{16,18},{18,... | collective-permute-start | bytes 2752520 | tf_op jit(solution)/shard_map/ppermute | solution.py:37
  386.3 22.7 %collective-permute-start.8 = (f32[64,28,128]{2,0,1:T(8,128)}, f32[64,28,128]{2,0,1:T(8,128)S(1)}, u32[]{:S(2)}, u32[]{:S(2)}) collective-permute-start(f32[64,28,128]{2,0,1:T(8,128)} %get-tuple-element.33), channel_id=1, source_target_pairs={{0,8},{2,10},{4,12},{6,14},{8,0},{10,2},{12,4},{14,6},{16,24},{18,... | collective-permute-start | bytes 2752520 | tf_op jit(solution)/shard_map/ppermute | solution.py:37
  386.9 23.0 %copy-start.4 = (f32[64,28,128]{2,0,1:T(8,128)S(1)}, f32[64,28,128]{2,0,1:T(8,128)}, u32[]{:S(2)}) copy-start(f32[64,28,128]{2,0,1:T(8,128)} %get-tuple-element.34) | copy-start | bytes 2752516
  408.2 12.8 %collective-permute-start.2 = (f32[32,28,128]{2,1,0:T(8,128)}, f32[32,28,128]{2,1,0:T(8,128)S(1)}, u32[]{:S(2)}, u32[]{:S(2)}) collective-permute-start(f32[32,28,128]{2,1,0:T(8,128)} %constant_dynamic-slice_fusion.14), channel_id=1, source_target_pairs={{0,8},{2,10},{4,12},{6,14},{8,0},{10,2},{12,4},{14,6},{16,24},{18,... | collective-permute-start | bytes 1376264 | tf_op jit(solution)/shard_map/ppermute | solution.py:37
  409.0 0.9 copy-start.5
  413.0 12.6 %collective-permute-start.9 = (f32[32,28,128]{2,1,0:T(8,128)}, f32[32,28,128]{2,1,0:T(8,128)S(1)}, u32[]{:S(2)}, u32[]{:S(2)}) collective-permute-start(f32[32,28,128]{2,1,0:T(8,128)} %constant_dynamic-slice_fusion.6), channel_id=1, source_target_pairs={{0,32},{2,34},{4,36},{6,38},{8,40},{10,42},{12,44},{14,46},{16,48}... | collective-permute-start | bytes 1376264 | tf_op jit(solution)/shard_map/ppermute | solution.py:37
  421.2 10.0 %collective-permute-start.3 = (f32[16,28,128]{2,1,0:T(8,128)S(1)}, f32[16,28,128]{2,1,0:T(8,128)S(1)}, u32[]{:S(2)}, u32[]{:S(2)}) collective-permute-start(f32[16,28,128]{2,1,0:T(8,128)S(1)} %constant_dynamic-slice_fusion.13), channel_id=1, source_target_pairs={{0,32},{2,34},{4,36},{6,38},{8,40},{10,42},{12,44},{14,46},{16,48}... | collective-permute-start | bytes 688136 | tf_op jit(solution)/shard_map/ppermute | solution.py:37
  425.6 7.5 %collective-permute-start.10 = (f32[16,28,128]{2,1,0:T(8,128)S(1)}, f32[16,28,128]{2,1,0:T(8,128)S(1)}, u32[]{:S(2)}, u32[]{:S(2)}) collective-permute-start(f32[16,28,128]{2,1,0:T(8,128)S(1)} %constant_dynamic-slice_fusion.5), channel_id=1, source_target_pairs={{0,2},{2,0},{4,6},{6,4},{8,10},{10,8},{12,14},{14,12},{16,18},{18,... | collective-permute-start | bytes 688136 | tf_op jit(solution)/shard_map/ppermute | solution.py:37
  431.2 6.8 %collective-permute-start.4 = (f32[8,28,128]{2,1,0:T(8,128)S(1)}, f32[8,28,128]{2,1,0:T(8,128)S(1)}, u32[]{:S(2)}, u32[]{:S(2)}) collective-permute-start(f32[8,28,128]{2,1,0:T(8,128)S(1)} %constant_dynamic-slice_fusion.12), channel_id=1, source_target_pairs={{0,4},{2,6},{4,0},{6,2},{8,12},{10,14},{12,8},{14,10},{16,20},{18,... | collective-permute-start | bytes 344072 | tf_op jit(solution)/shard_map/ppermute | solution.py:37
  433.2 6.9 %collective-permute-start.11 = (f32[8,28,128]{2,1,0:T(8,128)S(1)}, f32[8,28,128]{2,1,0:T(8,128)S(1)}, u32[]{:S(2)}, u32[]{:S(2)}) collective-permute-start(f32[8,28,128]{2,1,0:T(8,128)S(1)} %constant_dynamic-slice_fusion.4), channel_id=1, source_target_pairs={{0,16},{2,18},{4,20},{6,22},{8,24},{10,26},{12,28},{14,30},{16,0},... | collective-permute-start | bytes 344072 | tf_op jit(solution)/shard_map/ppermute | solution.py:37
  438.0 4.7 collective-permute-start.5
  440.2 5.0 collective-permute-start.12
  442.8 4.5 collective-permute-start.6
  445.3 4.4 collective-permute-start.13
  447.3 6.6 %collective-permute-start.7 = (f32[1,28,128]{2,1,0:T(8,128)S(1)}, f32[1,28,128]{2,1,0:T(8,128)S(1)}, u32[]{:S(2)}, u32[]{:S(2)}) collective-permute-start(f32[1,28,128]{2,1,0:T(8,128)S(1)} %constant_dynamic-slice_fusion.9), channel_id=1, source_target_pairs={{0,128},{2,130},{4,132},{6,134},{8,136},{10,138},{12,140},{14,142}... | collective-permute-start | bytes 43016 | tf_op jit(solution)/shard_map/ppermute | solution.py:37
  449.7 6.6 %collective-permute-start.14 = (f32[1,28,128]{2,1,0:T(8,128)S(1)}, f32[1,28,128]{2,1,0:T(8,128)S(1)}, u32[]{:S(2)}, u32[]{:S(2)}) collective-permute-start(f32[1,28,128]{2,1,0:T(8,128)S(1)} %constant_dynamic-slice_fusion.1), channel_id=1, source_target_pairs={{0,128},{2,130},{4,132},{6,134},{8,136},{10,138},{12,140},{14,142}... | collective-permute-start | bytes 43016 | tf_op jit(solution)/shard_map/ppermute | solution.py:37
  456.7 5.3 collective-permute-start.15
  462.0 5.6 collective-permute-start.16
  467.7 5.6 collective-permute-start.17
  473.3 6.8 %collective-permute-start.18 = (f32[256,256]{0,1:T(8,128)S(1)}, f32[256,256]{0,1:T(8,128)S(1)}, u32[]{:S(2)}, u32[]{:S(2)}) collective-permute-start(f32[256,256]{0,1:T(8,128)S(1)} %add.325), channel_id=1, source_target_pairs={{0,4},{2,6},{4,0},{6,2},{8,12},{10,14},{12,8},{14,10},{16,20},{18,... | collective-permute-start | bytes 786440 | tf_op jit(solution)/shard_map/ppermute | solution.py:45
  480.2 7.1 %collective-permute-start.19 = (f32[256,256]{0,1:T(8,128)S(1)}, f32[256,256]{0,1:T(8,128)S(1)}, u32[]{:S(2)}, u32[]{:S(2)}) collective-permute-start(f32[256,256]{0,1:T(8,128)S(1)} %add.326), channel_id=1, source_target_pairs={{0,16},{2,18},{4,20},{6,22},{8,24},{10,26},{12,28},{14,30},{16,0},... | collective-permute-start | bytes 786440 | tf_op jit(solution)/shard_map/ppermute | solution.py:45
  487.3 9.5 %collective-permute-start.20 = (f32[256,256]{0,1:T(8,128)S(1)}, f32[256,256]{0,1:T(8,128)S(1)}, u32[]{:S(2)}, u32[]{:S(2)}) collective-permute-start(f32[256,256]{0,1:T(8,128)S(1)} %add.327), channel_id=1, source_target_pairs={{0,64},{2,66},{4,68},{6,70},{8,72},{10,74},{12,76},{14,78},{16,80}... | collective-permute-start | bytes 786440 | tf_op jit(solution)/shard_map/ppermute | solution.py:45
  496.8 14.8 %collective-permute-start.21 = (f32[256,256]{0,1:T(8,128)S(1)}, f32[256,256]{0,1:T(8,128)S(1)}, u32[]{:S(2)}, u32[]{:S(2)}) collective-permute-start(f32[256,256]{0,1:T(8,128)S(1)} %add.328), channel_id=1, source_target_pairs={{0,128},{2,130},{4,132},{6,134},{8,136},{10,138},{12,140},{14,142}... | collective-permute-start | bytes 786440 | tf_op jit(solution)/shard_map/ppermute | solution.py:45
  511.6 80.6 %copy-start.1 = (bf16[128,8,1024]{2,1,0:T(8,128)(2,1)S(1)}, bf16[128,8,1024]{2,1,0:T(8,128)(2,1)}, u32[]{:S(2)}) copy-start(bf16[128,8,1024]{2,1,0:T(8,128)(2,1)} %param.7) | copy-start | bytes 6291460
  511.7 18.4 %collective-permute-start.22 = (f32[256,256]{0,1:T(8,128)S(1)}, f32[256,256]{0,1:T(8,128)S(1)}, u32[]{:S(2)}, u32[]{:S(2)}) collective-permute-start(f32[256,256]{0,1:T(8,128)S(1)} %add.329), channel_id=1, source_target_pairs={{0,1},{1,0},{2,3},{3,2},{4,5},{5,4},{6,7},{7,6},{8,9},{9,8},{10,11... | collective-permute-start | bytes 786440 | tf_op jit(solution)/shard_map/ppermute | solution.py:46

commit v3 on v1

--- a/solution.py
+++ b/solution.py
@@ -1,9 +1,10 @@
+import functools
 import math
 
 import jax
 import jax.numpy as jnp
 from jax import lax
-from jax.sharding import PartitionSpec as P
+from jax.sharding import Mesh, PartitionSpec as P
 
 damping = 0.1
 jitter = 1e-06
@@ -15,8 +16,49 @@
     )
 
 
-def local(hidden, routes, slots, down_weight, omega):
-    n_exp = lax.axis_size("expert")
+def torus_axes(n_exp):
+    if n_exp == 128:
+        return (("z", 8), ("x", 4), ("y", 4))
+    return (("e", n_exp),)
+
+
+def scatter_sum(term, orders, axes):
+    n_exp, rows, cols = term.shape
+    sizes = [size for _, size in axes]
+    width = cols // len(orders)
+    outs = []
+    for s, order in enumerate(orders):
+        part = term[:, :, s * width:(s + 1) * width].reshape(sizes + [rows, width])
+        part = part.transpose(list(order) + [len(axes), len(axes) + 1])
+        for a in order:
+            name, size = axes[a]
+            part = lax.all_to_all(part, name, 0, 0).sum(axis=0)
+        outs.append(part.reshape(rows, width))
+    return jnp.concatenate(outs, axis=-1)
+
+
+def all_sum(x, orders, axes):
+    height = x.shape[0] // len(orders)
+    outs = []
+    for s, order in enumerate(orders):
+        part = x[s * height:(s + 1) * height]
+        for a in order:
+            name, size = axes[a]
+            part = lax.all_to_all(jnp.broadcast_to(part, (size,) + part.shape), name, 0, 0).sum(axis=0)
+        outs.append(part)
+    x = jnp.concatenate(outs, axis=0)
+    return x + lax.ppermute(x, "dp", [(0, 1), (1, 0)])
+
+
+def axis_orders(n_ax):
+    if n_ax == 3:
+        return [(2, 1, 0), (1, 2, 0)]
+    return [tuple(range(n_ax))] * 2
+
+
+def local(hidden, routes, slots, down_weight, omega, axes):
+    expert = tuple(name for name, _ in axes)
+    n_exp = math.prod(size for _, size in axes)
     n_dp = lax.axis_size("dp")
     tok_rows, n_route, hid_width = hidden.shape
     capacity = 2 * tok_rows * n_route // n_exp
@@ -28,7 +70,7 @@
         .set(hidden.reshape(-1, hid_width))
         .reshape(n_exp, capacity, hid_width)
     )
-    received = lax.all_to_all(outgoing, "expert", split_axis=0, concat_axis=0, tiled=True).reshape(
+    received = lax.all_to_all(outgoing, expert, split_axis=0, concat_axis=0, tiled=True).reshape(
         n_exp * capacity, hid_width
     )
     partner = lax.ppermute(received, "dp", [(0, 1), (1, 0)])
@@ -45,10 +87,9 @@
     down_half = down_weight[0]
     half_cols = down_half.shape[1]
     term = contract(down_half, test_mat).reshape(n_exp, half_cols // n_exp, -1)
-    sketch = lax.psum_scatter(term, "expert", scatter_dimension=0, tiled=True)[0]
-    small_gram = lax.psum(
-        jnp.dot(sketch.T, sketch, precision=lax.Precision.HIGHEST), ("expert", "dp")
-    )
+    orders = axis_orders(len(axes))
+    sketch = scatter_sum(term, orders, axes)
+    small_gram = all_sum(jnp.dot(sketch.T, sketch, precision=lax.Precision.HIGHEST), orders, axes)
     qr_factor = jnp.linalg.cholesky(small_gram)
     basis_rows = jax.scipy.linalg.solve_triangular(qr_factor, sketch.T, lower=True).T * math.sqrt(
         half_cols * n_dp
@@ -60,17 +101,21 @@
 
 
 def solution(mesh):
+    n_exp = mesh.shape["expert"]
+    axes = torus_axes(n_exp)
+    names = tuple(name for name, _ in axes)
+    grid = Mesh(mesh.devices.reshape([size for _, size in axes] + [mesh.shape["dp"]]), names + ("dp",))
     placed = (
-        P(("expert", "dp"), None, None),
-        P(("expert", "dp"), None),
-        P(("expert", "dp"), None),
-        P("expert", None, "dp"),
-        P("expert", None, None),
+        P(names + ("dp",), None, None),
+        P(names + ("dp",), None),
+        P(names + ("dp",), None),
+        P(names, None, "dp"),
+        P(names, None, None),
     )
     return jax.shard_map(
-        local,
-        mesh=mesh,
+        functools.partial(local, axes=axes),
+        mesh=grid,
         in_specs=placed,
-        out_specs=(P("expert", "dp", None), P("dp", "expert", None)),
+        out_specs=(P(names, "dp", None), P("dp", names, None)),
         check_vma=False,
     )

time: 1420 us -> 657 us (0.46)
  waiting for transfers between devices: 953 us -> 126 us
  starting transfers between devices: 4.13 us -> 59.1 us
    reduce_scatter x1 -> x0, waiting for transfers between devices: 605 us -> none  [local(): lax.psum_scatter(term, 'expert', scatter_dimension=0, tiled=True)[0]]
    psum x1 -> x0, waiting for transfers between devices: 346 us -> none  [local(): lax.psum(jnp.dot(sketch.T, sketch, precision=lax.Precision.HIGHEST), ('ex...]
    all_to_all x0 -> x11, waiting for transfers between devices: none -> 123 us  [the longest x6 66.9 us: scatter_sum(): part = lax.all_to_all(part, name, 0, 0).sum(axis=0)]
    all_to_all x0 -> x11, starting transfers between devices: none -> 39.6 us  [the longest x6 22.1 us: scatter_sum(): part = lax.all_to_all(part, name, 0, 0).sum(axis=0)]
    ppermute x0 -> x1, starting transfers between devices: none -> 16.2 us  [all_sum(): return x + lax.ppermute(x, 'dp', [(0, 1), (1, 0)])]
    all_to_all x1 -> x2, blocking collectives: 110 us -> 119 us  [the longest x1 110 us: local(): lax.all_to_all(outgoing, expert, split_axis=0, concat_axis=0, tiled=True)]
  transfers between devices with their start and end apart: 3 -> 13, of which waited for: 3 -> 12; matrix products, arithmetic and copies ran while one was open for 1% -> 2% of each run, Pallas kernels for 0% -> 0%
where the time goes in v3:
time: 657 us; the launch traced here: 650 us
  other arithmetic  238 us (36%)
  waiting for transfers between devices  126 us (19%)
  blocking collectives  119 us (18%)
  starting transfers between devices  59.1 us (9%)
  local copies, waits for them, and re-layouts  53.1 us (8%)
  matrix products  45.3 us (7%)
  between operations  8.55 us (1%)
    another operation x30, other arithmetic, local(): whitening = jnp.linalg.cholesky(damped)  172 us
    all_to_all x1, blocking collectives, local(): lax.all_to_all(outgoing, expert, split_axis=0, concat_axis=0, tiled=True)  110 us
    all_to_all x6, waiting for transfers between devices, scatter_sum(): part = lax.all_to_all(part, name, 0, 0).sum(axis=0)  66.9 us
    all_to_all x5, waiting for transfers between devices, all_sum(): lax.all_to_all(jnp.broadcast_to(part, (size,) + part.shape), name, 0, 0)  56.6 us
    another operation x7, other arithmetic, local(): qr_factor = jnp.linalg.cholesky(small_gram)  34.6 us
    another operation x14, matrix products, local(): whitening = jnp.linalg.cholesky(damped)  23.1 us
    all_to_all x6, starting transfers between devices, scatter_sum(): part = lax.all_to_all(part, name, 0, 0).sum(axis=0)  22.1 us
    another operation x3, other arithmetic, local(): jax.scipy.linalg.solve_triangular(qr_factor, sketch.T, lower=True)  19.7 us
  transfers between devices with their start and end apart: 13, of which 12 were waited for; matrix products, arithmetic and copies ran while one was open for 2% of the time, Pallas kernels for 0%

profile of v3, /device:TPU:1, one launch (start us, length us, event | category | flops | bytes accessed | tf_op | source)
XLA Modules:
  0.0 649.7 jit_solution(10343015556284294394)
XLA Ops:
  2.3 7.9 %scatter_custom_fusion = bf16[2048,1024]{1,0:T(8,128)(2,1)} fusion(s32[1024]{0:T(1024)S(1)} %bitcast.125, bf16[128,8,1024]{2,1,0:T(8,128)(2,1)S(1)} %copy-done, bf16[]{:T(256)} %constant.336.clone.1), kind=kCustom, calls=%fused_computation.17 | custom fusion | bytes 6291458 | tf_op jit(solution)/shard_map/scatter | solution.py:70
  10.1 110.1 %all_to_all.65 = bf16[128,16,1024]{2,1,0:T(8,128)(2,1)S(1)} all-to-all(bf16[128,16,1024]{2,1,0:T(8,128)(2,1)} %bitcast.119), channel_id=1, replica_groups=mesh['z'=8,'x'=4,'y'=4,'dp'=2] {'z','x','y'}, dimensions={0} | all-to-all | bytes 8388608 | tf_op jit(solution)/shard_map/all_to_all | solution.py:73
  130.3 7.2 %select_reduce_fusion = (f32[]{:T(128)}, f32[1024,1024]{1,0:T(8,128)}) fusion(bf16[2048,1024]{1,0:T(8,128)(2,1)S(1)} %collective-permute-done, f32[1024,1024,1]{1,0,2:T(8,128)S(1)} %fusion.72), kind=kOutput, calls=%fused_computation.14 | convolution fusion | flops 4300210176 | bytes 12582916 | tf_op jit(solution)/shard_map/dot_general | solution.py:14
  150.3 11.7 %cholesky.249 = f32[128,128]{1,0:T(8,128)S(1)} custom-call(f32[128,128]{1,0:T(8,128)S(1)} %cholesky.650), custom_call_target="Cholesky" | custom-call | tf_op jit(solution)/shard_map/jit(cholesky)/cholesky | solution.py:83
  162.0 9.8 %custom-call.67 = f32[1,128,128]{1,2,0:T(8,128)S(1)} custom-call(f32[1,128,128]{2,1,0:T(8,128)S(1)} %get-tuple-element.62), custom_call_target="InvertDiagBlocksLowerTriangular" | custom-call | tf_op jit(solution)/shard_map/jit(cholesky)/cholesky | solution.py:83
  178.3 11.9 %cholesky.274 = f32[128,128]{1,0:T(8,128)S(1)} custom-call(f32[128,128]{1,0:T(8,128)S(1)} %cholesky.654), custom_call_target="Cholesky" | custom-call | tf_op jit(solution)/shard_map/jit(cholesky)/cholesky | solution.py:83
  190.8 9.8 %custom-call.68 = f32[1,128,128]{1,2,0:T(8,128)S(1)} custom-call(f32[1,128,128]{2,1,0:T(8,128)S(1)} %get-tuple-element.59), custom_call_target="InvertDiagBlocksLowerTriangular" | custom-call | tf_op jit(solution)/shard_map/jit(cholesky)/cholesky | solution.py:83
  203.9 11.7 %cholesky.299 = f32[128,128]{1,0:T(8,128)S(1)} custom-call(f32[128,128]{1,0:T(8,128)S(1)} %cholesky.659), custom_call_target="Cholesky" | custom-call | tf_op jit(solution)/shard_map/jit(cholesky)/cholesky | solution.py:83
  216.9 9.8 %custom-call.69 = f32[1,128,128]{1,2,0:T(8,128)S(1)} custom-call(f32[1,128,128]{2,1,0:T(8,128)S(1)} %get-tuple-element.56), custom_call_target="InvertDiagBlocksLowerTriangular" | custom-call | tf_op jit(solution)/shard_map/jit(cholesky)/cholesky | solution.py:83
  230.2 11.9 %cholesky.539 = f32[128,128]{1,0:T(8,128)S(1)} custom-call(f32[128,128]{1,0:T(8,128)S(1)} %cholesky.664), custom_call_target="Cholesky" | custom-call | tf_op jit(solution)/shard_map/jit(cholesky)/cholesky | solution.py:83
  243.4 9.8 %custom-call.70 = f32[1,128,128]{1,2,0:T(8,128)S(1)} custom-call(f32[1,128,128]{2,1,0:T(8,128)S(1)} %get-tuple-element.53), custom_call_target="InvertDiagBlocksLowerTriangular" | custom-call | tf_op jit(solution)/shard_map/jit(cholesky)/cholesky | solution.py:83
  256.7 11.7 %cholesky.558 = f32[128,128]{1,0:T(8,128)S(1)} custom-call(f32[128,128]{1,0:T(8,128)S(1)} %cholesky.669), custom_call_target="Cholesky" | custom-call | tf_op jit(solution)/shard_map/jit(cholesky)/cholesky | solution.py:83
  269.7 10.2 %custom-call.71 = f32[1,128,128]{1,2,0:T(8,128)S(1)} custom-call(f32[1,128,128]{2,1,0:T(8,128)S(1)} %get-tuple-element.50), custom_call_target="InvertDiagBlocksLowerTriangular" | custom-call | tf_op jit(solution)/shard_map/jit(cholesky)/cholesky | solution.py:83
  283.2 11.7 %cholesky.578 = f32[128,128]{1,0:T(8,128)S(1)} custom-call(f32[128,128]{1,0:T(8,128)S(1)} %cholesky.674), custom_call_target="Cholesky" | custom-call | tf_op jit(solution)/shard_map/jit(cholesky)/cholesky | solution.py:83
  296.2 9.8 %custom-call.72 = f32[1,128,128]{1,2,0:T(8,128)S(1)} custom-call(f32[1,128,128]{2,1,0:T(8,128)S(1)} %get-tuple-element.47), custom_call_target="InvertDiagBlocksLowerTriangular" | custom-call | tf_op jit(solution)/shard_map/jit(cholesky)/cholesky | solution.py:83
  309.0 11.8 %cholesky.598 = f32[128,128]{1,0:T(8,128)S(1)} custom-call(f32[128,128]{1,0:T(8,128)S(1)} %cholesky.679), custom_call_target="Cholesky" | custom-call | tf_op jit(solution)/shard_map/jit(cholesky)/cholesky | solution.py:83
  322.1 9.8 %custom-call.75 = f32[1,128,128]{1,2,0:T(8,128)S(1)} custom-call(f32[1,128,128]{2,1,0:T(8,128)S(1)} %get-tuple-element.44), custom_call_target="InvertDiagBlocksLowerTriangular" | custom-call | tf_op jit(solution)/shard_map/jit(cholesky)/cholesky/custom-call.17 | solution.py:83
  334.6 11.7 %cholesky.612 = f32[128,128]{1,0:T(8,128)S(1)} custom-call(f32[128,128]{1,0:T(8,128)S(1)} %slice_subtract_fusion.7), custom_call_target="Cholesky" | custom-call | tf_op jit(solution)/shard_map/jit(cholesky)/cholesky | solution.py:83
  359.9 7.0 %fusion.2 = f32[3584,256]{0,1:T(8,128)} fusion(bf16[1024,256]{1,0:T(8,128)(2,1)S(1)} %convolution_convert_fusion, bf16[1,1024,3584]{2,1,0:T(8,128)(2,1)} %param.10), kind=kOutput, calls=%fused_computation.7 | convolution fusion | flops 1879048192 | bytes 11534336 | tf_op jit(solution)/shard_map/dot_general | solution.py:14
  389.4 20.7 %all-to-all-done.1 = f32[4,4,8,28,128]{4,2,3,1,0:T(8,128)} async-done(((f32[4,4,8,28,128]{4,2,3,1,0:T(8,128)}), f32[4,4,8,28,128]{4,2,3,1,0:T(8,128)}, u32[]{:S(2)}, u32[]{:S(2)}) %all-to-all-start.1) | async-done | bytes 1835040 | tf_op jit(solution)/shard_map/all_to_all | solution.py:35
  416.1 19.7 %all-to-all-done.4 = f32[4,4,8,28,128]{4,2,3,1,0:T(8,128)S(1)} async-done(((f32[4,4,8,28,128]{4,2,3,1,0:T(8,128)}), f32[4,4,8,28,128]{4,2,3,1,0:T(8,128)S(1)}, u32[]{:S(2)}, u32[]{:S(2)}) %all-to-all-start.4) | async-done | bytes 1835040 | tf_op jit(solution)/shard_map/all_to_all | solution.py:35
  460.3 7.2 %all-to-all-done.3 = f32[8,28,128]{2,1,0:T(8,128)S(1)} async-done(((f32[8,28,128]{2,1,0:T(8,128)}), f32[8,28,128]{2,1,0:T(8,128)S(1)}, u32[]{:S(2)}, u32[]{:S(2)}) %all-to-all-start.3) | async-done | bytes 114720 | tf_op jit(solution)/shard_map/all_to_all | solution.py:35
  470.9 7.8 %all-to-all-done.6 = f32[8,28,128]{2,1,0:T(8,128)S(1)} async-done(((f32[8,28,128]{2,1,0:T(8,128)}), f32[8,28,128]{2,1,0:T(8,128)S(1)}, u32[]{:S(2)}, u32[]{:S(2)}) %all-to-all-start.6) | async-done | bytes 114720 | tf_op jit(solution)/shard_map/all_to_all | solution.py:35
  479.2 9.3 %all_to_all.66 = f32[4,128,256]{2,1,0:T(8,128)S(1)} all-to-all(f32[4,128,256]{2,1,0:T(8,128)S(1)} %broadcast_in_dim.39), channel_id=1, replica_groups=mesh['z'=8,'x'=4,'y'=4,'dp'=2] {'y'}, dimensions={0} | all-to-all | bytes 1048576 | tf_op jit(solution)/shard_map/all_to_all | solution.py:47
  504.1 7.0 %all-to-all-done.8 = f32[4,128,256]{2,1,0:T(8,128)S(1)} async-done(((f32[4,128,256]{2,1,0:T(8,128)}), f32[4,128,256]{2,1,0:T(8,128)S(1)}, u32[]{:S(2)}, u32[]{:S(2)}) %all-to-all-start.8) | async-done | bytes 524320 | tf_op jit(solution)/shard_map/all_to_all | solution.py:47
  527.0 17.8 %all-to-all-done.9 = f32[8,128,256]{2,1,0:T(8,128)S(1)} async-done(((f32[8,128,256]{2,1,0:T(8,128)}), f32[8,128,256]{2,1,0:T(8,128)S(1)}, u32[]{:S(2)}, u32[]{:S(2)}) %all-to-all-start.9) | async-done | bytes 1048608 | tf_op jit(solution)/shard_map/all_to_all | solution.py:47
  549.6 18.0 %all-to-all-done.12 = f32[8,128,256]{2,1,0:T(8,128)S(1)} async-done(((f32[8,128,256]{2,1,0:T(8,128)}), f32[8,128,256]{2,1,0:T(8,128)S(1)}, u32[]{:S(2)}, u32[]{:S(2)}) %all-to-all-start.12) | async-done | bytes 1048608 | tf_op jit(solution)/shard_map/all_to_all | solution.py:47
  567.9 16.2 %collective-permute-start.1 = (f32[256,256]{0,1:T(8,128)S(1)}, f32[256,256]{0,1:T(8,128)S(1)}, u32[]{:S(2)}, u32[]{:S(2)}) collective-permute-start(f32[256,256]{0,1:T(8,128)S(1)} %pad_maximum_fusion), channel_id=1, source_target_pairs={{0,1},{1,0},{2,3},{3,2},{4,5},{5,4},{6,7},{7,6},{8,9},{9,8},{10,11... | collective-permute-start | bytes 786440 | tf_op jit(solution)/shard_map/ppermute | solution.py:50
  587.4 11.7 %cholesky.625 = f32[128,128]{1,0:T(8,128)S(1)} custom-call(f32[128,128]{1,0:T(8,128)S(1)} %cholesky.683), custom_call_target="Cholesky" | custom-call | tf_op jit(solution)/shard_map/jit(cholesky)/cholesky | solution.py:93
  599.2 9.8 %custom-call.76 = f32[1,128,128]{1,2,0:T(8,128)S(1)} custom-call(f32[1,128,128]{2,1,0:T(8,128)S(1)} %get-tuple-element.40), custom_call_target="InvertDiagBlocksLowerTriangular" | custom-call | tf_op jit(solution)/shard_map/jit(cholesky)/cholesky/custom-call.17 | solution.py:93
  609.5 11.7 %cholesky.634 = f32[128,128]{1,0:T(8,128)S(1)} custom-call(f32[128,128]{1,0:T(8,128)S(1)} %slice_subtract_fusion.6), custom_call_target="Cholesky" | custom-call | tf_op jit(solution)/shard_map/jit(cholesky)/cholesky | solution.py:93
  628.3 19.7 %custom-call.73 = f32[2,128,128]{1,2,0:T(8,128)S(1)} custom-call(f32[2,128,128]{2,1,0:T(8,128)S(1)} %get-tuple-element.10), custom_call_target="InvertDiagBlocksLowerTriangular" | custom-call | tf_op jit(solution)/shard_map/jit(_solve_triangular)/triangular_solve | solution.py:94
  (133 shorter events, 173.2 us)
Async XLA Ops:
  0.6 1.6 copy-start
  120.2 10.1 %collective-permute-start = (bf16[2048,1024]{1,0:T(8,128)(2,1)S(1)}, bf16[2048,1024]{1,0:T(8,128)(2,1)S(1)}, u32[]{:S(2)}, u32[]{:S(2)}) collective-permute-start(bf16[2048,1024]{1,0:T(8,128)(2,1)S(1)} %bitcast.124), channel_id=1, source_target_pairs={{0,1},{1,0},{2,3},{3,2},{4,5},{5,4},{6,7},{7,6},{8,9},{9,8},{10,11... | collective-permute-start | bytes 12582920 | tf_op jit(solution)/shard_map/ppermute | solution.py:76
  148.3 1.9 copy-start.3
  353.2 4.7 copy-start.4
  355.9 1.9 copy-start.2
  382.3 27.7 %all-to-all-start.1 = ((f32[4,4,8,28,128]{4,2,3,1,0:T(8,128)}), f32[4,4,8,28,128]{4,2,3,1,0:T(8,128)}, u32[]{:S(2)}, u32[]{:S(2)}) async-start(f32[4,4,8,28,128]{4,2,3,1,0:T(8,128)} %bitcast.123), calls=%async_computation.1 | async-start | bytes 3670016 | tf_op jit(solution)/shard_map/all_to_all | solution.py:35
  410.0 25.8 %all-to-all-start.4 = ((f32[4,4,8,28,128]{4,2,3,1,0:T(8,128)}), f32[4,4,8,28,128]{4,2,3,1,0:T(8,128)S(1)}, u32[]{:S(2)}, u32[]{:S(2)}) async-start(f32[4,4,8,28,128]{4,2,3,1,0:T(8,128)} %bitcast.122), calls=%async_computation.4 | async-start | bytes 3670016 | tf_op jit(solution)/shard_map/all_to_all | solution.py:35
  435.8 10.0 %all-to-all-start.2 = ((f32[4,8,28,128]{3,1,2,0:T(8,128)}), f32[4,8,28,128]{3,1,2,0:T(8,128)S(1)}, u32[]{:S(2)}, u32[]{:S(2)}) async-start(f32[4,8,28,128]{3,1,2,0:T(8,128)} %reduce_sum.118), calls=%async_computation.2 | async-start | bytes 917504 | tf_op jit(solution)/shard_map/all_to_all | solution.py:35
  445.8 10.0 %all-to-all-start.5 = ((f32[4,8,28,128]{3,1,2,0:T(8,128)}), f32[4,8,28,128]{3,1,2,0:T(8,128)S(1)}, u32[]{:S(2)}, u32[]{:S(2)}) async-start(f32[4,8,28,128]{3,1,2,0:T(8,128)} %reduce_sum.121), calls=%async_computation.5 | async-start | bytes 917504 | tf_op jit(solution)/shard_map/all_to_all | solution.py:35
  455.8 11.6 %all-to-all-start.3 = ((f32[8,28,128]{2,1,0:T(8,128)}), f32[8,28,128]{2,1,0:T(8,128)S(1)}, u32[]{:S(2)}, u32[]{:S(2)}) async-start(f32[8,28,128]{2,1,0:T(8,128)} %copy.73), calls=%async_computation.3 | async-start | bytes 262144 | tf_op jit(solution)/shard_map/all_to_all | solution.py:35
  467.5 11.2 %all-to-all-start.6 = ((f32[8,28,128]{2,1,0:T(8,128)}), f32[8,28,128]{2,1,0:T(8,128)S(1)}, u32[]{:S(2)}, u32[]{:S(2)}) async-start(f32[8,28,128]{2,1,0:T(8,128)} %copy.77), calls=%async_computation.6 | async-start | bytes 262144 | tf_op jit(solution)/shard_map/all_to_all | solution.py:35
  489.4 10.4 %all-to-all-start.10 = ((f32[4,128,256]{2,1,0:T(8,128)}), f32[4,128,256]{2,1,0:T(8,128)S(1)}, u32[]{:S(2)}, u32[]{:S(2)}) async-start(f32[4,128,256]{2,1,0:T(8,128)} %broadcast_in_dim.42), calls=%async_computation.10 | async-start | bytes 1048576 | tf_op jit(solution)/shard_map/all_to_all | solution.py:47
  500.6 10.6 %all-to-all-start.8 = ((f32[4,128,256]{2,1,0:T(8,128)}), f32[4,128,256]{2,1,0:T(8,128)S(1)}, u32[]{:S(2)}, u32[]{:S(2)}) async-start(f32[4,128,256]{2,1,0:T(8,128)} %broadcast_in_dim.40), calls=%async_computation.8 | async-start | bytes 1048576 | tf_op jit(solution)/shard_map/all_to_all | solution.py:47
  512.0 10.4 %all-to-all-start.11 = ((f32[4,128,256]{2,1,0:T(8,128)}), f32[4,128,256]{2,1,0:T(8,128)S(1)}, u32[]{:S(2)}, u32[]{:S(2)}) async-start(f32[4,128,256]{2,1,0:T(8,128)} %broadcast_in_dim.43), calls=%async_computation.11 | async-start | bytes 1048576 | tf_op jit(solution)/shard_map/all_to_all | solution.py:47
  523.4 21.4 %all-to-all-start.9 = ((f32[8,128,256]{2,1,0:T(8,128)}), f32[8,128,256]{2,1,0:T(8,128)S(1)}, u32[]{:S(2)}, u32[]{:S(2)}) async-start(f32[8,128,256]{2,1,0:T(8,128)} %broadcast_in_dim.41), calls=%async_computation.9 | async-start | bytes 2097152 | tf_op jit(solution)/shard_map/all_to_all | solution.py:47
  545.9 21.8 %all-to-all-start.12 = ((f32[8,128,256]{2,1,0:T(8,128)}), f32[8,128,256]{2,1,0:T(8,128)S(1)}, u32[]{:S(2)}, u32[]{:S(2)}) async-start(f32[8,128,256]{2,1,0:T(8,128)} %broadcast_in_dim.44), calls=%async_computation.12 | async-start | bytes 2097152 | tf_op jit(solution)/shard_map/all_to_all | solution.py:47
  567.8 81.4 %copy-start.1 = (bf16[128,8,1024]{2,1,0:T(8,128)(2,1)S(1)}, bf16[128,8,1024]{2,1,0:T(8,128)(2,1)}, u32[]{:S(2)}) copy-start(bf16[128,8,1024]{2,1,0:T(8,128)(2,1)} %param.7) | copy-start | bytes 6291460
  567.9 19.4 %collective-permute-start.1 = (f32[256,256]{0,1:T(8,128)S(1)}, f32[256,256]{0,1:T(8,128)S(1)}, u32[]{:S(2)}, u32[]{:S(2)}) collective-permute-start(f32[256,256]{0,1:T(8,128)S(1)} %pad_maximum_fusion), channel_id=1, source_target_pairs={{0,1},{1,0},{2,3},{3,2},{4,5},{5,4},{6,7},{7,6},{8,9},{9,8},{10,11... | collective-permute-start | bytes 786440 | tf_op jit(solution)/shard_map/ppermute | solution.py:50

commit v4 on v2

--- a/solution.py
+++ b/solution.py
@@ -20,14 +20,16 @@
 
 
 def scatter_sum(term, orders):
-    n_exp, rows, cols = term.shape
+    cols = term.shape[0]
+    n_exp = lax.axis_size("expert")
+    rows = term.shape[1] // n_exp
     n_bits = n_exp.bit_length() - 1
     me = lax.axis_index("expert")
     width = cols // len(orders)
     outs = []
     for s, order in enumerate(orders):
-        part = term[:, :, s * width:(s + 1) * width].reshape([2] * n_bits + [rows, width])
-        perm = [n_bits - 1 - b for b in order] + [n_bits, n_bits + 1]
+        part = term[s * width:(s + 1) * width].reshape([width] + [2] * n_bits + [rows])
+        perm = [n_bits - b for b in order] + [n_bits + 1, 0]
         part = part.transpose(perm).reshape(n_exp, rows, width)
         for b in order:
             half = part.shape[0] // 2
@@ -85,17 +87,17 @@
     )
     diag_mean = jnp.sum(jnp.where(on_diag, gram_mat, 0.0)) / hid_width
     damped = jnp.where(on_diag, gram_mat + (damping * diag_mean + jitter), gram_mat)
-    whitening = jnp.linalg.cholesky(damped)
+    whitening = jnp.linalg.cholesky(damped, symmetrize_input=False)
     test_mat = jnp.dot(
         whitening, omega[0].astype(jnp.float32), precision=lax.Precision.HIGHEST
     ).astype(jnp.bfloat16)
     down_half = down_weight[0]
     half_cols = down_half.shape[1]
-    term = contract(down_half, test_mat).reshape(n_exp, half_cols // n_exp, -1)
+    term = contract(test_mat, down_half)
     orders = bit_orders(n_exp, 2)
     sketch = scatter_sum(term, orders)
     small_gram = all_sum(jnp.dot(sketch.T, sketch, precision=lax.Precision.HIGHEST), orders[0])
-    qr_factor = jnp.linalg.cholesky(small_gram)
+    qr_factor = jnp.linalg.cholesky(small_gram, symmetrize_input=False)
     basis_rows = jax.scipy.linalg.solve_triangular(qr_factor, sketch.T, lower=True).T * math.sqrt(
         half_cols * n_dp
     )

time: 602 us -> 587 us (0.975)
  local copies, waits for them, and re-layouts: 49.5 us -> 37.6 us
  transfers between devices with their start and end apart: 24 -> 24, of which waited for: 19 -> 18; matrix products, arithmetic and copies ran while one was open for 3% -> 4% of each run, Pallas kernels for 0% -> 0%
where the time goes in v4:
time: 587 us; the launch traced here: 578 us
  other arithmetic  238 us (41%)
  waiting for transfers between devices  178 us (30%)
  starting transfers between devices  68.8 us (12%)
  matrix products  46.9 us (8%)
  local copies, waits for them, and re-layouts  37.6 us (6%)
  between operations  8.77 us (1%)
    another operation x30, other arithmetic, local(): whitening = jnp.linalg.cholesky(damped, symmetrize_input=False)  172 us
    all_to_all x1, waiting for transfers between devices, local(): lax.all_to_all(outgoing, 'expert', split_axis=0, concat_axis=0, tiled=True)  93.3 us
    ppermute x14, waiting for transfers between devices, scatter_sum(): part = keep + lax.ppermute(send, 'expert', xor_pairs(n_exp, 1 << b))  42.7 us
    ppermute x7, waiting for transfers between devices, all_sum(): x = x + lax.ppermute(x, 'expert', xor_pairs(n_exp, 1 << b))  41.9 us
    another operation x7, other arithmetic, local(): qr_factor = jnp.linalg.cholesky(small_gram, symmetrize_input=False)  34.7 us
    another operation x14, matrix products, local(): whitening = jnp.linalg.cholesky(damped, symmetrize_input=False)  23.3 us
    dot_general x3, matrix products, contract(): lax.dot_general(left, right, (((0,), (0,)), ((), ())), preferred_element_...  20.1 us
    another operation x3, other arithmetic, local(): jax.scipy.linalg.solve_triangular(qr_factor, sketch.T, lower=True)  19.7 us
  transfers between devices with their start and end apart: 24, of which 18 were waited for; matrix products, arithmetic and copies ran while one was open for 4% of the time, Pallas kernels for 0%

profile of v4, /device:TPU:1, one launch (start us, length us, event | category | flops | bytes accessed | tf_op | source)
XLA Modules:
  0.0 578.2 jit_solution(681176644293211632)
XLA Ops:
  2.3 7.9 %scatter_custom_fusion = bf16[2048,1024]{1,0:T(8,128)(2,1)} fusion(s32[1024]{0:T(1024)S(1)} %bitcast.118, bf16[128,8,1024]{2,1,0:T(8,128)(2,1)S(1)} %copy-done, bf16[]{:T(256)} %constant.345.clone.1), kind=kCustom, calls=%fused_computation.12 | custom fusion | bytes 6291458 | tf_op jit(solution)/shard_map/scatter | solution.py:77
  10.2 16.9 %all-to-all-start = ((bf16[128,16,1024]{2,1,0:T(8,128)(2,1)}), bf16[128,16,1024]{2,1,0:T(8,128)(2,1)}, u32[]{:S(2)}, u32[]{:S(2)}) async-start(bf16[128,16,1024]{2,1,0:T(8,128)(2,1)} %bitcast.113), calls=%async_computation | async-start | bytes 8388608 | tf_op jit(solution)/shard_map/all_to_all | solution.py:80
  27.1 93.3 %all-to-all-done = bf16[128,16,1024]{2,1,0:T(8,128)(2,1)} async-done(((bf16[128,16,1024]{2,1,0:T(8,128)(2,1)}), bf16[128,16,1024]{2,1,0:T(8,128)(2,1)}, u32[]{:S(2)}, u32[]{:S(2)}) %all-to-all-start) | async-done | bytes 4194336 | tf_op jit(solution)/shard_map/all_to_all | solution.py:80
  123.5 7.6 %fusion.64 = f32[1024,1024,1]{1,0,2:T(8,128)S(1)} fusion(bf16[128,16,1024]{2,1,0:T(8,128)(2,1)} %all-to-all-done), kind=kOutput, calls=%fused_computation.160 | convolution fusion | flops 4294967296 | bytes 8388608 | tf_op jit(solution)/shard_map/dot_general | solution.py:13
  131.1 7.4 %select_reduce_fusion = (f32[]{:T(128)}, f32[1024,1024]{1,0:T(8,128)}) fusion(bf16[2048,1024]{1,0:T(8,128)(2,1)S(1)} %collective-permute-done, f32[1024,1024,1]{1,0,2:T(8,128)S(1)} %fusion.64), kind=kOutput, calls=%fused_computation.9 | convolution fusion | flops 4300210176 | bytes 12582916 | tf_op jit(solution)/shard_map/dot_general | solution.py:13
  143.7 11.7 %cholesky.249 = f32[128,128]{1,0:T(8,128)S(1)} custom-call(f32[128,128]{1,0:T(8,128)S(1)} %cholesky.650), custom_call_target="Cholesky" | custom-call | tf_op jit(solution)/shard_map/jit(cholesky)/cholesky | solution.py:90
  155.4 9.8 %custom-call.67 = f32[1,128,128]{1,2,0:T(8,128)S(1)} custom-call(f32[1,128,128]{2,1,0:T(8,128)S(1)} %get-tuple-element.60), custom_call_target="InvertDiagBlocksLowerTriangular" | custom-call | tf_op jit(solution)/shard_map/jit(cholesky)/cholesky | solution.py:90
  171.7 11.7 %cholesky.274 = f32[128,128]{1,0:T(8,128)S(1)} custom-call(f32[128,128]{1,0:T(8,128)S(1)} %cholesky.654), custom_call_target="Cholesky" | custom-call | tf_op jit(solution)/shard_map/jit(cholesky)/cholesky | solution.py:90
  184.0 10.2 %custom-call.68 = f32[1,128,128]{1,2,0:T(8,128)S(1)} custom-call(f32[1,128,128]{2,1,0:T(8,128)S(1)} %get-tuple-element.57), custom_call_target="InvertDiagBlocksLowerTriangular" | custom-call | tf_op jit(solution)/shard_map/jit(cholesky)/cholesky | solution.py:90
  197.6 11.7 %cholesky.299 = f32[128,128]{1,0:T(8,128)S(1)} custom-call(f32[128,128]{1,0:T(8,128)S(1)} %cholesky.659), custom_call_target="Cholesky" | custom-call | tf_op jit(solution)/shard_map/jit(cholesky)/cholesky | solution.py:90
  210.6 9.8 %custom-call.69 = f32[1,128,128]{1,2,0:T(8,128)S(1)} custom-call(f32[1,128,128]{2,1,0:T(8,128)S(1)} %get-tuple-element.54), custom_call_target="InvertDiagBlocksLowerTriangular" | custom-call | tf_op jit(solution)/shard_map/jit(cholesky)/cholesky | solution.py:90
  223.9 11.9 %cholesky.539 = f32[128,128]{1,0:T(8,128)S(1)} custom-call(f32[128,128]{1,0:T(8,128)S(1)} %cholesky.664), custom_call_target="Cholesky" | custom-call | tf_op jit(solution)/shard_map/jit(cholesky)/cholesky | solution.py:90
  237.0 9.8 %custom-call.70 = f32[1,128,128]{1,2,0:T(8,128)S(1)} custom-call(f32[1,128,128]{2,1,0:T(8,128)S(1)} %get-tuple-element.51), custom_call_target="InvertDiagBlocksLowerTriangular" | custom-call | tf_op jit(solution)/shard_map/jit(cholesky)/cholesky | solution.py:90
  250.3 11.7 %cholesky.558 = f32[128,128]{1,0:T(8,128)S(1)} custom-call(f32[128,128]{1,0:T(8,128)S(1)} %cholesky.669), custom_call_target="Cholesky" | custom-call | tf_op jit(solution)/shard_map/jit(cholesky)/cholesky | solution.py:90
  263.3 9.8 %custom-call.71 = f32[1,128,128]{1,2,0:T(8,128)S(1)} custom-call(f32[1,128,128]{2,1,0:T(8,128)S(1)} %get-tuple-element.48), custom_call_target="InvertDiagBlocksLowerTriangular" | custom-call | tf_op jit(solution)/shard_map/jit(cholesky)/cholesky | solution.py:90
  276.7 11.7 %cholesky.578 = f32[128,128]{1,0:T(8,128)S(1)} custom-call(f32[128,128]{1,0:T(8,128)S(1)} %cholesky.674), custom_call_target="Cholesky" | custom-call | tf_op jit(solution)/shard_map/jit(cholesky)/cholesky | solution.py:90
  289.6 9.8 %custom-call.72 = f32[1,128,128]{1,2,0:T(8,128)S(1)} custom-call(f32[1,128,128]{2,1,0:T(8,128)S(1)} %get-tuple-element.45), custom_call_target="InvertDiagBlocksLowerTriangular" | custom-call | tf_op jit(solution)/shard_map/jit(cholesky)/cholesky | solution.py:90
  302.4 11.7 %cholesky.598 = f32[128,128]{1,0:T(8,128)S(1)} custom-call(f32[128,128]{1,0:T(8,128)S(1)} %cholesky.679), custom_call_target="Cholesky" | custom-call | tf_op jit(solution)/shard_map/jit(cholesky)/cholesky | solution.py:90
  315.5 10.2 %custom-call.75 = f32[1,128,128]{1,2,0:T(8,128)S(1)} custom-call(f32[1,128,128]{2,1,0:T(8,128)S(1)} %get-tuple-element.42), custom_call_target="InvertDiagBlocksLowerTriangular" | custom-call | tf_op jit(solution)/shard_map/jit(cholesky)/cholesky/custom-call.17 | solution.py:90
  328.3 11.7 %cholesky.612 = f32[128,128]{1,0:T(8,128)S(1)} custom-call(f32[128,128]{1,0:T(8,128)S(1)} %slice_subtract_fusion.7), custom_call_target="Cholesky" | custom-call | tf_op jit(solution)/shard_map/jit(cholesky)/cholesky | solution.py:90
  351.9 5.2 fusion
  372.1 14.7 %collective-permute-done.1 = f32[64,28,128]{2,0,1:T(8,128)} collective-permute-done((f32[64,28,128]{2,0,1:T(8,128)}, f32[64,28,128]{2,0,1:T(8,128)}, u32[]{:S(2)}, u32[]{:S(2)}) %collective-permute-start.1) | collective-permute-done | bytes 917536 | tf_op jit(solution)/shard_map/ppermute | solution.py:39
  398.4 6.2 %collective-permute-done.2 = f32[32,28,128]{2,1,0:T(8,128)S(1)} collective-permute-done((f32[32,28,128]{2,1,0:T(8,128)}, f32[32,28,128]{2,1,0:T(8,128)S(1)}, u32[]{:S(2)}, u32[]{:S(2)}) %collective-permute-start.2) | collective-permute-done | bytes 458784 | tf_op jit(solution)/shard_map/ppermute | solution.py:39
  409.9 5.4 collective-permute-done.3
  458.5 5.9 %collective-permute-done.18 = f32[256,256]{1,0:T(8,128)S(1)} collective-permute-done((f32[256,256]{1,0:T(8,128)S(1)}, f32[256,256]{1,0:T(8,128)S(1)}, u32[]{:S(2)}, u32[]{:S(2)}) %collective-permute-start.18) | collective-permute-done | bytes 262176 | tf_op jit(solution)/shard_map/ppermute | solution.py:47
  474.6 6.9 %collective-permute-done.20 = f32[256,256]{1,0:T(8,128)S(1)} collective-permute-done((f32[256,256]{1,0:T(8,128)S(1)}, f32[256,256]{1,0:T(8,128)S(1)}, u32[]{:S(2)}, u32[]{:S(2)}) %collective-permute-start.20) | collective-permute-done | bytes 262176 | tf_op jit(solution)/shard_map/ppermute | solution.py:47
  484.9 11.4 %collective-permute-done.21 = f32[256,256]{1,0:T(8,128)S(1)} collective-permute-done((f32[256,256]{1,0:T(8,128)S(1)}, f32[256,256]{1,0:T(8,128)S(1)}, u32[]{:S(2)}, u32[]{:S(2)}) %collective-permute-start.21) | collective-permute-done | bytes 262176 | tf_op jit(solution)/shard_map/ppermute | solution.py:47
  496.3 16.3 %collective-permute-start.22 = (f32[256,256]{1,0:T(8,128)S(1)}, f32[256,256]{1,0:T(8,128)S(1)}, u32[]{:S(2)}, u32[]{:S(2)}) collective-permute-start(f32[256,256]{1,0:T(8,128)S(1)} %add.314), channel_id=1, source_target_pairs={{0,1},{1,0},{2,3},{3,2},{4,5},{5,4},{6,7},{7,6},{8,9},{9,8},{10,11... | collective-permute-start | bytes 786440 | tf_op jit(solution)/shard_map/ppermute | solution.py:48
  515.8 11.7 %cholesky.625 = f32[128,128]{1,0:T(8,128)S(1)} custom-call(f32[128,128]{1,0:T(8,128)S(1)} %cholesky.683), custom_call_target="Cholesky" | custom-call | tf_op jit(solution)/shard_map/jit(cholesky)/cholesky | solution.py:100
  527.5 9.8 %custom-call.76 = f32[1,128,128]{1,2,0:T(8,128)S(1)} custom-call(f32[1,128,128]{2,1,0:T(8,128)S(1)} %get-tuple-element.38), custom_call_target="InvertDiagBlocksLowerTriangular" | custom-call | tf_op jit(solution)/shard_map/jit(cholesky)/cholesky/custom-call.17 | solution.py:100
  537.8 11.7 %cholesky.634 = f32[128,128]{1,0:T(8,128)S(1)} custom-call(f32[128,128]{1,0:T(8,128)S(1)} %slice_subtract_fusion.6), custom_call_target="Cholesky" | custom-call | tf_op jit(solution)/shard_map/jit(cholesky)/cholesky | solution.py:100
  556.8 19.7 %custom-call.73 = f32[2,128,128]{1,2,0:T(8,128)S(1)} custom-call(f32[2,128,128]{2,1,0:T(8,128)S(1)} %get-tuple-element.10), custom_call_target="InvertDiagBlocksLowerTriangular" | custom-call | tf_op jit(solution)/shard_map/jit(_solve_triangular)/triangular_solve | solution.py:101
  (169 shorter events, 152.5 us)
Async XLA Ops:
  0.6 1.6 copy-start
  10.2 110.2 %all-to-all-start = ((bf16[128,16,1024]{2,1,0:T(8,128)(2,1)}), bf16[128,16,1024]{2,1,0:T(8,128)(2,1)}, u32[]{:S(2)}, u32[]{:S(2)}) async-start(bf16[128,16,1024]{2,1,0:T(8,128)(2,1)} %bitcast.113), calls=%async_computation | async-start | bytes 8388608 | tf_op jit(solution)/shard_map/all_to_all | solution.py:80
  120.4 10.7 %collective-permute-start = (bf16[2048,1024]{1,0:T(8,128)(2,1)}, bf16[2048,1024]{1,0:T(8,128)(2,1)S(1)}, u32[]{:S(2)}, u32[]{:S(2)}) collective-permute-start(bf16[2048,1024]{1,0:T(8,128)(2,1)} %bitcast.4), channel_id=1, source_target_pairs={{0,1},{1,0},{2,3},{3,2},{4,5},{5,4},{6,7},{7,6},{8,9},{9,8},{10,11... | collective-permute-start | bytes 12582920 | tf_op jit(solution)/shard_map/ppermute | solution.py:83
  141.7 1.9 copy-start.3
  347.1 2.8 copy-start.7
  349.8 7.2 %copy-start.2 = (f32[1024,1024]{1,0:T(8,128)}, f32[1024,1024]{1,0:T(8,128)S(1)}, u32[]{:S(2)}) copy-start(f32[1024,1024]{1,0:T(8,128)S(1)} %select_select_fusion) | copy-start | bytes 12582916
  363.4 1.8 copy-start.4
  364.5 22.2 %collective-permute-start.1 = (f32[64,28,128]{2,0,1:T(8,128)}, f32[64,28,128]{2,0,1:T(8,128)}, u32[]{:S(2)}, u32[]{:S(2)}) collective-permute-start(f32[64,28,128]{2,0,1:T(8,128)} %get-tuple-element.31), channel_id=1, source_target_pairs={{0,2},{2,0},{4,6},{6,4},{8,10},{10,8},{12,14},{14,12},{16,18},{18,... | collective-permute-start | bytes 2752520 | tf_op jit(solution)/shard_map/ppermute | solution.py:39
  371.3 22.1 %collective-permute-start.8 = (f32[64,28,128]{2,0,1:T(8,128)}, f32[64,28,128]{2,0,1:T(8,128)S(1)}, u32[]{:S(2)}, u32[]{:S(2)}) collective-permute-start(f32[64,28,128]{2,0,1:T(8,128)} %get-tuple-element.33), channel_id=1, source_target_pairs={{0,8},{2,10},{4,12},{6,14},{8,0},{10,2},{12,4},{14,6},{16,24},{18,... | collective-permute-start | bytes 2752520 | tf_op jit(solution)/shard_map/ppermute | solution.py:39
  372.1 22.2 %copy-start.5 = (f32[64,28,128]{2,0,1:T(8,128)S(1)}, f32[64,28,128]{2,0,1:T(8,128)}, u32[]{:S(2)}) copy-start(f32[64,28,128]{2,0,1:T(8,128)} %get-tuple-element.34) | copy-start | bytes 2752516
  389.8 14.9 %collective-permute-start.2 = (f32[32,28,128]{2,1,0:T(8,128)}, f32[32,28,128]{2,1,0:T(8,128)S(1)}, u32[]{:S(2)}, u32[]{:S(2)}) collective-permute-start(f32[32,28,128]{2,1,0:T(8,128)} %constant_dynamic-slice_fusion.14), channel_id=1, source_target_pairs={{0,8},{2,10},{4,12},{6,14},{8,0},{10,2},{12,4},{14,6},{16,24},{18,... | collective-permute-start | bytes 1376264 | tf_op jit(solution)/shard_map/ppermute | solution.py:39
  393.4 0.9 copy-start.6
  397.4 12.3 %collective-permute-start.9 = (f32[32,28,128]{2,1,0:T(8,128)}, f32[32,28,128]{2,1,0:T(8,128)S(1)}, u32[]{:S(2)}, u32[]{:S(2)}) collective-permute-start(f32[32,28,128]{2,1,0:T(8,128)} %constant_dynamic-slice_fusion.6), channel_id=1, source_target_pairs={{0,32},{2,34},{4,36},{6,38},{8,40},{10,42},{12,44},{14,46},{16,48}... | collective-permute-start | bytes 1376264 | tf_op jit(solution)/shard_map/ppermute | solution.py:39
  404.8 10.6 %collective-permute-start.3 = (f32[16,28,128]{2,1,0:T(8,128)S(1)}, f32[16,28,128]{2,1,0:T(8,128)S(1)}, u32[]{:S(2)}, u32[]{:S(2)}) collective-permute-start(f32[16,28,128]{2,1,0:T(8,128)S(1)} %constant_dynamic-slice_fusion.13), channel_id=1, source_target_pairs={{0,32},{2,34},{4,36},{6,38},{8,40},{10,42},{12,44},{14,46},{16,48}... | collective-permute-start | bytes 688136 | tf_op jit(solution)/shard_map/ppermute | solution.py:39
  409.8 7.4 %collective-permute-start.10 = (f32[16,28,128]{2,1,0:T(8,128)S(1)}, f32[16,28,128]{2,1,0:T(8,128)S(1)}, u32[]{:S(2)}, u32[]{:S(2)}) collective-permute-start(f32[16,28,128]{2,1,0:T(8,128)S(1)} %constant_dynamic-slice_fusion.5), channel_id=1, source_target_pairs={{0,2},{2,0},{4,6},{6,4},{8,10},{10,8},{12,14},{14,12},{16,18},{18,... | collective-permute-start | bytes 688136 | tf_op jit(solution)/shard_map/ppermute | solution.py:39
  415.4 6.8 %collective-permute-start.4 = (f32[8,28,128]{2,1,0:T(8,128)S(1)}, f32[8,28,128]{2,1,0:T(8,128)S(1)}, u32[]{:S(2)}, u32[]{:S(2)}) collective-permute-start(f32[8,28,128]{2,1,0:T(8,128)S(1)} %constant_dynamic-slice_fusion.12), channel_id=1, source_target_pairs={{0,4},{2,6},{4,0},{6,2},{8,12},{10,14},{12,8},{14,10},{16,20},{18,... | collective-permute-start | bytes 344072 | tf_op jit(solution)/shard_map/ppermute | solution.py:39
  417.3 6.5 %collective-permute-start.11 = (f32[8,28,128]{2,1,0:T(8,128)S(1)}, f32[8,28,128]{2,1,0:T(8,128)S(1)}, u32[]{:S(2)}, u32[]{:S(2)}) collective-permute-start(f32[8,28,128]{2,1,0:T(8,128)S(1)} %constant_dynamic-slice_fusion.4), channel_id=1, source_target_pairs={{0,16},{2,18},{4,20},{6,22},{8,24},{10,26},{12,28},{14,30},{16,0},... | collective-permute-start | bytes 344072 | tf_op jit(solution)/shard_map/ppermute | solution.py:39
  422.2 5.4 collective-permute-start.5
  423.9 5.1 collective-permute-start.12
  427.7 4.7 collective-permute-start.6
  429.0 4.6 collective-permute-start.13
  432.3 6.6 %collective-permute-start.7 = (f32[1,28,128]{2,1,0:T(8,128)S(1)}, f32[1,28,128]{2,1,0:T(8,128)S(1)}, u32[]{:S(2)}, u32[]{:S(2)}) collective-permute-start(f32[1,28,128]{2,1,0:T(8,128)S(1)} %constant_dynamic-slice_fusion.9), channel_id=1, source_target_pairs={{0,128},{2,130},{4,132},{6,134},{8,136},{10,138},{12,140},{14,142}... | collective-permute-start | bytes 43016 | tf_op jit(solution)/shard_map/ppermute | solution.py:39
  433.6 6.6 %collective-permute-start.14 = (f32[1,28,128]{2,1,0:T(8,128)S(1)}, f32[1,28,128]{2,1,0:T(8,128)S(1)}, u32[]{:S(2)}, u32[]{:S(2)}) collective-permute-start(f32[1,28,128]{2,1,0:T(8,128)S(1)} %constant_dynamic-slice_fusion.1), channel_id=1, source_target_pairs={{0,128},{2,130},{4,132},{6,134},{8,136},{10,138},{12,140},{14,142}... | collective-permute-start | bytes 43016 | tf_op jit(solution)/shard_map/ppermute | solution.py:39
  440.6 5.6 collective-permute-start.15
  446.3 5.6 collective-permute-start.16
  451.9 5.6 collective-permute-start.17
  457.5 6.8 %collective-permute-start.18 = (f32[256,256]{1,0:T(8,128)S(1)}, f32[256,256]{1,0:T(8,128)S(1)}, u32[]{:S(2)}, u32[]{:S(2)}) collective-permute-start(f32[256,256]{1,0:T(8,128)S(1)} %add.310), channel_id=1, source_target_pairs={{0,4},{2,6},{4,0},{6,2},{8,12},{10,14},{12,8},{14,10},{16,20},{18,... | collective-permute-start | bytes 786440 | tf_op jit(solution)/shard_map/ppermute | solution.py:47
  464.4 6.8 %collective-permute-start.19 = (f32[256,256]{1,0:T(8,128)S(1)}, f32[256,256]{1,0:T(8,128)S(1)}, u32[]{:S(2)}, u32[]{:S(2)}) collective-permute-start(f32[256,256]{1,0:T(8,128)S(1)} %add.311), channel_id=1, source_target_pairs={{0,16},{2,18},{4,20},{6,22},{8,24},{10,26},{12,28},{14,30},{16,0},... | collective-permute-start | bytes 786440 | tf_op jit(solution)/shard_map/ppermute | solution.py:47
  471.2 10.3 %collective-permute-start.20 = (f32[256,256]{1,0:T(8,128)S(1)}, f32[256,256]{1,0:T(8,128)S(1)}, u32[]{:S(2)}, u32[]{:S(2)}) collective-permute-start(f32[256,256]{1,0:T(8,128)S(1)} %add.312), channel_id=1, source_target_pairs={{0,64},{2,66},{4,68},{6,70},{8,72},{10,74},{12,76},{14,78},{16,80}... | collective-permute-start | bytes 786440 | tf_op jit(solution)/shard_map/ppermute | solution.py:47
  481.5 14.7 %collective-permute-start.21 = (f32[256,256]{1,0:T(8,128)S(1)}, f32[256,256]{1,0:T(8,128)S(1)}, u32[]{:S(2)}, u32[]{:S(2)}) collective-permute-start(f32[256,256]{1,0:T(8,128)S(1)} %add.313), channel_id=1, source_target_pairs={{0,128},{2,130},{4,132},{6,134},{8,136},{10,138},{12,140},{14,142}... | collective-permute-start | bytes 786440 | tf_op jit(solution)/shard_map/ppermute | solution.py:47
  496.2 81.4 %copy-start.1 = (bf16[128,8,1024]{2,1,0:T(8,128)(2,1)S(1)}, bf16[128,8,1024]{2,1,0:T(8,128)(2,1)}, u32[]{:S(2)}) copy-start(bf16[128,8,1024]{2,1,0:T(8,128)(2,1)} %param.7) | copy-start | bytes 6291460
  496.3 19.4 %collective-permute-start.22 = (f32[256,256]{1,0:T(8,128)S(1)}, f32[256,256]{1,0:T(8,128)S(1)}, u32[]{:S(2)}, u32[]{:S(2)}) collective-permute-start(f32[256,256]{1,0:T(8,128)S(1)} %add.314), channel_id=1, source_target_pairs={{0,1},{1,0},{2,3},{3,2},{4,5},{5,4},{6,7},{7,6},{8,9},{9,8},{10,11... | collective-permute-start | bytes 786440 | tf_op jit(solution)/shard_map/ppermute | solution.py:48

commit v5 on v4

--- a/solution.py
+++ b/solution.py
@@ -64,6 +64,23 @@
     return orders
 
 
+def hdot(left, right):
+    return jnp.dot(left, right, precision=lax.Precision.HIGHEST)
+
+
+def right_solve_chol(gram, rows):
+    h = gram.shape[0] // 2
+    eye = jnp.eye(h, dtype=gram.dtype)
+    l11 = jnp.linalg.cholesky(gram[:h, :h], symmetrize_input=False)
+    i11 = jax.scipy.linalg.solve_triangular(l11, eye, lower=True)
+    l21 = hdot(gram[h:, :h], i11.T)
+    l22 = jnp.linalg.cholesky(gram[h:, h:] - hdot(l21, l21.T), symmetrize_input=False)
+    i22 = jax.scipy.linalg.solve_triangular(l22, eye, lower=True)
+    x1 = hdot(rows[:, :h], i11.T)
+    x2 = hdot(rows[:, h:] - hdot(x1, l21.T), i22.T)
+    return jnp.concatenate([x1, x2], axis=1)
+
+
 def local(hidden, routes, slots, down_weight, omega):
     n_exp = lax.axis_size("expert")
     n_dp = lax.axis_size("dp")
@@ -97,10 +114,7 @@
     orders = bit_orders(n_exp, 2)
     sketch = scatter_sum(term, orders)
     small_gram = all_sum(jnp.dot(sketch.T, sketch, precision=lax.Precision.HIGHEST), orders[0])
-    qr_factor = jnp.linalg.cholesky(small_gram, symmetrize_input=False)
-    basis_rows = jax.scipy.linalg.solve_triangular(qr_factor, sketch.T, lower=True).T * math.sqrt(
-        half_cols * n_dp
-    )
+    basis_rows = right_solve_chol(small_gram, sketch) * math.sqrt(half_cols * n_dp)
     own_rows = lax.dynamic_slice_in_dim(
         whitening, lax.axis_index("dp") * (hid_width // n_dp), hid_width // n_dp, 0
     )

time: 587 us -> 572 us (0.974)
  other arithmetic: 238 us -> 229 us
    another operation x10, other arithmetic: 54.4 us -> 45.7 us  [the longest x3 12.4 us: right_solve_chol(): jnp.linalg.cholesky(gram[h:, h:] - hdot(l21, l21.T), symmetrize_input=False)]
where the time goes in v5:
time: 572 us; the launch traced here: 564 us
  other arithmetic  229 us (40%)
  waiting for transfers between devices  178 us (31%)
  starting transfers between devices  68.5 us (12%)
  matrix products  47.6 us (8%)
  local copies, waits for them, and re-layouts  33.5 us (6%)
  between operations  7.17 us (1%)
    another operation x30, other arithmetic, local(): whitening = jnp.linalg.cholesky(damped, symmetrize_input=False)  172 us
    all_to_all x1, waiting for transfers between devices, local(): lax.all_to_all(outgoing, 'expert', split_axis=0, concat_axis=0, tiled=True)  93.3 us
    ppermute x14, waiting for transfers between devices, scatter_sum(): part = keep + lax.ppermute(send, 'expert', xor_pairs(n_exp, 1 << b))  42.7 us
    ppermute x7, waiting for transfers between devices, all_sum(): x = x + lax.ppermute(x, 'expert', xor_pairs(n_exp, 1 << b))  41.9 us
    another operation x14, matrix products, local(): whitening = jnp.linalg.cholesky(damped, symmetrize_input=False)  23.3 us
    dot_general x3, matrix products, contract(): lax.dot_general(left, right, (((0,), (0,)), ((), ())), preferred_element_...  20.1 us
    ppermute x14, starting transfers between devices, scatter_sum(): part = keep + lax.ppermute(send, 'expert', xor_pairs(n_exp, 1 << b))  19 us
    all_to_all x1, starting transfers between devices, local(): lax.all_to_all(outgoing, 'expert', split_axis=0, concat_axis=0, tiled=True)  16.9 us
  transfers between devices with their start and end apart: 24, of which 18 were waited for; matrix products, arithmetic and copies ran while one was open for 4% of the time, Pallas kernels for 0%

profile of v5, /device:TPU:1, one launch (start us, length us, event | category | flops | bytes accessed | tf_op | source)
XLA Modules:
  0.0 563.9 jit_solution(10790517261854774133)
XLA Ops:
  2.3 7.9 %scatter_custom_fusion = bf16[2048,1024]{1,0:T(8,128)(2,1)} fusion(s32[1024]{0:T(1024)S(1)} %bitcast.102, bf16[128,8,1024]{2,1,0:T(8,128)(2,1)S(1)} %copy-done, bf16[]{:T(256)} %constant.316.clone.1), kind=kCustom, calls=%fused_computation.10 | custom fusion | bytes 6291458 | tf_op jit(solution)/shard_map/scatter | solution.py:94
  10.2 16.9 %all-to-all-start = ((bf16[128,16,1024]{2,1,0:T(8,128)(2,1)}), bf16[128,16,1024]{2,1,0:T(8,128)(2,1)}, u32[]{:S(2)}, u32[]{:S(2)}) async-start(bf16[128,16,1024]{2,1,0:T(8,128)(2,1)} %bitcast.96), calls=%async_computation | async-start | bytes 8388608 | tf_op jit(solution)/shard_map/all_to_all | solution.py:97
  27.1 93.3 %all-to-all-done = bf16[128,16,1024]{2,1,0:T(8,128)(2,1)} async-done(((bf16[128,16,1024]{2,1,0:T(8,128)(2,1)}), bf16[128,16,1024]{2,1,0:T(8,128)(2,1)}, u32[]{:S(2)}, u32[]{:S(2)}) %all-to-all-start) | async-done | bytes 4194336 | tf_op jit(solution)/shard_map/all_to_all | solution.py:97
  123.5 7.6 %fusion.67 = f32[1024,1024,1]{1,0,2:T(8,128)S(1)} fusion(bf16[128,16,1024]{2,1,0:T(8,128)(2,1)} %all-to-all-done), kind=kOutput, calls=%fused_computation.154 | convolution fusion | flops 4294967296 | bytes 8388608 | tf_op jit(solution)/shard_map/dot_general | solution.py:13
  131.1 7.4 %select_reduce_fusion = (f32[]{:T(128)}, f32[1024,1024]{1,0:T(8,128)}) fusion(bf16[2048,1024]{1,0:T(8,128)(2,1)S(1)} %collective-permute-done, f32[1024,1024,1]{1,0,2:T(8,128)S(1)} %fusion.67), kind=kOutput, calls=%fused_computation.7 | convolution fusion | flops 4300210176 | bytes 12582916 | tf_op jit(solution)/shard_map/dot_general | solution.py:13
  143.7 11.7 %cholesky.242 = f32[128,128]{1,0:T(8,128)S(1)} custom-call(f32[128,128]{1,0:T(8,128)S(1)} %cholesky.654), custom_call_target="Cholesky" | custom-call | tf_op jit(solution)/shard_map/jit(cholesky)/cholesky | solution.py:107
  155.4 9.8 %custom-call.64 = f32[1,128,128]{1,2,0:T(8,128)S(1)} custom-call(f32[1,128,128]{2,1,0:T(8,128)S(1)} %get-tuple-element.39), custom_call_target="InvertDiagBlocksLowerTriangular" | custom-call | tf_op jit(solution)/shard_map/jit(cholesky)/cholesky | solution.py:107
  171.7 11.7 %cholesky.265 = f32[128,128]{1,0:T(8,128)S(1)} custom-call(f32[128,128]{1,0:T(8,128)S(1)} %cholesky.658), custom_call_target="Cholesky" | custom-call | tf_op jit(solution)/shard_map/jit(cholesky)/cholesky | solution.py:107
  184.0 10.2 %custom-call.65 = f32[1,128,128]{1,2,0:T(8,128)S(1)} custom-call(f32[1,128,128]{2,1,0:T(8,128)S(1)} %get-tuple-element.36), custom_call_target="InvertDiagBlocksLowerTriangular" | custom-call | tf_op jit(solution)/shard_map/jit(cholesky)/cholesky | solution.py:107
  197.6 11.7 %cholesky.506 = f32[128,128]{1,0:T(8,128)S(1)} custom-call(f32[128,128]{1,0:T(8,128)S(1)} %cholesky.663), custom_call_target="Cholesky" | custom-call | tf_op jit(solution)/shard_map/jit(cholesky)/cholesky | solution.py:107
  210.5 9.8 %custom-call.66 = f32[1,128,128]{1,2,0:T(8,128)S(1)} custom-call(f32[1,128,128]{2,1,0:T(8,128)S(1)} %get-tuple-element.33), custom_call_target="InvertDiagBlocksLowerTriangular" | custom-call | tf_op jit(solution)/shard_map/jit(cholesky)/cholesky | solution.py:107
  223.9 11.9 %cholesky.525 = f32[128,128]{1,0:T(8,128)S(1)} custom-call(f32[128,128]{1,0:T(8,128)S(1)} %cholesky.668), custom_call_target="Cholesky" | custom-call | tf_op jit(solution)/shard_map/jit(cholesky)/cholesky | solution.py:107
  237.0 9.8 %custom-call.67 = f32[1,128,128]{1,2,0:T(8,128)S(1)} custom-call(f32[1,128,128]{2,1,0:T(8,128)S(1)} %get-tuple-element.30), custom_call_target="InvertDiagBlocksLowerTriangular" | custom-call | tf_op jit(solution)/shard_map/jit(cholesky)/cholesky | solution.py:107
  250.3 11.7 %cholesky.544 = f32[128,128]{1,0:T(8,128)S(1)} custom-call(f32[128,128]{1,0:T(8,128)S(1)} %cholesky.673), custom_call_target="Cholesky" | custom-call | tf_op jit(solution)/shard_map/jit(cholesky)/cholesky | solution.py:107
  263.3 9.8 %custom-call.68 = f32[1,128,128]{1,2,0:T(8,128)S(1)} custom-call(f32[1,128,128]{2,1,0:T(8,128)S(1)} %get-tuple-element.27), custom_call_target="InvertDiagBlocksLowerTriangular" | custom-call | tf_op jit(solution)/shard_map/jit(cholesky)/cholesky | solution.py:107
  276.6 11.7 %cholesky.564 = f32[128,128]{1,0:T(8,128)S(1)} custom-call(f32[128,128]{1,0:T(8,128)S(1)} %cholesky.678), custom_call_target="Cholesky" | custom-call | tf_op jit(solution)/shard_map/jit(cholesky)/cholesky | solution.py:107
  289.6 9.8 %custom-call.69 = f32[1,128,128]{1,2,0:T(8,128)S(1)} custom-call(f32[1,128,128]{2,1,0:T(8,128)S(1)} %get-tuple-element.24), custom_call_target="InvertDiagBlocksLowerTriangular" | custom-call | tf_op jit(solution)/shard_map/jit(cholesky)/cholesky | solution.py:107
  302.4 11.7 %cholesky.584 = f32[128,128]{1,0:T(8,128)S(1)} custom-call(f32[128,128]{1,0:T(8,128)S(1)} %cholesky.683), custom_call_target="Cholesky" | custom-call | tf_op jit(solution)/shard_map/jit(cholesky)/cholesky | solution.py:107
  315.4 10.2 %custom-call.70 = f32[1,128,128]{1,2,0:T(8,128)S(1)} custom-call(f32[1,128,128]{2,1,0:T(8,128)S(1)} %get-tuple-element.21), custom_call_target="InvertDiagBlocksLowerTriangular" | custom-call | tf_op jit(solution)/shard_map/jit(cholesky)/cholesky | solution.py:107
  328.2 11.7 %cholesky.602 = f32[128,128]{1,0:T(8,128)S(1)} custom-call(f32[128,128]{1,0:T(8,128)S(1)} %slice_subtract_fusion.7), custom_call_target="Cholesky" | custom-call | tf_op jit(solution)/shard_map/jit(cholesky)/cholesky | solution.py:107
  351.6 5.2 fusion
  371.9 14.7 %collective-permute-done.1 = f32[64,28,128]{2,0,1:T(8,128)} collective-permute-done((f32[64,28,128]{2,0,1:T(8,128)}, f32[64,28,128]{2,0,1:T(8,128)}, u32[]{:S(2)}, u32[]{:S(2)}) %collective-permute-start.1) | collective-permute-done | bytes 917536 | tf_op jit(solution)/shard_map/ppermute | solution.py:39
  398.2 6.2 %collective-permute-done.2 = f32[32,28,128]{2,1,0:T(8,128)S(1)} collective-permute-done((f32[32,28,128]{2,1,0:T(8,128)}, f32[32,28,128]{2,1,0:T(8,128)S(1)}, u32[]{:S(2)}, u32[]{:S(2)}) %collective-permute-start.2) | collective-permute-done | bytes 458784 | tf_op jit(solution)/shard_map/ppermute | solution.py:39
  409.7 5.4 collective-permute-done.3
  458.3 5.9 %collective-permute-done.18 = f32[256,256]{1,0:T(8,128)S(1)} collective-permute-done((f32[256,256]{1,0:T(8,128)S(1)}, f32[256,256]{1,0:T(8,128)S(1)}, u32[]{:S(2)}, u32[]{:S(2)}) %collective-permute-start.18) | collective-permute-done | bytes 262176 | tf_op jit(solution)/shard_map/ppermute | solution.py:47
  474.4 6.9 %collective-permute-done.20 = f32[256,256]{1,0:T(8,128)S(1)} collective-permute-done((f32[256,256]{1,0:T(8,128)S(1)}, f32[256,256]{1,0:T(8,128)S(1)}, u32[]{:S(2)}, u32[]{:S(2)}) %collective-permute-start.20) | collective-permute-done | bytes 262176 | tf_op jit(solution)/shard_map/ppermute | solution.py:47
  484.7 11.4 %collective-permute-done.21 = f32[256,256]{1,0:T(8,128)S(1)} collective-permute-done((f32[256,256]{1,0:T(8,128)S(1)}, f32[256,256]{1,0:T(8,128)S(1)}, u32[]{:S(2)}, u32[]{:S(2)}) %collective-permute-start.21) | collective-permute-done | bytes 262176 | tf_op jit(solution)/shard_map/ppermute | solution.py:47
  496.1 16.0 %collective-permute-start.22 = (f32[256,256]{1,0:T(8,128)S(1)}, f32[256,256]{1,0:T(8,128)S(1)}, u32[]{:S(2)}, u32[]{:S(2)}) collective-permute-start(f32[256,256]{1,0:T(8,128)S(1)} %add.308), channel_id=1, source_target_pairs={{0,1},{1,0},{2,3},{3,2},{4,5},{5,4},{6,7},{7,6},{8,9},{9,8},{10,11... | collective-permute-start | bytes 786440 | tf_op jit(solution)/shard_map/ppermute | solution.py:48
  515.3 11.7 %cholesky.634 = f32[128,128]{1,0:T(8,128)S(1)} custom-call(f32[128,128]{1,0:T(8,128)S(1)} %slice.207), custom_call_target="Cholesky" | custom-call | tf_op jit(solution)/shard_map/jit(cholesky)/cholesky | solution.py:74
  528.3 9.8 %custom-call.72 = f32[1,128,128]{1,2,0:T(8,128)S(1)} custom-call(f32[1,128,128]{2,1,0:T(8,128)S(1)} %fusion.43), custom_call_target="InvertDiagBlocksLowerTriangular" | custom-call | tf_op jit(solution)/shard_map/jit(_solve_triangular)/triangular_solve | solution.py:75
  539.2 11.7 %cholesky.645 = f32[128,128]{1,0:T(8,128)S(1)} custom-call(f32[128,128]{1,0:T(8,128)S(1)} %slice_subtract_fusion.6), custom_call_target="Cholesky" | custom-call | tf_op jit(solution)/shard_map/jit(cholesky)/cholesky | solution.py:77
  552.3 9.8 %custom-call.73 = f32[1,128,128]{1,2,0:T(8,128)S(1)} custom-call(f32[1,128,128]{2,1,0:T(8,128)S(1)} %fusion.44), custom_call_target="InvertDiagBlocksLowerTriangular" | custom-call | tf_op jit(solution)/shard_map/jit(_solve_triangular)/triangular_solve | solution.py:78
  (160 shorter events, 145.8 us)
Async XLA Ops:
  0.6 1.6 copy-start
  10.2 110.2 %all-to-all-start = ((bf16[128,16,1024]{2,1,0:T(8,128)(2,1)}), bf16[128,16,1024]{2,1,0:T(8,128)(2,1)}, u32[]{:S(2)}, u32[]{:S(2)}) async-start(bf16[128,16,1024]{2,1,0:T(8,128)(2,1)} %bitcast.96), calls=%async_computation | async-start | bytes 8388608 | tf_op jit(solution)/shard_map/all_to_all | solution.py:97
  120.4 10.7 %collective-permute-start = (bf16[2048,1024]{1,0:T(8,128)(2,1)}, bf16[2048,1024]{1,0:T(8,128)(2,1)S(1)}, u32[]{:S(2)}, u32[]{:S(2)}) collective-permute-start(bf16[2048,1024]{1,0:T(8,128)(2,1)} %bitcast.4), channel_id=1, source_target_pairs={{0,1},{1,0},{2,3},{3,2},{4,5},{5,4},{6,7},{7,6},{8,9},{9,8},{10,11... | collective-permute-start | bytes 12582920 | tf_op jit(solution)/shard_map/ppermute | solution.py:100
  141.7 1.9 copy-start.3
  346.8 2.8 copy-start.7
  349.6 7.2 %copy-start.2 = (f32[1024,1024]{1,0:T(8,128)}, f32[1024,1024]{1,0:T(8,128)S(1)}, u32[]{:S(2)}) copy-start(f32[1024,1024]{1,0:T(8,128)S(1)} %select_select_fusion) | copy-start | bytes 12582916
  363.2 1.8 copy-start.4
  364.3 22.2 %collective-permute-start.1 = (f32[64,28,128]{2,0,1:T(8,128)}, f32[64,28,128]{2,0,1:T(8,128)}, u32[]{:S(2)}, u32[]{:S(2)}) collective-permute-start(f32[64,28,128]{2,0,1:T(8,128)} %get-tuple-element.14), channel_id=1, source_target_pairs={{0,2},{2,0},{4,6},{6,4},{8,10},{10,8},{12,14},{14,12},{16,18},{18,... | collective-permute-start | bytes 2752520 | tf_op jit(solution)/shard_map/ppermute | solution.py:39
  371.1 22.1 %collective-permute-start.8 = (f32[64,28,128]{2,0,1:T(8,128)}, f32[64,28,128]{2,0,1:T(8,128)S(1)}, u32[]{:S(2)}, u32[]{:S(2)}) collective-permute-start(f32[64,28,128]{2,0,1:T(8,128)} %get-tuple-element.16), channel_id=1, source_target_pairs={{0,8},{2,10},{4,12},{6,14},{8,0},{10,2},{12,4},{14,6},{16,24},{18,... | collective-permute-start | bytes 2752520 | tf_op jit(solution)/shard_map/ppermute | solution.py:39
  371.9 22.2 %copy-start.5 = (f32[64,28,128]{2,0,1:T(8,128)S(1)}, f32[64,28,128]{2,0,1:T(8,128)}, u32[]{:S(2)}) copy-start(f32[64,28,128]{2,0,1:T(8,128)} %get-tuple-element.17) | copy-start | bytes 2752516
  389.5 14.9 %collective-permute-start.2 = (f32[32,28,128]{2,1,0:T(8,128)}, f32[32,28,128]{2,1,0:T(8,128)S(1)}, u32[]{:S(2)}, u32[]{:S(2)}) collective-permute-start(f32[32,28,128]{2,1,0:T(8,128)} %constant_dynamic-slice_fusion.13), channel_id=1, source_target_pairs={{0,8},{2,10},{4,12},{6,14},{8,0},{10,2},{12,4},{14,6},{16,24},{18,... | collective-permute-start | bytes 1376264 | tf_op jit(solution)/shard_map/ppermute | solution.py:39
  393.2 0.9 copy-start.6
  397.1 12.3 %collective-permute-start.9 = (f32[32,28,128]{2,1,0:T(8,128)}, f32[32,28,128]{2,1,0:T(8,128)S(1)}, u32[]{:S(2)}, u32[]{:S(2)}) collective-permute-start(f32[32,28,128]{2,1,0:T(8,128)} %constant_dynamic-slice_fusion.5), channel_id=1, source_target_pairs={{0,32},{2,34},{4,36},{6,38},{8,40},{10,42},{12,44},{14,46},{16,48}... | collective-permute-start | bytes 1376264 | tf_op jit(solution)/shard_map/ppermute | solution.py:39
  404.5 10.6 %collective-permute-start.3 = (f32[16,28,128]{2,1,0:T(8,128)S(1)}, f32[16,28,128]{2,1,0:T(8,128)S(1)}, u32[]{:S(2)}, u32[]{:S(2)}) collective-permute-start(f32[16,28,128]{2,1,0:T(8,128)S(1)} %constant_dynamic-slice_fusion.12), channel_id=1, source_target_pairs={{0,32},{2,34},{4,36},{6,38},{8,40},{10,42},{12,44},{14,46},{16,48}... | collective-permute-start | bytes 688136 | tf_op jit(solution)/shard_map/ppermute | solution.py:39
  409.6 7.4 %collective-permute-start.10 = (f32[16,28,128]{2,1,0:T(8,128)S(1)}, f32[16,28,128]{2,1,0:T(8,128)S(1)}, u32[]{:S(2)}, u32[]{:S(2)}) collective-permute-start(f32[16,28,128]{2,1,0:T(8,128)S(1)} %constant_dynamic-slice_fusion.4), channel_id=1, source_target_pairs={{0,2},{2,0},{4,6},{6,4},{8,10},{10,8},{12,14},{14,12},{16,18},{18,... | collective-permute-start | bytes 688136 | tf_op jit(solution)/shard_map/ppermute | solution.py:39
  415.2 6.8 %collective-permute-start.4 = (f32[8,28,128]{2,1,0:T(8,128)S(1)}, f32[8,28,128]{2,1,0:T(8,128)S(1)}, u32[]{:S(2)}, u32[]{:S(2)}) collective-permute-start(f32[8,28,128]{2,1,0:T(8,128)S(1)} %constant_dynamic-slice_fusion.11), channel_id=1, source_target_pairs={{0,4},{2,6},{4,0},{6,2},{8,12},{10,14},{12,8},{14,10},{16,20},{18,... | collective-permute-start | bytes 344072 | tf_op jit(solution)/shard_map/ppermute | solution.py:39
  417.1 6.5 %collective-permute-start.11 = (f32[8,28,128]{2,1,0:T(8,128)S(1)}, f32[8,28,128]{2,1,0:T(8,128)S(1)}, u32[]{:S(2)}, u32[]{:S(2)}) collective-permute-start(f32[8,28,128]{2,1,0:T(8,128)S(1)} %constant_dynamic-slice_fusion.3), channel_id=1, source_target_pairs={{0,16},{2,18},{4,20},{6,22},{8,24},{10,26},{12,28},{14,30},{16,0},... | collective-permute-start | bytes 344072 | tf_op jit(solution)/shard_map/ppermute | solution.py:39
  422.0 5.4 collective-permute-start.5
  423.6 5.1 collective-permute-start.12
  427.4 4.7 collective-permute-start.6
  428.8 4.6 collective-permute-start.13
  432.1 6.6 %collective-permute-start.7 = (f32[1,28,128]{2,1,0:T(8,128)S(1)}, f32[1,28,128]{2,1,0:T(8,128)S(1)}, u32[]{:S(2)}, u32[]{:S(2)}) collective-permute-start(f32[1,28,128]{2,1,0:T(8,128)S(1)} %constant_dynamic-slice_fusion.8), channel_id=1, source_target_pairs={{0,128},{2,130},{4,132},{6,134},{8,136},{10,138},{12,140},{14,142}... | collective-permute-start | bytes 43016 | tf_op jit(solution)/shard_map/ppermute | solution.py:39
  433.4 6.6 %collective-permute-start.14 = (f32[1,28,128]{2,1,0:T(8,128)S(1)}, f32[1,28,128]{2,1,0:T(8,128)S(1)}, u32[]{:S(2)}, u32[]{:S(2)}) collective-permute-start(f32[1,28,128]{2,1,0:T(8,128)S(1)} %constant_dynamic-slice_fusion), channel_id=1, source_target_pairs={{0,128},{2,130},{4,132},{6,134},{8,136},{10,138},{12,140},{14,142}... | collective-permute-start | bytes 43016 | tf_op jit(solution)/shard_map/ppermute | solution.py:39
  440.4 5.6 collective-permute-start.15
  446.0 5.6 collective-permute-start.16
  451.7 5.6 collective-permute-start.17
  457.3 6.8 %collective-permute-start.18 = (f32[256,256]{1,0:T(8,128)S(1)}, f32[256,256]{1,0:T(8,128)S(1)}, u32[]{:S(2)}, u32[]{:S(2)}) collective-permute-start(f32[256,256]{1,0:T(8,128)S(1)} %add.304), channel_id=1, source_target_pairs={{0,4},{2,6},{4,0},{6,2},{8,12},{10,14},{12,8},{14,10},{16,20},{18,... | collective-permute-start | bytes 786440 | tf_op jit(solution)/shard_map/ppermute | solution.py:47
  464.2 6.8 %collective-permute-start.19 = (f32[256,256]{1,0:T(8,128)S(1)}, f32[256,256]{1,0:T(8,128)S(1)}, u32[]{:S(2)}, u32[]{:S(2)}) collective-permute-start(f32[256,256]{1,0:T(8,128)S(1)} %add.305), channel_id=1, source_target_pairs={{0,16},{2,18},{4,20},{6,22},{8,24},{10,26},{12,28},{14,30},{16,0},... | collective-permute-start | bytes 786440 | tf_op jit(solution)/shard_map/ppermute | solution.py:47
  471.0 92.5 %copy-start.1 = (bf16[128,8,1024]{2,1,0:T(8,128)(2,1)S(1)}, bf16[128,8,1024]{2,1,0:T(8,128)(2,1)}, u32[]{:S(2)}) copy-start(bf16[128,8,1024]{2,1,0:T(8,128)(2,1)} %param.8) | copy-start | bytes 6291460
  471.0 10.3 %collective-permute-start.20 = (f32[256,256]{1,0:T(8,128)S(1)}, f32[256,256]{1,0:T(8,128)S(1)}, u32[]{:S(2)}, u32[]{:S(2)}) collective-permute-start(f32[256,256]{1,0:T(8,128)S(1)} %add.306), channel_id=1, source_target_pairs={{0,64},{2,66},{4,68},{6,70},{8,72},{10,74},{12,76},{14,78},{16,80}... | collective-permute-start | bytes 786440 | tf_op jit(solution)/shard_map/ppermute | solution.py:47
  481.3 14.7 %collective-permute-start.21 = (f32[256,256]{1,0:T(8,128)S(1)}, f32[256,256]{1,0:T(8,128)S(1)}, u32[]{:S(2)}, u32[]{:S(2)}) collective-permute-start(f32[256,256]{1,0:T(8,128)S(1)} %add.307), channel_id=1, source_target_pairs={{0,128},{2,130},{4,132},{6,134},{8,136},{10,138},{12,140},{14,142}... | collective-permute-start | bytes 786440 | tf_op jit(solution)/shard_map/ppermute | solution.py:47
  496.1 19.2 %collective-permute-start.22 = (f32[256,256]{1,0:T(8,128)S(1)}, f32[256,256]{1,0:T(8,128)S(1)}, u32[]{:S(2)}, u32[]{:S(2)}) collective-permute-start(f32[256,256]{1,0:T(8,128)S(1)} %add.308), channel_id=1, source_target_pairs={{0,1},{1,0},{2,3},{3,2},{4,5},{5,4},{6,7},{7,6},{8,9},{9,8},{10,11... | collective-permute-start | bytes 786440 | tf_op jit(solution)/shard_map/ppermute | solution.py:48

commit v6 on v5

--- a/solution.py
+++ b/solution.py
@@ -68,13 +68,19 @@
     return jnp.dot(left, right, precision=lax.Precision.HIGHEST)
 
 
-def right_solve_chol(gram, rows):
-    h = gram.shape[0] // 2
-    eye = jnp.eye(h, dtype=gram.dtype)
-    l11 = jnp.linalg.cholesky(gram[:h, :h], symmetrize_input=False)
+def lower_blocks(rows):
+    h = rows.shape[1] // 2
+    left, right = rows[:, :h], rows[:, h:]
+    return jnp.concatenate([hdot(left.T, left), hdot(right.T, left), hdot(right.T, right)], axis=0)
+
+
+def right_solve_chol(blocks, rows):
+    h = blocks.shape[1]
+    eye = jnp.eye(h, dtype=blocks.dtype)
+    l11 = jnp.linalg.cholesky(blocks[:h], symmetrize_input=False)
     i11 = jax.scipy.linalg.solve_triangular(l11, eye, lower=True)
-    l21 = hdot(gram[h:, :h], i11.T)
-    l22 = jnp.linalg.cholesky(gram[h:, h:] - hdot(l21, l21.T), symmetrize_input=False)
+    l21 = hdot(blocks[h:2 * h], i11.T)
+    l22 = jnp.linalg.cholesky(blocks[2 * h:] - hdot(l21, l21.T), symmetrize_input=False)
     i22 = jax.scipy.linalg.solve_triangular(l22, eye, lower=True)
     x1 = hdot(rows[:, :h], i11.T)
     x2 = hdot(rows[:, h:] - hdot(x1, l21.T), i22.T)
@@ -88,12 +94,11 @@
     capacity = 2 * tok_rows * n_route // n_exp
     n_slot = n_exp * n_dp * capacity
     slot_index = (routes * capacity + slots).reshape(-1)
-    outgoing = jnp.zeros((n_exp * capacity, hid_width), jnp.bfloat16)
-    outgoing = (
-        outgoing.at[slot_index]
-        .set(hidden.reshape(-1, hid_width))
-        .reshape(n_exp, capacity, hid_width)
-    )
+    one_hot = (
+        slot_index[:, None] == lax.broadcasted_iota(jnp.int32, (1, n_exp * capacity), 1)
+    ).astype(jnp.bfloat16)
+    outgoing = contract(one_hot, hidden.reshape(-1, hid_width)).astype(jnp.bfloat16)
+    outgoing = outgoing.reshape(n_exp, capacity, hid_width)
     received = lax.all_to_all(outgoing, "expert", split_axis=0, concat_axis=0, tiled=True).reshape(
         n_exp * capacity, hid_width
     )
@@ -113,7 +118,7 @@
     term = contract(test_mat, down_half)
     orders = bit_orders(n_exp, 2)
     sketch = scatter_sum(term, orders)
-    small_gram = all_sum(jnp.dot(sketch.T, sketch, precision=lax.Precision.HIGHEST), orders[0])
+    small_gram = all_sum(lower_blocks(sketch), orders[0])
     basis_rows = right_solve_chol(small_gram, sketch) * math.sqrt(half_cols * n_dp)
     own_rows = lax.dynamic_slice_in_dim(
         whitening, lax.axis_index("dp") * (hid_width // n_dp), hid_width // n_dp, 0

time: 572 us -> 557 us (0.974)
  waiting for transfers between devices: 178 us -> 167 us
  local copies, waits for them, and re-layouts: 33.5 us -> 24.1 us
  matrix products: 47.6 us -> 54.3 us
    scatter x1 -> x0, local copies, waits for them, and re-layouts: 7.93 us -> none  [local(): outgoing = outgoing.at[slot_index].set(hidden.reshape(-1, hid_width)).res...]
    dot_general x3 -> x4, matrix products: 20.1 us -> 26.4 us  [contract(): lax.dot_general(left, right, (((0,), (0,)), ((), ())), preferred_element_...]
    ppermute x7, waiting for transfers between devices: 41.9 us -> 35.9 us  [all_sum(): x = x + lax.ppermute(x, 'expert', xor_pairs(n_exp, 1 << b))]
where the time goes in v6:
time: 557 us; the launch traced here: 550 us
  other arithmetic  229 us (41%)
  waiting for transfers between devices  167 us (30%)
  starting transfers between devices  68.1 us (12%)
  matrix products  54.3 us (10%)
  local copies, waits for them, and re-layouts  24.1 us (4%)
  between operations  7.23 us (1%)
    another operation x30, other arithmetic, local(): whitening = jnp.linalg.cholesky(damped, symmetrize_input=False)  172 us
    all_to_all x1, waiting for transfers between devices, local(): lax.all_to_all(outgoing, 'expert', split_axis=0, concat_axis=0, tiled=True)  93.3 us
    ppermute x14, waiting for transfers between devices, scatter_sum(): part = keep + lax.ppermute(send, 'expert', xor_pairs(n_exp, 1 << b))  37.6 us
    ppermute x7, waiting for transfers between devices, all_sum(): x = x + lax.ppermute(x, 'expert', xor_pairs(n_exp, 1 << b))  35.9 us
    dot_general x4, matrix products, contract(): lax.dot_general(left, right, (((0,), (0,)), ((), ())), preferred_element_...  26.4 us
    ppermute x14, starting transfers between devices, scatter_sum(): part = keep + lax.ppermute(send, 'expert', xor_pairs(n_exp, 1 << b))  23.9 us
    another operation x14, matrix products, local(): whitening = jnp.linalg.cholesky(damped, symmetrize_input=False)  23.3 us
    all_to_all x1, starting transfers between devices, local(): lax.all_to_all(outgoing, 'expert', split_axis=0, concat_axis=0, tiled=True)  16.9 us
  transfers between devices with their start and end apart: 24, of which 18 were waited for; matrix products, arithmetic and copies ran while one was open for 4% of the time, Pallas kernels for 0%

profile of v6, /device:TPU:1, one launch (start us, length us, event | category | flops | bytes accessed | tf_op | source)
XLA Modules:
  0.0 549.8 jit_solution(5719525133471643235)
XLA Ops:
  2.3 6.3 %fusion.5 = bf16[2048,1024]{1,0:T(8,128)(2,1)} fusion(s32[1024]{0:T(1024)S(1)} %eq.22, bf16[128,8,1024]{2,1,0:T(8,128)(2,1)S(1)} %copy-done), kind=kOutput, calls=%fused_computation.12 | convolution fusion | flops 4299161600 | bytes 6295552 | tf_op jit(solution)/shard_map/dot_general | solution.py:13
  8.5 16.9 %all-to-all-start = ((bf16[128,16,1024]{2,1,0:T(8,128)(2,1)}), bf16[128,16,1024]{2,1,0:T(8,128)(2,1)}, u32[]{:S(2)}, u32[]{:S(2)}) async-start(bf16[128,16,1024]{2,1,0:T(8,128)(2,1)} %bitcast.108), calls=%async_computation | async-start | bytes 8388608 | tf_op jit(solution)/shard_map/all_to_all | solution.py:102
  25.4 93.3 %all-to-all-done = bf16[128,16,1024]{2,1,0:T(8,128)(2,1)} async-done(((bf16[128,16,1024]{2,1,0:T(8,128)(2,1)}), bf16[128,16,1024]{2,1,0:T(8,128)(2,1)}, u32[]{:S(2)}, u32[]{:S(2)}) %all-to-all-start) | async-done | bytes 4194336 | tf_op jit(solution)/shard_map/all_to_all | solution.py:102
  121.9 7.6 %fusion.76 = f32[1024,1024,1]{1,0,2:T(8,128)S(1)} fusion(bf16[128,16,1024]{2,1,0:T(8,128)(2,1)} %all-to-all-done), kind=kOutput, calls=%fused_computation.162 | convolution fusion | flops 4294967296 | bytes 8388608 | tf_op jit(solution)/shard_map/dot_general | solution.py:13
  129.5 7.4 %select_reduce_fusion = (f32[]{:T(128)}, f32[1024,1024]{1,0:T(8,128)}) fusion(bf16[2048,1024]{1,0:T(8,128)(2,1)S(1)} %collective-permute-done, f32[1024,1024,1]{1,0,2:T(8,128)S(1)} %fusion.76), kind=kOutput, calls=%fused_computation.8 | convolution fusion | flops 4300210176 | bytes 12582916 | tf_op jit(solution)/shard_map/dot_general | solution.py:13
  142.0 11.7 %cholesky.242 = f32[128,128]{1,0:T(8,128)S(1)} custom-call(f32[128,128]{1,0:T(8,128)S(1)} %cholesky.654), custom_call_target="Cholesky" | custom-call | tf_op jit(solution)/shard_map/jit(cholesky)/cholesky | solution.py:112
  153.8 9.8 %custom-call.64 = f32[1,128,128]{1,2,0:T(8,128)S(1)} custom-call(f32[1,128,128]{2,1,0:T(8,128)S(1)} %get-tuple-element.37), custom_call_target="InvertDiagBlocksLowerTriangular" | custom-call | tf_op jit(solution)/shard_map/jit(cholesky)/cholesky | solution.py:112
  170.0 11.7 %cholesky.265 = f32[128,128]{1,0:T(8,128)S(1)} custom-call(f32[128,128]{1,0:T(8,128)S(1)} %cholesky.658), custom_call_target="Cholesky" | custom-call | tf_op jit(solution)/shard_map/jit(cholesky)/cholesky | solution.py:112
  182.4 10.2 %custom-call.65 = f32[1,128,128]{1,2,0:T(8,128)S(1)} custom-call(f32[1,128,128]{2,1,0:T(8,128)S(1)} %get-tuple-element.34), custom_call_target="InvertDiagBlocksLowerTriangular" | custom-call | tf_op jit(solution)/shard_map/jit(cholesky)/cholesky | solution.py:112
  195.9 11.7 %cholesky.506 = f32[128,128]{1,0:T(8,128)S(1)} custom-call(f32[128,128]{1,0:T(8,128)S(1)} %cholesky.663), custom_call_target="Cholesky" | custom-call | tf_op jit(solution)/shard_map/jit(cholesky)/cholesky | solution.py:112
  208.9 9.8 %custom-call.66 = f32[1,128,128]{1,2,0:T(8,128)S(1)} custom-call(f32[1,128,128]{2,1,0:T(8,128)S(1)} %get-tuple-element.31), custom_call_target="InvertDiagBlocksLowerTriangular" | custom-call | tf_op jit(solution)/shard_map/jit(cholesky)/cholesky | solution.py:112
  222.2 11.9 %cholesky.525 = f32[128,128]{1,0:T(8,128)S(1)} custom-call(f32[128,128]{1,0:T(8,128)S(1)} %cholesky.668), custom_call_target="Cholesky" | custom-call | tf_op jit(solution)/shard_map/jit(cholesky)/cholesky | solution.py:112
  235.4 9.8 %custom-call.67 = f32[1,128,128]{1,2,0:T(8,128)S(1)} custom-call(f32[1,128,128]{2,1,0:T(8,128)S(1)} %get-tuple-element.28), custom_call_target="InvertDiagBlocksLowerTriangular" | custom-call | tf_op jit(solution)/shard_map/jit(cholesky)/cholesky | solution.py:112
  248.6 11.7 %cholesky.544 = f32[128,128]{1,0:T(8,128)S(1)} custom-call(f32[128,128]{1,0:T(8,128)S(1)} %cholesky.673), custom_call_target="Cholesky" | custom-call | tf_op jit(solution)/shard_map/jit(cholesky)/cholesky | solution.py:112
  261.6 9.8 %custom-call.68 = f32[1,128,128]{1,2,0:T(8,128)S(1)} custom-call(f32[1,128,128]{2,1,0:T(8,128)S(1)} %get-tuple-element.25), custom_call_target="InvertDiagBlocksLowerTriangular" | custom-call | tf_op jit(solution)/shard_map/jit(cholesky)/cholesky | solution.py:112
  275.0 11.7 %cholesky.564 = f32[128,128]{1,0:T(8,128)S(1)} custom-call(f32[128,128]{1,0:T(8,128)S(1)} %cholesky.678), custom_call_target="Cholesky" | custom-call | tf_op jit(solution)/shard_map/jit(cholesky)/cholesky | solution.py:112
  288.0 9.8 %custom-call.69 = f32[1,128,128]{1,2,0:T(8,128)S(1)} custom-call(f32[1,128,128]{2,1,0:T(8,128)S(1)} %get-tuple-element.22), custom_call_target="InvertDiagBlocksLowerTriangular" | custom-call | tf_op jit(solution)/shard_map/jit(cholesky)/cholesky | solution.py:112
  300.8 11.7 %cholesky.584 = f32[128,128]{1,0:T(8,128)S(1)} custom-call(f32[128,128]{1,0:T(8,128)S(1)} %cholesky.683), custom_call_target="Cholesky" | custom-call | tf_op jit(solution)/shard_map/jit(cholesky)/cholesky | solution.py:112
  313.8 10.2 %custom-call.70 = f32[1,128,128]{1,2,0:T(8,128)S(1)} custom-call(f32[1,128,128]{2,1,0:T(8,128)S(1)} %get-tuple-element.19), custom_call_target="InvertDiagBlocksLowerTriangular" | custom-call | tf_op jit(solution)/shard_map/jit(cholesky)/cholesky | solution.py:112
  326.6 11.7 %cholesky.602 = f32[128,128]{1,0:T(8,128)S(1)} custom-call(f32[128,128]{1,0:T(8,128)S(1)} %slice_subtract_fusion.7), custom_call_target="Cholesky" | custom-call | tf_op jit(solution)/shard_map/jit(cholesky)/cholesky | solution.py:112
  350.1 5.2 fusion.1
  371.3 13.8 %collective-permute-done.1 = f32[64,28,128]{2,0,1:T(8,128)} collective-permute-done((f32[64,28,128]{2,0,1:T(8,128)S(1)}, f32[64,28,128]{2,0,1:T(8,128)}, u32[]{:S(2)}, u32[]{:S(2)}) %collective-permute-start.1) | collective-permute-done | bytes 917536 | tf_op jit(solution)/shard_map/ppermute | solution.py:39
  387.2 5.3 collective-permute-done.8
  396.5 5.8 %collective-permute-done.2 = f32[32,28,128]{2,0,1:T(8,128)} collective-permute-done((f32[32,28,128]{2,0,1:T(8,128)S(1)}, f32[32,28,128]{2,0,1:T(8,128)}, u32[]{:S(2)}, u32[]{:S(2)}) %collective-permute-start.2) | collective-permute-done | bytes 458784 | tf_op jit(solution)/shard_map/ppermute | solution.py:39
  453.1 4.9 collective-permute-done.18
  465.2 6.6 %collective-permute-done.20 = f32[384,128]{1,0:T(8,128)S(1)} collective-permute-done((f32[384,128]{1,0:T(8,128)S(1)}, f32[384,128]{1,0:T(8,128)S(1)}, u32[]{:S(2)}, u32[]{:S(2)}) %collective-permute-start.20) | collective-permute-done | bytes 196640 | tf_op jit(solution)/shard_map/ppermute | solution.py:47
  473.9 7.8 %collective-permute-done.21 = f32[384,128]{1,0:T(8,128)S(1)} collective-permute-done((f32[384,128]{1,0:T(8,128)S(1)}, f32[384,128]{1,0:T(8,128)S(1)}, u32[]{:S(2)}, u32[]{:S(2)}) %collective-permute-start.21) | collective-permute-done | bytes 196640 | tf_op jit(solution)/shard_map/ppermute | solution.py:47
  481.8 16.3 %collective-permute-start.22 = (f32[384,128]{1,0:T(8,128)S(1)}, f32[384,128]{1,0:T(8,128)S(1)}, u32[]{:S(2)}, u32[]{:S(2)}) collective-permute-start(f32[384,128]{1,0:T(8,128)S(1)} %add.293), channel_id=1, source_target_pairs={{0,1},{1,0},{2,3},{3,2},{4,5},{5,4},{6,7},{7,6},{8,9},{9,8},{10,11... | collective-permute-start | bytes 589832 | tf_op jit(solution)/shard_map/ppermute | solution.py:48
  501.2 11.7 %cholesky.634 = f32[128,128]{1,0:T(8,128)S(1)} custom-call(f32[128,128]{1,0:T(8,128)S(1)} %slice.207), custom_call_target="Cholesky" | custom-call | tf_op jit(solution)/shard_map/jit(cholesky)/cholesky | solution.py:80
  514.3 9.8 %custom-call.72 = f32[1,128,128]{1,2,0:T(8,128)S(1)} custom-call(f32[1,128,128]{2,1,0:T(8,128)S(1)} %fusion.44), custom_call_target="InvertDiagBlocksLowerTriangular" | custom-call | tf_op jit(solution)/shard_map/jit(_solve_triangular)/triangular_solve | solution.py:81
  525.2 11.7 %cholesky.645 = f32[128,128]{1,0:T(8,128)S(1)} custom-call(f32[128,128]{1,0:T(8,128)S(1)} %slice_subtract_fusion.6), custom_call_target="Cholesky" | custom-call | tf_op jit(solution)/shard_map/jit(cholesky)/cholesky | solution.py:83
  538.2 9.8 %custom-call.73 = f32[1,128,128]{1,2,0:T(8,128)S(1)} custom-call(f32[1,128,128]{2,1,0:T(8,128)S(1)} %fusion.45), custom_call_target="InvertDiagBlocksLowerTriangular" | custom-call | tf_op jit(solution)/shard_map/jit(_solve_triangular)/triangular_solve | solution.py:84
  (162 shorter events, 139.2 us)
Async XLA Ops:
  0.6 1.6 copy-start
  8.5 110.2 %all-to-all-start = ((bf16[128,16,1024]{2,1,0:T(8,128)(2,1)}), bf16[128,16,1024]{2,1,0:T(8,128)(2,1)}, u32[]{:S(2)}, u32[]{:S(2)}) async-start(bf16[128,16,1024]{2,1,0:T(8,128)(2,1)} %bitcast.108), calls=%async_computation | async-start | bytes 8388608 | tf_op jit(solution)/shard_map/all_to_all | solution.py:102
  118.7 10.7 %collective-permute-start = (bf16[2048,1024]{1,0:T(8,128)(2,1)}, bf16[2048,1024]{1,0:T(8,128)(2,1)S(1)}, u32[]{:S(2)}, u32[]{:S(2)}) collective-permute-start(bf16[2048,1024]{1,0:T(8,128)(2,1)} %bitcast.3), channel_id=1, source_target_pairs={{0,1},{1,0},{2,3},{3,2},{4,5},{5,4},{6,7},{7,6},{8,9},{9,8},{10,11... | collective-permute-start | bytes 12582920 | tf_op jit(solution)/shard_map/ppermute | solution.py:105
  140.1 1.9 copy-start.3
  345.3 2.8 copy-start.7
  348.0 7.2 %copy-start.2 = (f32[1024,1024]{1,0:T(8,128)}, f32[1024,1024]{1,0:T(8,128)S(1)}, u32[]{:S(2)}) copy-start(f32[1024,1024]{1,0:T(8,128)S(1)} %select_select_fusion) | copy-start | bytes 12582916
  361.6 1.3 copy-start.4
  362.9 22.1 %collective-permute-start.1 = (f32[64,28,128]{2,0,1:T(8,128)S(1)}, f32[64,28,128]{2,0,1:T(8,128)}, u32[]{:S(2)}, u32[]{:S(2)}) collective-permute-start(f32[64,28,128]{2,0,1:T(8,128)S(1)} %constant_dynamic-slice_fusion.14), channel_id=1, source_target_pairs={{0,2},{2,0},{4,6},{6,4},{8,10},{10,8},{12,14},{14,12},{16,18},{18,... | collective-permute-start | bytes 2752520 | tf_op jit(solution)/shard_map/ppermute | solution.py:39
  369.1 15.9 %copy-start.5 = (f32[2,2,2,2,2,2,2,28,128]{8,6,5,4,3,2,1,0,7:T(2,128)S(1)}, f32[2,2,2,2,2,2,2,28,128]{8,6,5,4,3,2,1,0,7:T(2,128)}, u32[]{:S(2)}) copy-start(f32[2,2,2,2,2,2,2,28,128]{8,6,5,4,3,2,1,0,7:T(2,128)} %copy-done.4) | copy-start | bytes 5505028
  370.6 21.9 %collective-permute-start.8 = (f32[64,28,128]{2,0,1:T(8,128)}, f32[64,28,128]{2,0,1:T(8,128)}, u32[]{:S(2)}, u32[]{:S(2)}) collective-permute-start(f32[64,28,128]{2,0,1:T(8,128)} %get-tuple-element.14), channel_id=1, source_target_pairs={{0,8},{2,10},{4,12},{6,14},{8,0},{10,2},{12,4},{14,6},{16,24},{18,... | collective-permute-start | bytes 2752520 | tf_op jit(solution)/shard_map/ppermute | solution.py:39
  371.3 21.3 %copy-start.6 = (f32[64,28,128]{2,0,1:T(8,128)S(1)}, f32[64,28,128]{2,0,1:T(8,128)}, u32[]{:S(2)}) copy-start(f32[64,28,128]{2,0,1:T(8,128)} %get-tuple-element.15) | copy-start | bytes 2752516
  386.4 16.0 %collective-permute-start.2 = (f32[32,28,128]{2,0,1:T(8,128)S(1)}, f32[32,28,128]{2,0,1:T(8,128)}, u32[]{:S(2)}, u32[]{:S(2)}) collective-permute-start(f32[32,28,128]{2,0,1:T(8,128)S(1)} %constant_dynamic-slice_fusion.13), channel_id=1, source_target_pairs={{0,8},{2,10},{4,12},{6,14},{8,0},{10,2},{12,4},{14,6},{16,24},{18,... | collective-permute-start | bytes 1376264 | tf_op jit(solution)/shard_map/ppermute | solution.py:39
  394.8 12.0 %collective-permute-start.9 = (f32[32,28,128]{2,1,0:T(8,128)S(1)}, f32[32,28,128]{2,1,0:T(8,128)S(1)}, u32[]{:S(2)}, u32[]{:S(2)}) collective-permute-start(f32[32,28,128]{2,1,0:T(8,128)S(1)} %constant_dynamic-slice_fusion.5), channel_id=1, source_target_pairs={{0,32},{2,34},{4,36},{6,38},{8,40},{10,42},{12,44},{14,46},{16,48}... | collective-permute-start | bytes 1376264 | tf_op jit(solution)/shard_map/ppermute | solution.py:39
  403.5 8.3 %collective-permute-start.3 = (f32[16,28,128]{2,0,1:T(8,128)S(1)}, f32[16,28,128]{2,0,1:T(8,128)S(1)}, u32[]{:S(2)}, u32[]{:S(2)}) collective-permute-start(f32[16,28,128]{2,0,1:T(8,128)S(1)} %constant_dynamic-slice_fusion.12), channel_id=1, source_target_pairs={{0,32},{2,34},{4,36},{6,38},{8,40},{10,42},{12,44},{14,46},{16,48}... | collective-permute-start | bytes 688136 | tf_op jit(solution)/shard_map/ppermute | solution.py:39
  406.9 7.4 %collective-permute-start.10 = (f32[16,28,128]{2,1,0:T(8,128)S(1)}, f32[16,28,128]{2,1,0:T(8,128)S(1)}, u32[]{:S(2)}, u32[]{:S(2)}) collective-permute-start(f32[16,28,128]{2,1,0:T(8,128)S(1)} %constant_dynamic-slice_fusion.4), channel_id=1, source_target_pairs={{0,2},{2,0},{4,6},{6,4},{8,10},{10,8},{12,14},{14,12},{16,18},{18,... | collective-permute-start | bytes 688136 | tf_op jit(solution)/shard_map/ppermute | solution.py:39
  411.8 6.1 %collective-permute-start.4 = (f32[8,28,128]{2,0,1:T(8,128)S(1)}, f32[8,28,128]{2,0,1:T(8,128)S(1)}, u32[]{:S(2)}, u32[]{:S(2)}) collective-permute-start(f32[8,28,128]{2,0,1:T(8,128)S(1)} %constant_dynamic-slice_fusion.11), channel_id=1, source_target_pairs={{0,4},{2,6},{4,0},{6,2},{8,12},{10,14},{12,8},{14,10},{16,20},{18,... | collective-permute-start | bytes 344072 | tf_op jit(solution)/shard_map/ppermute | solution.py:39
  414.4 5.8 %collective-permute-start.11 = (f32[8,28,128]{2,1,0:T(8,128)S(1)}, f32[8,28,128]{2,1,0:T(8,128)S(1)}, u32[]{:S(2)}, u32[]{:S(2)}) collective-permute-start(f32[8,28,128]{2,1,0:T(8,128)S(1)} %constant_dynamic-slice_fusion.3), channel_id=1, source_target_pairs={{0,16},{2,18},{4,20},{6,22},{8,24},{10,26},{12,28},{14,30},{16,0},... | collective-permute-start | bytes 344072 | tf_op jit(solution)/shard_map/ppermute | solution.py:39
  418.0 4.6 collective-permute-start.5
  420.3 4.4 collective-permute-start.12
  422.6 4.6 collective-permute-start.6
  424.7 5.8 %collective-permute-start.13 = (f32[2,28,128]{2,1,0:T(8,128)S(1)}, f32[2,28,128]{2,1,0:T(8,128)S(1)}, u32[]{:S(2)}, u32[]{:S(2)}) collective-permute-start(f32[2,28,128]{2,1,0:T(8,128)S(1)} %constant_dynamic-slice_fusion.1), channel_id=1, source_target_pairs={{0,4},{2,6},{4,0},{6,2},{8,12},{10,14},{12,8},{14,10},{16,20},{18,... | collective-permute-start | bytes 86024 | tf_op jit(solution)/shard_map/ppermute | solution.py:39
  427.3 6.6 %collective-permute-start.7 = (f32[1,28,128]{2,0,1:T(1,128)S(1)}, f32[1,28,128]{2,0,1:T(1,128)S(1)}, u32[]{:S(2)}, u32[]{:S(2)}) collective-permute-start(f32[1,28,128]{2,0,1:T(1,128)S(1)} %constant_dynamic-slice_fusion.8), channel_id=1, source_target_pairs={{0,128},{2,130},{4,132},{6,134},{8,136},{10,138},{12,140},{14,142}... | collective-permute-start | bytes 43016 | tf_op jit(solution)/shard_map/ppermute | solution.py:39
  430.5 6.6 %collective-permute-start.14 = (f32[1,28,128]{2,1,0:T(8,128)S(1)}, f32[1,28,128]{2,1,0:T(8,128)S(1)}, u32[]{:S(2)}, u32[]{:S(2)}) collective-permute-start(f32[1,28,128]{2,1,0:T(8,128)S(1)} %constant_dynamic-slice_fusion), channel_id=1, source_target_pairs={{0,128},{2,130},{4,132},{6,134},{8,136},{10,138},{12,140},{14,142}... | collective-permute-start | bytes 43016 | tf_op jit(solution)/shard_map/ppermute | solution.py:39
  437.8 4.9 collective-permute-start.15
  442.7 4.6 collective-permute-start.16
  447.3 4.6 collective-permute-start.17
  451.9 6.1 %collective-permute-start.18 = (f32[384,128]{1,0:T(8,128)S(1)}, f32[384,128]{1,0:T(8,128)S(1)}, u32[]{:S(2)}, u32[]{:S(2)}) collective-permute-start(f32[384,128]{1,0:T(8,128)S(1)} %add.289), channel_id=1, source_target_pairs={{0,4},{2,6},{4,0},{6,2},{8,12},{10,14},{12,8},{14,10},{16,20},{18,... | collective-permute-start | bytes 589832 | tf_op jit(solution)/shard_map/ppermute | solution.py:47
  458.1 91.4 %copy-start.1 = (bf16[128,8,1024]{2,1,0:T(8,128)(2,1)S(1)}, bf16[128,8,1024]{2,1,0:T(8,128)(2,1)}, u32[]{:S(2)}) copy-start(bf16[128,8,1024]{2,1,0:T(8,128)(2,1)} %param.8) | copy-start | bytes 6291460
  458.1 6.1 %collective-permute-start.19 = (f32[384,128]{1,0:T(8,128)S(1)}, f32[384,128]{1,0:T(8,128)S(1)}, u32[]{:S(2)}, u32[]{:S(2)}) collective-permute-start(f32[384,128]{1,0:T(8,128)S(1)} %add.290), channel_id=1, source_target_pairs={{0,16},{2,18},{4,20},{6,22},{8,24},{10,26},{12,28},{14,30},{16,0},... | collective-permute-start | bytes 589832 | tf_op jit(solution)/shard_map/ppermute | solution.py:47
  464.2 7.6 %collective-permute-start.20 = (f32[384,128]{1,0:T(8,128)S(1)}, f32[384,128]{1,0:T(8,128)S(1)}, u32[]{:S(2)}, u32[]{:S(2)}) collective-permute-start(f32[384,128]{1,0:T(8,128)S(1)} %add.291), channel_id=1, source_target_pairs={{0,64},{2,66},{4,68},{6,70},{8,72},{10,74},{12,76},{14,78},{16,80}... | collective-permute-start | bytes 589832 | tf_op jit(solution)/shard_map/ppermute | solution.py:47
  471.9 9.9 %collective-permute-start.21 = (f32[384,128]{1,0:T(8,128)S(1)}, f32[384,128]{1,0:T(8,128)S(1)}, u32[]{:S(2)}, u32[]{:S(2)}) collective-permute-start(f32[384,128]{1,0:T(8,128)S(1)} %add.292), channel_id=1, source_target_pairs={{0,128},{2,130},{4,132},{6,134},{8,136},{10,138},{12,140},{14,142}... | collective-permute-start | bytes 589832 | tf_op jit(solution)/shard_map/ppermute | solution.py:47
  481.8 19.4 %collective-permute-start.22 = (f32[384,128]{1,0:T(8,128)S(1)}, f32[384,128]{1,0:T(8,128)S(1)}, u32[]{:S(2)}, u32[]{:S(2)}) collective-permute-start(f32[384,128]{1,0:T(8,128)S(1)} %add.293), channel_id=1, source_target_pairs={{0,1},{1,0},{2,3},{3,2},{4,5},{5,4},{6,7},{7,6},{8,9},{9,8},{10,11... | collective-permute-start | bytes 589832 | tf_op jit(solution)/shard_map/ppermute | solution.py:48

commit v7 on v6

--- a/solution.py
+++ b/solution.py
@@ -27,18 +27,25 @@
     me = lax.axis_index("expert")
     width = cols // len(orders)
     outs = []
+    def halve(part, b):
+        half = part.shape[0] // 2
+        v = (me >> b) & 1
+        keep = lax.dynamic_slice_in_dim(part, v * half, half, 0)
+        send = lax.dynamic_slice_in_dim(part, (1 - v) * half, half, 0)
+        return keep + lax.ppermute(send, "expert", xor_pairs(n_exp, 1 << b))
+
+    lead = next(k for k in range(n_bits + 1) if all(o[k:] == orders[0][k:] for o in orders))
     for s, order in enumerate(orders):
         part = term[s * width:(s + 1) * width].reshape([width] + [2] * n_bits + [rows])
         perm = [n_bits - b for b in order] + [n_bits + 1, 0]
         part = part.transpose(perm).reshape(n_exp, rows, width)
-        for b in order:
-            half = part.shape[0] // 2
-            v = (me >> b) & 1
-            keep = lax.dynamic_slice_in_dim(part, v * half, half, 0)
-            send = lax.dynamic_slice_in_dim(part, (1 - v) * half, half, 0)
-            part = keep + lax.ppermute(send, "expert", xor_pairs(n_exp, 1 << b))
-        outs.append(part[0])
-    return jnp.concatenate(outs, axis=-1)
+        for b in order[:lead]:
+            part = halve(part, b)
+        outs.append(part)
+    part = jnp.concatenate(outs, axis=-1)
+    for b in orders[0][lead:]:
+        part = halve(part, b)
+    return part[0]
 
 
 def all_sum(x, order):
@@ -57,9 +64,9 @@
     orders = []
     for s in range(n_streams):
         turn = axes[s % len(axes):] + axes[:s % len(axes)]
-        order = []
-        for level in range(max(len(a) for a in turn)):
-            order += [a[level] for a in turn if level < len(a)]
+        order = [a[0] for a in turn]
+        for level in range(1, max(len(a) for a in axes)):
+            order += [a[level] for a in axes if level < len(a)]
         orders.append(order)
     return orders
 

time: 557 us -> 559 us (level)
  waiting for transfers between devices: 167 us -> 173 us
  starting transfers between devices: 68.1 us -> 62.3 us
    ppermute x14 -> x10, waiting for transfers between devices: 37.6 us -> 45.7 us  [halve(): return keep + lax.ppermute(send, 'expert', xor_pairs(n_exp, 1 << b))]
    ppermute x14 -> x10, starting transfers between devices: 23.9 us -> 15.9 us  [halve(): return keep + lax.ppermute(send, 'expert', xor_pairs(n_exp, 1 << b))]
  transfers between devices with their start and end apart: 24 -> 20, of which waited for: 18 -> 17; matrix products, arithmetic and copies ran while one was open for 4% -> 4% of each run, Pallas kernels for 0% -> 0%
where the time goes in v7:
time: 559 us; the launch traced here: 552 us
  other arithmetic  229 us (41%)
  waiting for transfers between devices  173 us (31%)
  starting transfers between devices  62.3 us (11%)
  matrix products  54.3 us (10%)
  local copies, waits for them, and re-layouts  25.2 us (5%)
  between operations  7.15 us (1%)
    another operation x30, other arithmetic, local(): whitening = jnp.linalg.cholesky(damped, symmetrize_input=False)  172 us
    all_to_all x1, waiting for transfers between devices, local(): lax.all_to_all(outgoing, 'expert', split_axis=0, concat_axis=0, tiled=True)  93.3 us
    ppermute x10, waiting for transfers between devices, halve(): return keep + lax.ppermute(send, 'expert', xor_pairs(n_exp, 1 << b))  45.7 us
    ppermute x7, waiting for transfers between devices, all_sum(): x = x + lax.ppermute(x, 'expert', xor_pairs(n_exp, 1 << b))  34.5 us
    dot_general x4, matrix products, contract(): lax.dot_general(left, right, (((0,), (0,)), ((), ())), preferred_element_...  26.4 us
    another operation x14, matrix products, local(): whitening = jnp.linalg.cholesky(damped, symmetrize_input=False)  23.3 us
    all_to_all x1, starting transfers between devices, local(): lax.all_to_all(outgoing, 'expert', split_axis=0, concat_axis=0, tiled=True)  16.9 us
    ppermute x10, starting transfers between devices, halve(): return keep + lax.ppermute(send, 'expert', xor_pairs(n_exp, 1 << b))  15.9 us
  transfers between devices with their start and end apart: 20, of which 17 were waited for; matrix products, arithmetic and copies ran while one was open for 4% of the time, Pallas kernels for 0%

profile of v7, /device:TPU:1, one launch (start us, length us, event | category | flops | bytes accessed | tf_op | source)
XLA Modules:
  0.0 551.7 jit_solution(9278961473990871942)
XLA Ops:
  2.3 6.3 %fusion.5 = bf16[2048,1024]{1,0:T(8,128)(2,1)} fusion(s32[1024]{0:T(1024)S(1)} %eq.22, bf16[128,8,1024]{2,1,0:T(8,128)(2,1)S(1)} %copy-done), kind=kOutput, calls=%fused_computation.12 | convolution fusion | flops 4299161600 | bytes 6295552 | tf_op jit(solution)/shard_map/dot_general | solution.py:13
  8.5 16.9 %all-to-all-start = ((bf16[128,16,1024]{2,1,0:T(8,128)(2,1)}), bf16[128,16,1024]{2,1,0:T(8,128)(2,1)}, u32[]{:S(2)}, u32[]{:S(2)}) async-start(bf16[128,16,1024]{2,1,0:T(8,128)(2,1)} %bitcast.96), calls=%async_computation | async-start | bytes 8388608 | tf_op jit(solution)/shard_map/all_to_all | solution.py:109
  25.4 93.3 %all-to-all-done = bf16[128,16,1024]{2,1,0:T(8,128)(2,1)} async-done(((bf16[128,16,1024]{2,1,0:T(8,128)(2,1)}), bf16[128,16,1024]{2,1,0:T(8,128)(2,1)}, u32[]{:S(2)}, u32[]{:S(2)}) %all-to-all-start) | async-done | bytes 4194336 | tf_op jit(solution)/shard_map/all_to_all | solution.py:109
  121.9 7.6 %fusion.76 = f32[1024,1024,1]{1,0,2:T(8,128)S(1)} fusion(bf16[128,16,1024]{2,1,0:T(8,128)(2,1)} %all-to-all-done), kind=kOutput, calls=%fused_computation.157 | convolution fusion | flops 4294967296 | bytes 8388608 | tf_op jit(solution)/shard_map/dot_general | solution.py:13
  129.5 7.4 %select_reduce_fusion = (f32[]{:T(128)}, f32[1024,1024]{1,0:T(8,128)}) fusion(bf16[2048,1024]{1,0:T(8,128)(2,1)S(1)} %collective-permute-done, f32[1024,1024,1]{1,0,2:T(8,128)S(1)} %fusion.76), kind=kOutput, calls=%fused_computation.8 | convolution fusion | flops 4300210176 | bytes 12582916 | tf_op jit(solution)/shard_map/dot_general | solution.py:13
  142.0 11.7 %cholesky.242 = f32[128,128]{1,0:T(8,128)S(1)} custom-call(f32[128,128]{1,0:T(8,128)S(1)} %cholesky.654), custom_call_target="Cholesky" | custom-call | tf_op jit(solution)/shard_map/jit(cholesky)/cholesky | solution.py:119
  153.8 9.8 %custom-call.64 = f32[1,128,128]{1,2,0:T(8,128)S(1)} custom-call(f32[1,128,128]{2,1,0:T(8,128)S(1)} %get-tuple-element.39), custom_call_target="InvertDiagBlocksLowerTriangular" | custom-call | tf_op jit(solution)/shard_map/jit(cholesky)/cholesky | solution.py:119
  170.0 11.7 %cholesky.265 = f32[128,128]{1,0:T(8,128)S(1)} custom-call(f32[128,128]{1,0:T(8,128)S(1)} %cholesky.658), custom_call_target="Cholesky" | custom-call | tf_op jit(solution)/shard_map/jit(cholesky)/cholesky | solution.py:119
  182.4 10.2 %custom-call.65 = f32[1,128,128]{1,2,0:T(8,128)S(1)} custom-call(f32[1,128,128]{2,1,0:T(8,128)S(1)} %get-tuple-element.36), custom_call_target="InvertDiagBlocksLowerTriangular" | custom-call | tf_op jit(solution)/shard_map/jit(cholesky)/cholesky | solution.py:119
  195.9 11.7 %cholesky.506 = f32[128,128]{1,0:T(8,128)S(1)} custom-call(f32[128,128]{1,0:T(8,128)S(1)} %cholesky.663), custom_call_target="Cholesky" | custom-call | tf_op jit(solution)/shard_map/jit(cholesky)/cholesky | solution.py:119
  208.9 9.8 %custom-call.66 = f32[1,128,128]{1,2,0:T(8,128)S(1)} custom-call(f32[1,128,128]{2,1,0:T(8,128)S(1)} %get-tuple-element.33), custom_call_target="InvertDiagBlocksLowerTriangular" | custom-call | tf_op jit(solution)/shard_map/jit(cholesky)/cholesky | solution.py:119
  222.2 11.9 %cholesky.525 = f32[128,128]{1,0:T(8,128)S(1)} custom-call(f32[128,128]{1,0:T(8,128)S(1)} %cholesky.668), custom_call_target="Cholesky" | custom-call | tf_op jit(solution)/shard_map/jit(cholesky)/cholesky | solution.py:119
  235.4 9.8 %custom-call.67 = f32[1,128,128]{1,2,0:T(8,128)S(1)} custom-call(f32[1,128,128]{2,1,0:T(8,128)S(1)} %get-tuple-element.30), custom_call_target="InvertDiagBlocksLowerTriangular" | custom-call | tf_op jit(solution)/shard_map/jit(cholesky)/cholesky | solution.py:119
  248.6 11.7 %cholesky.544 = f32[128,128]{1,0:T(8,128)S(1)} custom-call(f32[128,128]{1,0:T(8,128)S(1)} %cholesky.673), custom_call_target="Cholesky" | custom-call | tf_op jit(solution)/shard_map/jit(cholesky)/cholesky | solution.py:119
  261.6 9.8 %custom-call.68 = f32[1,128,128]{1,2,0:T(8,128)S(1)} custom-call(f32[1,128,128]{2,1,0:T(8,128)S(1)} %get-tuple-element.27), custom_call_target="InvertDiagBlocksLowerTriangular" | custom-call | tf_op jit(solution)/shard_map/jit(cholesky)/cholesky | solution.py:119
  275.0 11.7 %cholesky.564 = f32[128,128]{1,0:T(8,128)S(1)} custom-call(f32[128,128]{1,0:T(8,128)S(1)} %cholesky.678), custom_call_target="Cholesky" | custom-call | tf_op jit(solution)/shard_map/jit(cholesky)/cholesky | solution.py:119
  288.0 9.8 %custom-call.69 = f32[1,128,128]{1,2,0:T(8,128)S(1)} custom-call(f32[1,128,128]{2,1,0:T(8,128)S(1)} %get-tuple-element.24), custom_call_target="InvertDiagBlocksLowerTriangular" | custom-call | tf_op jit(solution)/shard_map/jit(cholesky)/cholesky | solution.py:119
  300.8 11.7 %cholesky.584 = f32[128,128]{1,0:T(8,128)S(1)} custom-call(f32[128,128]{1,0:T(8,128)S(1)} %cholesky.683), custom_call_target="Cholesky" | custom-call | tf_op jit(solution)/shard_map/jit(cholesky)/cholesky | solution.py:119
  313.8 10.2 %custom-call.70 = f32[1,128,128]{1,2,0:T(8,128)S(1)} custom-call(f32[1,128,128]{2,1,0:T(8,128)S(1)} %get-tuple-element.21), custom_call_target="InvertDiagBlocksLowerTriangular" | custom-call | tf_op jit(solution)/shard_map/jit(cholesky)/cholesky | solution.py:119
  326.6 11.7 %cholesky.602 = f32[128,128]{1,0:T(8,128)S(1)} custom-call(f32[128,128]{1,0:T(8,128)S(1)} %slice_subtract_fusion.7), custom_call_target="Cholesky" | custom-call | tf_op jit(solution)/shard_map/jit(cholesky)/cholesky | solution.py:119
  350.1 5.2 fusion.1
  369.9 15.0 %collective-permute-done.4 = f32[64,28,128]{2,0,1:T(8,128)} collective-permute-done((f32[64,28,128]{2,0,1:T(8,128)}, f32[64,28,128]{2,0,1:T(8,128)}, u32[]{:S(2)}, u32[]{:S(2)}) %collective-permute-start.4) | collective-permute-done | bytes 917536 | tf_op jit(solution)/shard_map/ppermute | solution.py:35
  396.1 4.7 collective-permute-done.5
  401.8 6.2 %collective-permute-done.2 = f32[32,28,128]{2,1,0:T(8,128)S(1)} collective-permute-done((f32[32,28,128]{2,1,0:T(8,128)}, f32[32,28,128]{2,1,0:T(8,128)S(1)}, u32[]{:S(2)}, u32[]{:S(2)}) %collective-permute-start.2) | collective-permute-done | bytes 458784 | tf_op jit(solution)/shard_map/ppermute | solution.py:35
  409.5 4.5 collective-permute-done.3
  466.9 7.0 %collective-permute-done.16 = f32[384,128]{1,0:T(8,128)S(1)} collective-permute-done((f32[384,128]{1,0:T(8,128)S(1)}, f32[384,128]{1,0:T(8,128)S(1)}, u32[]{:S(2)}, u32[]{:S(2)}) %collective-permute-start.16) | collective-permute-done | bytes 196640 | tf_op jit(solution)/shard_map/ppermute | solution.py:54
  476.7 7.9 %collective-permute-done.17 = f32[384,128]{1,0:T(8,128)S(1)} collective-permute-done((f32[384,128]{1,0:T(8,128)S(1)}, f32[384,128]{1,0:T(8,128)S(1)}, u32[]{:S(2)}, u32[]{:S(2)}) %collective-permute-start.17) | collective-permute-done | bytes 196640 | tf_op jit(solution)/shard_map/ppermute | solution.py:54
  484.6 15.3 %collective-permute-start.18 = (f32[384,128]{1,0:T(8,128)S(1)}, f32[384,128]{1,0:T(8,128)S(1)}, u32[]{:S(2)}, u32[]{:S(2)}) collective-permute-start(f32[384,128]{1,0:T(8,128)S(1)} %add.251), channel_id=1, source_target_pairs={{0,1},{1,0},{2,3},{3,2},{4,5},{5,4},{6,7},{7,6},{8,9},{9,8},{10,11... | collective-permute-start | bytes 589832 | tf_op jit(solution)/shard_map/ppermute | solution.py:55
  503.1 11.7 %cholesky.634 = f32[128,128]{1,0:T(8,128)S(1)} custom-call(f32[128,128]{1,0:T(8,128)S(1)} %slice.219), custom_call_target="Cholesky" | custom-call | tf_op jit(solution)/shard_map/jit(cholesky)/cholesky | solution.py:87
  516.1 9.8 %custom-call.72 = f32[1,128,128]{1,2,0:T(8,128)S(1)} custom-call(f32[1,128,128]{2,1,0:T(8,128)S(1)} %fusion.47), custom_call_target="InvertDiagBlocksLowerTriangular" | custom-call | tf_op jit(solution)/shard_map/jit(_solve_triangular)/triangular_solve | solution.py:88
  527.0 11.7 %cholesky.645 = f32[128,128]{1,0:T(8,128)S(1)} custom-call(f32[128,128]{1,0:T(8,128)S(1)} %slice_subtract_fusion.6), custom_call_target="Cholesky" | custom-call | tf_op jit(solution)/shard_map/jit(cholesky)/cholesky | solution.py:90
  540.1 9.8 %custom-call.73 = f32[1,128,128]{1,2,0:T(8,128)S(1)} custom-call(f32[1,128,128]{2,1,0:T(8,128)S(1)} %fusion.48), custom_call_target="InvertDiagBlocksLowerTriangular" | custom-call | tf_op jit(solution)/shard_map/jit(_solve_triangular)/triangular_solve | solution.py:91
  (146 shorter events, 141.1 us)
Async XLA Ops:
  0.6 1.6 copy-start
  8.5 110.2 %all-to-all-start = ((bf16[128,16,1024]{2,1,0:T(8,128)(2,1)}), bf16[128,16,1024]{2,1,0:T(8,128)(2,1)}, u32[]{:S(2)}, u32[]{:S(2)}) async-start(bf16[128,16,1024]{2,1,0:T(8,128)(2,1)} %bitcast.96), calls=%async_computation | async-start | bytes 8388608 | tf_op jit(solution)/shard_map/all_to_all | solution.py:109
  118.7 10.7 %collective-permute-start = (bf16[2048,1024]{1,0:T(8,128)(2,1)}, bf16[2048,1024]{1,0:T(8,128)(2,1)S(1)}, u32[]{:S(2)}, u32[]{:S(2)}) collective-permute-start(bf16[2048,1024]{1,0:T(8,128)(2,1)} %bitcast.3), channel_id=1, source_target_pairs={{0,1},{1,0},{2,3},{3,2},{4,5},{5,4},{6,7},{7,6},{8,9},{9,8},{10,11... | collective-permute-start | bytes 12582920 | tf_op jit(solution)/shard_map/ppermute | solution.py:112
  140.1 1.9 copy-start.3
  345.3 2.8 copy-start.7
  348.0 7.2 %copy-start.2 = (f32[1024,1024]{1,0:T(8,128)}, f32[1024,1024]{1,0:T(8,128)S(1)}, u32[]{:S(2)}) copy-start(f32[1024,1024]{1,0:T(8,128)S(1)} %select_select_fusion) | copy-start | bytes 12582916
  361.6 1.9 copy-start.4
  362.7 22.2 %collective-permute-start.4 = (f32[64,28,128]{2,0,1:T(8,128)}, f32[64,28,128]{2,0,1:T(8,128)}, u32[]{:S(2)}, u32[]{:S(2)}) collective-permute-start(f32[64,28,128]{2,0,1:T(8,128)} %get-tuple-element.14), channel_id=1, source_target_pairs={{0,8},{2,10},{4,12},{6,14},{8,0},{10,2},{12,4},{14,6},{16,24},{18,... | collective-permute-start | bytes 2752520 | tf_op jit(solution)/shard_map/ppermute | solution.py:35
  369.6 21.8 %collective-permute-start.1 = (f32[64,28,128]{2,0,1:T(8,128)}, f32[64,28,128]{2,0,1:T(8,128)S(1)}, u32[]{:S(2)}, u32[]{:S(2)}) collective-permute-start(f32[64,28,128]{2,0,1:T(8,128)} %get-tuple-element.16), channel_id=1, source_target_pairs={{0,2},{2,0},{4,6},{6,4},{8,10},{10,8},{12,14},{14,12},{16,18},{18,... | collective-permute-start | bytes 2752520 | tf_op jit(solution)/shard_map/ppermute | solution.py:35
  369.9 22.4 %copy-start.5 = (f32[64,28,128]{2,0,1:T(8,128)S(1)}, f32[64,28,128]{2,0,1:T(8,128)}, u32[]{:S(2)}) copy-start(f32[64,28,128]{2,0,1:T(8,128)} %get-tuple-element.17) | copy-start | bytes 2752516
  388.0 12.8 %collective-permute-start.5 = (f32[32,28,128]{2,1,0:T(8,128)}, f32[32,28,128]{2,1,0:T(8,128)S(1)}, u32[]{:S(2)}, u32[]{:S(2)}) collective-permute-start(f32[32,28,128]{2,1,0:T(8,128)} %constant_dynamic-slice_fusion.4), channel_id=1, source_target_pairs={{0,32},{2,34},{4,36},{6,38},{8,40},{10,42},{12,44},{14,46},{16,48}... | collective-permute-start | bytes 1376264 | tf_op jit(solution)/shard_map/ppermute | solution.py:35
  391.4 0.9 copy-start.6
  395.4 12.5 %collective-permute-start.2 = (f32[32,28,128]{2,1,0:T(8,128)}, f32[32,28,128]{2,1,0:T(8,128)S(1)}, u32[]{:S(2)}, u32[]{:S(2)}) collective-permute-start(f32[32,28,128]{2,1,0:T(8,128)} %constant_dynamic-slice_fusion.8), channel_id=1, source_target_pairs={{0,8},{2,10},{4,12},{6,14},{8,0},{10,2},{12,4},{14,6},{16,24},{18,... | collective-permute-start | bytes 1376264 | tf_op jit(solution)/shard_map/ppermute | solution.py:35
  400.9 8.6 %collective-permute-start.6 = (f32[16,28,128]{2,1,0:T(8,128)S(1)}, f32[16,28,128]{2,1,0:T(8,128)S(1)}, u32[]{:S(2)}, u32[]{:S(2)}) collective-permute-start(f32[16,28,128]{2,1,0:T(8,128)S(1)} %constant_dynamic-slice_fusion.3), channel_id=1, source_target_pairs={{0,2},{2,0},{4,6},{6,4},{8,10},{10,8},{12,14},{14,12},{16,18},{18,... | collective-permute-start | bytes 688136 | tf_op jit(solution)/shard_map/ppermute | solution.py:35
  408.1 6.0 %collective-permute-start.3 = (f32[16,28,128]{2,1,0:T(8,128)S(1)}, f32[16,28,128]{2,1,0:T(8,128)S(1)}, u32[]{:S(2)}, u32[]{:S(2)}) collective-permute-start(f32[16,28,128]{2,1,0:T(8,128)S(1)} %constant_dynamic-slice_fusion.7), channel_id=1, source_target_pairs={{0,32},{2,34},{4,36},{6,38},{8,40},{10,42},{12,44},{14,46},{16,48}... | collective-permute-start | bytes 688136 | tf_op jit(solution)/shard_map/ppermute | solution.py:35
  414.1 6.8 %collective-permute-start.7 = (f32[8,28,256]{2,1,0:T(8,128)S(1)}, f32[8,28,256]{2,1,0:T(8,128)S(1)}, u32[]{:S(2)}, u32[]{:S(2)}) collective-permute-start(f32[8,28,256]{2,1,0:T(8,128)S(1)} %fusion.26), channel_id=1, source_target_pairs={{0,4},{2,6},{4,0},{6,2},{8,12},{10,14},{12,8},{14,10},{16,20},{18,... | collective-permute-start | bytes 688136 | tf_op jit(solution)/shard_map/ppermute | solution.py:35
  421.0 5.6 %collective-permute-start.8 = (f32[4,28,256]{2,1,0:T(8,128)S(1)}, f32[4,28,256]{2,1,0:T(8,128)S(1)}, u32[]{:S(2)}, u32[]{:S(2)}) collective-permute-start(f32[4,28,256]{2,1,0:T(8,128)S(1)} %constant_dynamic-slice_fusion.2), channel_id=1, source_target_pairs={{0,16},{2,18},{4,20},{6,22},{8,24},{10,26},{12,28},{14,30},{16,0},... | collective-permute-start | bytes 344072 | tf_op jit(solution)/shard_map/ppermute | solution.py:35
  426.6 4.4 collective-permute-start.9
  431.1 6.8 %collective-permute-start.10 = (f32[1,28,256]{2,1,0:T(8,128)S(1)}, f32[1,28,256]{2,1,0:T(8,128)S(1)}, u32[]{:S(2)}, u32[]{:S(2)}) collective-permute-start(f32[1,28,256]{2,1,0:T(8,128)S(1)} %constant_dynamic-slice_fusion), channel_id=1, source_target_pairs={{0,128},{2,130},{4,132},{6,134},{8,136},{10,138},{12,140},{14,142}... | collective-permute-start | bytes 86024 | tf_op jit(solution)/shard_map/ppermute | solution.py:35
  438.7 5.6 %collective-permute-start.11 = (f32[384,128]{1,0:T(8,128)S(1)}, f32[384,128]{1,0:T(8,128)S(1)}, u32[]{:S(2)}, u32[]{:S(2)}) collective-permute-start(f32[384,128]{1,0:T(8,128)S(1)} %pad_maximum_fusion), channel_id=1, source_target_pairs={{0,2},{2,0},{4,6},{6,4},{8,10},{10,8},{12,14},{14,12},{16,18},{18,... | collective-permute-start | bytes 589832 | tf_op jit(solution)/shard_map/ppermute | solution.py:54
  444.4 4.9 collective-permute-start.12
  449.3 4.6 collective-permute-start.13
  454.0 6.1 %collective-permute-start.14 = (f32[384,128]{1,0:T(8,128)S(1)}, f32[384,128]{1,0:T(8,128)S(1)}, u32[]{:S(2)}, u32[]{:S(2)}) collective-permute-start(f32[384,128]{1,0:T(8,128)S(1)} %add.247), channel_id=1, source_target_pairs={{0,4},{2,6},{4,0},{6,2},{8,12},{10,14},{12,8},{14,10},{16,20},{18,... | collective-permute-start | bytes 589832 | tf_op jit(solution)/shard_map/ppermute | solution.py:54
  460.1 91.2 %copy-start.1 = (bf16[128,8,1024]{2,1,0:T(8,128)(2,1)S(1)}, bf16[128,8,1024]{2,1,0:T(8,128)(2,1)}, u32[]{:S(2)}) copy-start(bf16[128,8,1024]{2,1,0:T(8,128)(2,1)} %param.8) | copy-start | bytes 6291460
  460.1 6.1 %collective-permute-start.15 = (f32[384,128]{1,0:T(8,128)S(1)}, f32[384,128]{1,0:T(8,128)S(1)}, u32[]{:S(2)}, u32[]{:S(2)}) collective-permute-start(f32[384,128]{1,0:T(8,128)S(1)} %add.248), channel_id=1, source_target_pairs={{0,16},{2,18},{4,20},{6,22},{8,24},{10,26},{12,28},{14,30},{16,0},... | collective-permute-start | bytes 589832 | tf_op jit(solution)/shard_map/ppermute | solution.py:54
  466.2 7.6 %collective-permute-start.16 = (f32[384,128]{1,0:T(8,128)S(1)}, f32[384,128]{1,0:T(8,128)S(1)}, u32[]{:S(2)}, u32[]{:S(2)}) collective-permute-start(f32[384,128]{1,0:T(8,128)S(1)} %add.249), channel_id=1, source_target_pairs={{0,64},{2,66},{4,68},{6,70},{8,72},{10,74},{12,76},{14,78},{16,80}... | collective-permute-start | bytes 589832 | tf_op jit(solution)/shard_map/ppermute | solution.py:54
  473.9 10.7 %collective-permute-start.17 = (f32[384,128]{1,0:T(8,128)S(1)}, f32[384,128]{1,0:T(8,128)S(1)}, u32[]{:S(2)}, u32[]{:S(2)}) collective-permute-start(f32[384,128]{1,0:T(8,128)S(1)} %add.250), channel_id=1, source_target_pairs={{0,128},{2,130},{4,132},{6,134},{8,136},{10,138},{12,140},{14,142}... | collective-permute-start | bytes 589832 | tf_op jit(solution)/shard_map/ppermute | solution.py:54
  484.6 18.4 %collective-permute-start.18 = (f32[384,128]{1,0:T(8,128)S(1)}, f32[384,128]{1,0:T(8,128)S(1)}, u32[]{:S(2)}, u32[]{:S(2)}) collective-permute-start(f32[384,128]{1,0:T(8,128)S(1)} %add.251), channel_id=1, source_target_pairs={{0,1},{1,0},{2,3},{3,2},{4,5},{5,4},{6,7},{7,6},{8,9},{9,8},{10,11... | collective-permute-start | bytes 589832 | tf_op jit(solution)/shard_map/ppermute | solution.py:55

commit v8 on v6

--- a/solution.py
+++ b/solution.py
@@ -103,7 +103,17 @@
         n_exp * capacity, hid_width
     )
     partner = lax.ppermute(received, "dp", [(0, 1), (1, 0)])
-    gram_mat = (contract(received, received) + contract(partner, partner)) / n_slot
+    half_w = hid_width // 2
+
+    def block(i, j):
+        ri = slice(i * half_w, (i + 1) * half_w)
+        rj = slice(j * half_w, (j + 1) * half_w)
+        return contract(received[:, ri], received[:, rj]) + contract(partner[:, ri], partner[:, rj])
+
+    g11, g21, g22 = block(0, 0), block(1, 0), block(1, 1)
+    gram_mat = jnp.concatenate(
+        [jnp.concatenate([g11, g21.T], axis=1), jnp.concatenate([g21, g22], axis=1)], axis=0
+    ) / n_slot
     on_diag = lax.broadcasted_iota(jnp.int32, gram_mat.shape, 0) == lax.broadcasted_iota(
         jnp.int32, gram_mat.shape, 1
     )

time: 557 us -> 566 us (1.016)
  blocking collectives: 0 us -> 110 us
  waiting for transfers between devices: 167 us -> 71.7 us
  starting transfers between devices: 68.1 us -> 48.8 us
  matrix products: 54.3 us -> 60.2 us
    all_to_all x0 -> x1, blocking collectives: none -> 110 us  [local(): lax.all_to_all(outgoing, 'expert', split_axis=0, concat_axis=0, tiled=True)]
    all_to_all x1 -> x0, waiting for transfers between devices: 93.3 us -> none  [local(): lax.all_to_all(outgoing, 'expert', split_axis=0, concat_axis=0, tiled=True)]
    all_to_all x1 -> x0, starting transfers between devices: 16.9 us -> none  [local(): lax.all_to_all(outgoing, 'expert', split_axis=0, concat_axis=0, tiled=True)]
    dot_general x4 -> x8, matrix products: 26.4 us -> 32.5 us  [contract(): lax.dot_general(left, right, (((0,), (0,)), ((), ())), preferred_element_...]
  transfers between devices with their start and end apart: 24 -> 23, of which waited for: 18 -> 18; matrix products, arithmetic and copies ran while one was open for 4% -> 5% of each run, Pallas kernels for 0% -> 0%
where the time goes in v8:
time: 566 us; the launch traced here: 558 us
  other arithmetic  231 us (41%)
  blocking collectives  110 us (19%)
  waiting for transfers between devices  71.7 us (13%)
  matrix products  60.2 us (11%)
  starting transfers between devices  48.8 us (9%)
  local copies, waits for them, and re-layouts  28.9 us (5%)
  between operations  7.39 us (1%)
    another operation x30, other arithmetic, local(): whitening = jnp.linalg.cholesky(damped, symmetrize_input=False)  173 us
    all_to_all x1, blocking collectives, local(): lax.all_to_all(outgoing, 'expert', split_axis=0, concat_axis=0, tiled=True)  110 us
    ppermute x14, waiting for transfers between devices, scatter_sum(): part = keep + lax.ppermute(send, 'expert', xor_pairs(n_exp, 1 << b))  36.2 us
    ppermute x7, waiting for transfers between devices, all_sum(): x = x + lax.ppermute(x, 'expert', xor_pairs(n_exp, 1 << b))  35.5 us
    dot_general x8, matrix products, contract(): lax.dot_general(left, right, (((0,), (0,)), ((), ())), preferred_element_...  32.5 us
    another operation x14, matrix products, local(): whitening = jnp.linalg.cholesky(damped, symmetrize_input=False)  23.1 us
    ppermute x14, starting transfers between devices, scatter_sum(): part = keep + lax.ppermute(send, 'expert', xor_pairs(n_exp, 1 << b))  21.1 us
    ppermute x1, starting transfers between devices, all_sum(): return x + lax.ppermute(x, 'dp', [(0, 1), (1, 0)])  16 us
  transfers between devices with their start and end apart: 23, of which 18 were waited for; matrix products, arithmetic and copies ran while one was open for 5% of the time, Pallas kernels for 0%

profile of v8, /device:TPU:1, one launch (start us, length us, event | category | flops | bytes accessed | tf_op | source)
XLA Modules:
  0.0 558.3 jit_solution(7776696252263733302)
XLA Ops:
  2.3 4.9 fusion.4
  7.2 110.0 %all_to_all.5 = bf16[128,16,1024]{2,1,0:T(8,128)(2,1)} all-to-all(bf16[128,16,1024]{2,1,0:T(8,128)(2,1)S(1)} %bitcast.103), channel_id=1, replica_groups=mesh['expert'=128,'dp'=2] {'expert'}, dimensions={0} | all-to-all | bytes 8388608 | tf_op jit(solution)/shard_map/all_to_all | solution.py:102
  120.3 4.6 fusion.10
  152.4 11.7 %cholesky.242 = f32[128,128]{1,0:T(8,128)S(1)} custom-call(f32[128,128]{1,0:T(8,128)S(1)} %cholesky.654), custom_call_target="Cholesky" | custom-call | tf_op jit(solution)/shard_map/jit(cholesky)/cholesky | solution.py:122
  166.7 9.8 %custom-call.64 = f32[1,128,128]{1,2,0:T(8,128)S(1)} custom-call(f32[1,128,128]{2,1,0:T(8,128)S(1)} %get-tuple-element.31), custom_call_target="InvertDiagBlocksLowerTriangular" | custom-call | tf_op jit(solution)/shard_map/jit(cholesky)/cholesky | solution.py:122
  180.4 12.1 %cholesky.265 = f32[128,128]{1,0:T(8,128)S(1)} custom-call(f32[128,128]{1,0:T(8,128)S(1)} %cholesky.658), custom_call_target="Cholesky" | custom-call | tf_op jit(solution)/shard_map/jit(cholesky)/cholesky | solution.py:122
  193.2 9.8 %custom-call.65 = f32[1,128,128]{1,2,0:T(8,128)S(1)} custom-call(f32[1,128,128]{2,1,0:T(8,128)S(1)} %get-tuple-element.28), custom_call_target="InvertDiagBlocksLowerTriangular" | custom-call | tf_op jit(solution)/shard_map/jit(cholesky)/cholesky | solution.py:122
  206.4 11.7 %cholesky.506 = f32[128,128]{1,0:T(8,128)S(1)} custom-call(f32[128,128]{1,0:T(8,128)S(1)} %cholesky.663), custom_call_target="Cholesky" | custom-call | tf_op jit(solution)/shard_map/jit(cholesky)/cholesky | solution.py:122
  218.7 9.8 %custom-call.66 = f32[1,128,128]{1,2,0:T(8,128)S(1)} custom-call(f32[1,128,128]{2,1,0:T(8,128)S(1)} %get-tuple-element.25), custom_call_target="InvertDiagBlocksLowerTriangular" | custom-call | tf_op jit(solution)/shard_map/jit(cholesky)/cholesky | solution.py:122
  232.0 11.9 %cholesky.525 = f32[128,128]{1,0:T(8,128)S(1)} custom-call(f32[128,128]{1,0:T(8,128)S(1)} %cholesky.668), custom_call_target="Cholesky" | custom-call | tf_op jit(solution)/shard_map/jit(cholesky)/cholesky | solution.py:122
  244.5 9.8 %custom-call.67 = f32[1,128,128]{1,2,0:T(8,128)S(1)} custom-call(f32[1,128,128]{2,1,0:T(8,128)S(1)} %get-tuple-element.22), custom_call_target="InvertDiagBlocksLowerTriangular" | custom-call | tf_op jit(solution)/shard_map/jit(cholesky)/cholesky | solution.py:122
  257.8 11.7 %cholesky.544 = f32[128,128]{1,0:T(8,128)S(1)} custom-call(f32[128,128]{1,0:T(8,128)S(1)} %cholesky.673), custom_call_target="Cholesky" | custom-call | tf_op jit(solution)/shard_map/jit(cholesky)/cholesky | solution.py:122
  270.2 10.0 %custom-call.68 = f32[1,128,128]{1,2,0:T(8,128)S(1)} custom-call(f32[1,128,128]{2,1,0:T(8,128)S(1)} %get-tuple-element.19), custom_call_target="InvertDiagBlocksLowerTriangular" | custom-call | tf_op jit(solution)/shard_map/jit(cholesky)/cholesky | solution.py:122
  283.5 11.7 %cholesky.564 = f32[128,128]{1,0:T(8,128)S(1)} custom-call(f32[128,128]{1,0:T(8,128)S(1)} %cholesky.678), custom_call_target="Cholesky" | custom-call | tf_op jit(solution)/shard_map/jit(cholesky)/cholesky | solution.py:122
  295.8 9.8 %custom-call.69 = f32[1,128,128]{1,2,0:T(8,128)S(1)} custom-call(f32[1,128,128]{2,1,0:T(8,128)S(1)} %get-tuple-element.16), custom_call_target="InvertDiagBlocksLowerTriangular" | custom-call | tf_op jit(solution)/shard_map/jit(cholesky)/cholesky | solution.py:122
  308.6 12.1 %cholesky.584 = f32[128,128]{1,0:T(8,128)S(1)} custom-call(f32[128,128]{1,0:T(8,128)S(1)} %cholesky.683), custom_call_target="Cholesky" | custom-call | tf_op jit(solution)/shard_map/jit(cholesky)/cholesky | solution.py:122
  321.4 9.8 %custom-call.70 = f32[1,128,128]{1,2,0:T(8,128)S(1)} custom-call(f32[1,128,128]{2,1,0:T(8,128)S(1)} %get-tuple-element.13), custom_call_target="InvertDiagBlocksLowerTriangular" | custom-call | tf_op jit(solution)/shard_map/jit(cholesky)/cholesky | solution.py:122
  333.9 11.7 %cholesky.602 = f32[128,128]{1,0:T(8,128)S(1)} custom-call(f32[128,128]{1,0:T(8,128)S(1)} %slice_subtract_fusion.7), custom_call_target="Cholesky" | custom-call | tf_op jit(solution)/shard_map/jit(cholesky)/cholesky | solution.py:122
  360.7 5.2 fusion.1
  382.7 13.0 %collective-permute-done.8 = f32[64,28,128]{2,0,1:T(8,128)} collective-permute-done((f32[64,28,128]{2,0,1:T(8,128)S(1)}, f32[64,28,128]{2,0,1:T(8,128)}, u32[]{:S(2)}, u32[]{:S(2)}) %collective-permute-start.8) | collective-permute-done | bytes 917536 | tf_op jit(solution)/shard_map/ppermute | solution.py:39
  398.4 5.9 %collective-permute-done.1 = f32[64,28,128]{2,0,1:T(8,128)} collective-permute-done((f32[64,28,128]{2,0,1:T(8,128)}, f32[64,28,128]{2,0,1:T(8,128)}, u32[]{:S(2)}, u32[]{:S(2)}) %collective-permute-start.1) | collective-permute-done | bytes 917536 | tf_op jit(solution)/shard_map/ppermute | solution.py:39
  410.6 6.9 %collective-permute-done.2 = f32[32,28,128]{2,0,1:T(8,128)S(1)} collective-permute-done((f32[32,28,128]{2,0,1:T(8,128)S(1)}, f32[32,28,128]{2,0,1:T(8,128)S(1)}, u32[]{:S(2)}, u32[]{:S(2)}) %collective-permute-start.2) | collective-permute-done | bytes 458784 | tf_op jit(solution)/shard_map/ppermute | solution.py:39
  446.7 4.4 collective-permute-done.15
  451.9 4.2 collective-permute-done.16
  468.5 4.5 collective-permute-done.19
  474.3 6.3 %collective-permute-done.20 = f32[384,128]{1,0:T(8,128)S(1)} collective-permute-done((f32[384,128]{1,0:T(8,128)S(1)}, f32[384,128]{1,0:T(8,128)S(1)}, u32[]{:S(2)}, u32[]{:S(2)}) %collective-permute-start.20) | collective-permute-done | bytes 196640 | tf_op jit(solution)/shard_map/ppermute | solution.py:47
  482.6 8.0 %collective-permute-done.21 = f32[384,128]{1,0:T(8,128)S(1)} collective-permute-done((f32[384,128]{1,0:T(8,128)S(1)}, f32[384,128]{1,0:T(8,128)S(1)}, u32[]{:S(2)}, u32[]{:S(2)}) %collective-permute-start.21) | collective-permute-done | bytes 196640 | tf_op jit(solution)/shard_map/ppermute | solution.py:47
  490.6 16.0 %collective-permute-start.22 = (f32[384,128]{1,0:T(8,128)S(1)}, f32[384,128]{1,0:T(8,128)S(1)}, u32[]{:S(2)}, u32[]{:S(2)}) collective-permute-start(f32[384,128]{1,0:T(8,128)S(1)} %add.306), channel_id=1, source_target_pairs={{0,1},{1,0},{2,3},{3,2},{4,5},{5,4},{6,7},{7,6},{8,9},{9,8},{10,11... | collective-permute-start | bytes 589832 | tf_op jit(solution)/shard_map/ppermute | solution.py:48
  509.7 11.7 %cholesky.634 = f32[128,128]{1,0:T(8,128)S(1)} custom-call(f32[128,128]{1,0:T(8,128)S(1)} %slice.235), custom_call_target="Cholesky" | custom-call | tf_op jit(solution)/shard_map/jit(cholesky)/cholesky | solution.py:80
  522.8 9.8 %custom-call.72 = f32[1,128,128]{1,2,0:T(8,128)S(1)} custom-call(f32[1,128,128]{2,1,0:T(8,128)S(1)} %fusion.68), custom_call_target="InvertDiagBlocksLowerTriangular" | custom-call | tf_op jit(solution)/shard_map/jit(_solve_triangular)/triangular_solve | solution.py:81
  533.9 11.7 %cholesky.645 = f32[128,128]{1,0:T(8,128)S(1)} custom-call(f32[128,128]{1,0:T(8,128)S(1)} %slice_subtract_fusion.6), custom_call_target="Cholesky" | custom-call | tf_op jit(solution)/shard_map/jit(cholesky)/cholesky | solution.py:83
  547.0 9.8 %custom-call.73 = f32[1,128,128]{1,2,0:T(8,128)S(1)} custom-call(f32[1,128,128]{2,1,0:T(8,128)S(1)} %fusion.69), custom_call_target="InvertDiagBlocksLowerTriangular" | custom-call | tf_op jit(solution)/shard_map/jit(_solve_triangular)/triangular_solve | solution.py:84
  (172 shorter events, 150.6 us)
Async XLA Ops:
  0.6 1.6 copy-start
  117.2 14.7 %collective-permute-start = (bf16[2048,1024]{1,0:T(8,128)(2,1)}, bf16[2048,1024]{1,0:T(8,128)(2,1)}, u32[]{:S(2)}, u32[]{:S(2)}) collective-permute-start(bf16[2048,1024]{1,0:T(8,128)(2,1)} %bitcast.2), channel_id=1, source_target_pairs={{0,1},{1,0},{2,3},{3,2},{4,5},{5,4},{6,7},{7,6},{8,9},{9,8},{10,11... | collective-permute-start | bytes 12582920 | tf_op jit(solution)/shard_map/ppermute | solution.py:105
  146.4 1.0 copy-start.7
  150.5 1.9 copy-start.3
  355.9 2.8 copy-start.9
  358.7 7.2 %copy-start.2 = (f32[1024,1024]{1,0:T(8,128)}, f32[1024,1024]{1,0:T(8,128)S(1)}, u32[]{:S(2)}) copy-start(f32[1024,1024]{1,0:T(8,128)S(1)} %select_select_fusion) | copy-start | bytes 12582916
  372.2 1.3 copy-start.4
  373.5 22.1 %collective-permute-start.8 = (f32[64,28,128]{2,0,1:T(8,128)S(1)}, f32[64,28,128]{2,0,1:T(8,128)}, u32[]{:S(2)}, u32[]{:S(2)}) collective-permute-start(f32[64,28,128]{2,0,1:T(8,128)S(1)} %constant_dynamic-slice_fusion.6), channel_id=1, source_target_pairs={{0,8},{2,10},{4,12},{6,14},{8,0},{10,2},{12,4},{14,6},{16,24},{18,... | collective-permute-start | bytes 2752520 | tf_op jit(solution)/shard_map/ppermute | solution.py:39
  380.1 1.2 copy-start.5
  382.4 21.9 %copy-start.6 = (f32[2,2,2,2,2,2,2,28,128]{8,6,5,4,3,2,1,0,7:T(2,128)S(1)}, f32[2,2,2,2,2,2,2,28,128]{8,6,5,4,3,2,1,0,7:T(2,128)}, u32[]{:S(2)}) copy-start(f32[2,2,2,2,2,2,2,28,128]{8,6,5,4,3,2,1,0,7:T(2,128)} %copy-done.5) | copy-start | bytes 5505028
  382.4 21.9 %collective-permute-start.1 = (f32[64,28,128]{2,0,1:T(8,128)}, f32[64,28,128]{2,0,1:T(8,128)}, u32[]{:S(2)}, u32[]{:S(2)}) collective-permute-start(f32[64,28,128]{2,0,1:T(8,128)} %constant_dynamic-slice_fusion.13), channel_id=1, source_target_pairs={{0,2},{2,0},{4,6},{6,4},{8,10},{10,8},{12,14},{14,12},{16,18},{18,... | collective-permute-start | bytes 2752520 | tf_op jit(solution)/shard_map/ppermute | solution.py:39
  397.2 11.4 %collective-permute-start.9 = (f32[32,28,128]{2,0,1:T(8,128)S(1)}, f32[32,28,128]{2,0,1:T(8,128)}, u32[]{:S(2)}, u32[]{:S(2)}) collective-permute-start(f32[32,28,128]{2,0,1:T(8,128)S(1)} %constant_dynamic-slice_fusion.5), channel_id=1, source_target_pairs={{0,32},{2,34},{4,36},{6,38},{8,40},{10,42},{12,44},{14,46},{16,48}... | collective-permute-start | bytes 1376264 | tf_op jit(solution)/shard_map/ppermute | solution.py:39
  406.6 11.0 %collective-permute-start.2 = (f32[32,28,128]{2,0,1:T(8,128)S(1)}, f32[32,28,128]{2,0,1:T(8,128)S(1)}, u32[]{:S(2)}, u32[]{:S(2)}) collective-permute-start(f32[32,28,128]{2,0,1:T(8,128)S(1)} %constant_dynamic-slice_fusion.12), channel_id=1, source_target_pairs={{0,8},{2,10},{4,12},{6,14},{8,0},{10,2},{12,4},{14,6},{16,24},{18,... | collective-permute-start | bytes 1376264 | tf_op jit(solution)/shard_map/ppermute | solution.py:39
  409.8 10.4 %collective-permute-start.10 = (f32[16,28,128]{2,0,1:T(8,128)S(1)}, f32[16,28,128]{2,0,1:T(8,128)S(1)}, u32[]{:S(2)}, u32[]{:S(2)}) collective-permute-start(f32[16,28,128]{2,0,1:T(8,128)S(1)} %constant_dynamic-slice_fusion.4), channel_id=1, source_target_pairs={{0,2},{2,0},{4,6},{6,4},{8,10},{10,8},{12,14},{14,12},{16,18},{18,... | collective-permute-start | bytes 688136 | tf_op jit(solution)/shard_map/ppermute | solution.py:39
  418.7 5.0 collective-permute-start.3
  420.2 6.4 %collective-permute-start.11 = (f32[8,28,128]{2,0,1:T(8,128)S(1)}, f32[8,28,128]{2,0,1:T(8,128)S(1)}, u32[]{:S(2)}, u32[]{:S(2)}) collective-permute-start(f32[8,28,128]{2,0,1:T(8,128)S(1)} %constant_dynamic-slice_fusion.3), channel_id=1, source_target_pairs={{0,16},{2,18},{4,20},{6,22},{8,24},{10,26},{12,28},{14,30},{16,0},... | collective-permute-start | bytes 344072 | tf_op jit(solution)/shard_map/ppermute | solution.py:39
  423.7 5.2 collective-permute-start.4
  426.6 4.6 collective-permute-start.12
  429.0 4.6 collective-permute-start.5
  431.3 4.3 collective-permute-start.13
  433.7 5.3 collective-permute-start.6
  435.7 6.6 %collective-permute-start.14 = (f32[1,28,128]{2,0,1:T(1,128)S(1)}, f32[1,28,128]{2,0,1:T(1,128)S(1)}, u32[]{:S(2)}, u32[]{:S(2)}) collective-permute-start(f32[1,28,128]{2,0,1:T(1,128)S(1)} %constant_dynamic-slice_fusion), channel_id=1, source_target_pairs={{0,128},{2,130},{4,132},{6,134},{8,136},{10,138},{12,140},{14,142}... | collective-permute-start | bytes 43016 | tf_op jit(solution)/shard_map/ppermute | solution.py:39
  439.0 6.6 %collective-permute-start.7 = (f32[1,28,128]{2,0,1:T(1,128)S(1)}, f32[1,28,128]{2,0,1:T(1,128)S(1)}, u32[]{:S(2)}, u32[]{:S(2)}) collective-permute-start(f32[1,28,128]{2,0,1:T(1,128)S(1)} %constant_dynamic-slice_fusion.7), channel_id=1, source_target_pairs={{0,128},{2,130},{4,132},{6,134},{8,136},{10,138},{12,140},{14,142}... | collective-permute-start | bytes 43016 | tf_op jit(solution)/shard_map/ppermute | solution.py:39
  446.3 4.9 collective-permute-start.15
  451.2 4.9 collective-permute-start.16
  456.1 4.6 collective-permute-start.17
  460.7 6.1 %collective-permute-start.18 = (f32[384,128]{1,0:T(8,128)S(1)}, f32[384,128]{1,0:T(8,128)S(1)}, u32[]{:S(2)}, u32[]{:S(2)}) collective-permute-start(f32[384,128]{1,0:T(8,128)S(1)} %add.302), channel_id=1, source_target_pairs={{0,4},{2,6},{4,0},{6,2},{8,12},{10,14},{12,8},{14,10},{16,20},{18,... | collective-permute-start | bytes 589832 | tf_op jit(solution)/shard_map/ppermute | solution.py:47
  466.9 91.1 %copy-start.1 = (bf16[128,8,1024]{2,1,0:T(8,128)(2,1)S(1)}, bf16[128,8,1024]{2,1,0:T(8,128)(2,1)}, u32[]{:S(2)}) copy-start(bf16[128,8,1024]{2,1,0:T(8,128)(2,1)} %param.8) | copy-start | bytes 6291460
  466.9 6.1 %collective-permute-start.19 = (f32[384,128]{1,0:T(8,128)S(1)}, f32[384,128]{1,0:T(8,128)S(1)}, u32[]{:S(2)}, u32[]{:S(2)}) collective-permute-start(f32[384,128]{1,0:T(8,128)S(1)} %add.303), channel_id=1, source_target_pairs={{0,16},{2,18},{4,20},{6,22},{8,24},{10,26},{12,28},{14,30},{16,0},... | collective-permute-start | bytes 589832 | tf_op jit(solution)/shard_map/ppermute | solution.py:47
  473.0 7.6 %collective-permute-start.20 = (f32[384,128]{1,0:T(8,128)S(1)}, f32[384,128]{1,0:T(8,128)S(1)}, u32[]{:S(2)}, u32[]{:S(2)}) collective-permute-start(f32[384,128]{1,0:T(8,128)S(1)} %add.304), channel_id=1, source_target_pairs={{0,64},{2,66},{4,68},{6,70},{8,72},{10,74},{12,76},{14,78},{16,80}... | collective-permute-start | bytes 589832 | tf_op jit(solution)/shard_map/ppermute | solution.py:47
  480.7 9.9 %collective-permute-start.21 = (f32[384,128]{1,0:T(8,128)S(1)}, f32[384,128]{1,0:T(8,128)S(1)}, u32[]{:S(2)}, u32[]{:S(2)}) collective-permute-start(f32[384,128]{1,0:T(8,128)S(1)} %add.305), channel_id=1, source_target_pairs={{0,128},{2,130},{4,132},{6,134},{8,136},{10,138},{12,140},{14,142}... | collective-permute-start | bytes 589832 | tf_op jit(solution)/shard_map/ppermute | solution.py:47
  490.6 19.1 %collective-permute-start.22 = (f32[384,128]{1,0:T(8,128)S(1)}, f32[384,128]{1,0:T(8,128)S(1)}, u32[]{:S(2)}, u32[]{:S(2)}) collective-permute-start(f32[384,128]{1,0:T(8,128)S(1)} %add.306), channel_id=1, source_target_pairs={{0,1},{1,0},{2,3},{3,2},{4,5},{5,4},{6,7},{7,6},{8,9},{9,8},{10,11... | collective-permute-start | bytes 589832 | tf_op jit(solution)/shard_map/ppermute | solution.py:48
  (1 other events, 0.9 us)

commit v9 on v6

--- a/solution.py
+++ b/solution.py
@@ -19,16 +19,15 @@
     return [(i, i ^ mask) for i in range(n)]
 
 
-def scatter_sum(term, orders):
-    cols = term.shape[0]
-    n_exp = lax.axis_size("expert")
-    rows = term.shape[1] // n_exp
+def scatter_sum(term, n_cols, n_rows, orders):
+    cols, n_exp = n_cols, lax.axis_size("expert")
+    rows = n_rows // n_exp
     n_bits = n_exp.bit_length() - 1
     me = lax.axis_index("expert")
     width = cols // len(orders)
     outs = []
     for s, order in enumerate(orders):
-        part = term[s * width:(s + 1) * width].reshape([width] + [2] * n_bits + [rows])
+        part = term(s * width, width).reshape([width] + [2] * n_bits + [rows])
         perm = [n_bits - b for b in order] + [n_bits + 1, 0]
         part = part.transpose(perm).reshape(n_exp, rows, width)
         for b in order:
@@ -115,9 +114,11 @@
     ).astype(jnp.bfloat16)
     down_half = down_weight[0]
     half_cols = down_half.shape[1]
-    term = contract(test_mat, down_half)
+    def term(start, width):
+        return contract(test_mat[:, start:start + width], down_half)
+
     orders = bit_orders(n_exp, 2)
-    sketch = scatter_sum(term, orders)
+    sketch = scatter_sum(term, test_mat.shape[1], half_cols, orders)
     small_gram = all_sum(lower_blocks(sketch), orders[0])
     basis_rows = right_solve_chol(small_gram, sketch) * math.sqrt(half_cols * n_dp)
     own_rows = lax.dynamic_slice_in_dim(

time: 557 us -> 553 us (level)
  waiting for transfers between devices: 167 us -> 146 us
  local copies, waits for them, and re-layouts: 24.1 us -> 37.1 us
    all_to_all x1, waiting for transfers between devices: 93.3 us -> 72 us  [local(): lax.all_to_all(outgoing, 'expert', split_axis=0, concat_axis=0, tiled=True)]
    dot_general x0 -> x2, local copies, waits for them, and re-layouts: none -> 21.3 us  [contract(): lax.dot_general(left, right, (((0,), (0,)), ((), ())), preferred_element_...]
    slice x3 -> x0, local copies, waits for them, and re-layouts: 5.91 us -> none  [scatter_sum(): term[s * width:(s + 1) * width].reshape([width] + [2] * n_bits + [rows])]
    dot_general x4 -> x5, matrix products: 26.4 us -> 29.6 us  [contract(): lax.dot_general(left, right, (((0,), (0,)), ((), ())), preferred_element_...]
  transfers between devices with their start and end apart: 24 -> 24, of which waited for: 18 -> 17; matrix products, arithmetic and copies ran while one was open for 4% -> 8% of each run, Pallas kernels for 0% -> 0%
where the time goes in v9:
time: 553 us; the launch traced here: 545 us
  other arithmetic  229 us (41%)
  waiting for transfers between devices  146 us (26%)
  starting transfers between devices  67.7 us (12%)
  matrix products  57.6 us (10%)
  local copies, waits for them, and re-layouts  37.1 us (7%)
  between operations  7.26 us (1%)
    another operation x30, other arithmetic, local(): whitening = jnp.linalg.cholesky(damped, symmetrize_input=False)  172 us
    all_to_all x1, waiting for transfers between devices, local(): lax.all_to_all(outgoing, 'expert', split_axis=0, concat_axis=0, tiled=True)  72 us
    ppermute x14, waiting for transfers between devices, scatter_sum(): part = keep + lax.ppermute(send, 'expert', xor_pairs(n_exp, 1 << b))  37.5 us
    ppermute x7, waiting for transfers between devices, all_sum(): x = x + lax.ppermute(x, 'expert', xor_pairs(n_exp, 1 << b))  36.2 us
    dot_general x5, matrix products, contract(): lax.dot_general(left, right, (((0,), (0,)), ((), ())), preferred_element_...  29.6 us
    ppermute x14, starting transfers between devices, scatter_sum(): part = keep + lax.ppermute(send, 'expert', xor_pairs(n_exp, 1 << b))  24.2 us
    another operation x14, matrix products, local(): whitening = jnp.linalg.cholesky(damped, symmetrize_input=False)  23.3 us
    dot_general x2, local copies, waits for them, and re-layouts, contract(): lax.dot_general(left, right, (((0,), (0,)), ((), ())), preferred_element_...  21.3 us
  transfers between devices with their start and end apart: 24, of which 17 were waited for; matrix products, arithmetic and copies ran while one was open for 8% of the time, Pallas kernels for 0%

profile of v9, /device:TPU:1, one launch (start us, length us, event | category | flops | bytes accessed | tf_op | source)
XLA Modules:
  0.0 544.8 jit_solution(15631475754019229128)
XLA Ops:
  2.3 6.3 %fusion.3 = bf16[2048,1024]{1,0:T(8,128)(2,1)} fusion(s32[1024]{0:T(1024)S(1)} %eq.22, bf16[128,8,1024]{2,1,0:T(8,128)(2,1)S(1)} %copy-done), kind=kOutput, calls=%fused_computation.10 | convolution fusion | flops 4299161600 | bytes 6295552 | tf_op jit(solution)/shard_map/dot_general | solution.py:13
  8.6 16.9 %all-to-all-start = ((bf16[128,16,1024]{2,1,0:T(8,128)(2,1)}), bf16[128,16,1024]{2,1,0:T(8,128)(2,1)}, u32[]{:S(2)}, u32[]{:S(2)}) async-start(bf16[128,16,1024]{2,1,0:T(8,128)(2,1)} %bitcast.118), calls=%async_computation | async-start | bytes 8388608 | tf_op jit(solution)/shard_map/all_to_all | solution.py:101
  25.4 10.4 %copy.30 = bf16[3584,1024]{1,0:T(8,128)(2,1)} copy(bf16[3584,1024]{0,1:T(8,128)(2,1)} %bitcast.114) | data formatting | bytes 14680064 | tf_op jit(solution)/shard_map/dot_general | solution.py:13
  35.8 10.9 %dot_general.51 = bf16[2,2,2,2,2,2,2,28,1024]{8,7,6,5,4,3,2,1,0:T(8,128)(2,1)} reshape(bf16[3584,1024]{1,0:T(8,128)(2,1)} %copy.30) | data formatting | bytes 14680064 | tf_op jit(solution)/shard_map/dot_general | solution.py:13
  46.7 72.0 %all-to-all-done = bf16[128,16,1024]{2,1,0:T(8,128)(2,1)} async-done(((bf16[128,16,1024]{2,1,0:T(8,128)(2,1)}), bf16[128,16,1024]{2,1,0:T(8,128)(2,1)}, u32[]{:S(2)}, u32[]{:S(2)}) %all-to-all-start) | async-done | bytes 4194336 | tf_op jit(solution)/shard_map/all_to_all | solution.py:101
  121.9 7.6 %fusion.73 = f32[1024,1024,1]{1,0,2:T(8,128)S(1)} fusion(bf16[128,16,1024]{2,1,0:T(8,128)(2,1)} %all-to-all-done), kind=kOutput, calls=%fused_computation.163 | convolution fusion | flops 4294967296 | bytes 8388608 | tf_op jit(solution)/shard_map/dot_general | solution.py:13
  129.5 7.4 %select_reduce_fusion = (f32[]{:T(128)}, f32[1024,1024]{1,0:T(8,128)}) fusion(bf16[2048,1024]{1,0:T(8,128)(2,1)S(1)} %collective-permute-done, f32[1024,1024,1]{1,0,2:T(8,128)S(1)} %fusion.73), kind=kOutput, calls=%fused_computation.6 | convolution fusion | flops 4300210176 | bytes 12582916 | tf_op jit(solution)/shard_map/dot_general | solution.py:13
  142.1 11.7 %cholesky.242 = f32[128,128]{1,0:T(8,128)S(1)} custom-call(f32[128,128]{1,0:T(8,128)S(1)} %cholesky.654), custom_call_target="Cholesky" | custom-call | tf_op jit(solution)/shard_map/jit(cholesky)/cholesky | solution.py:111
  153.8 9.8 %custom-call.64 = f32[1,128,128]{1,2,0:T(8,128)S(1)} custom-call(f32[1,128,128]{2,1,0:T(8,128)S(1)} %get-tuple-element.35), custom_call_target="InvertDiagBlocksLowerTriangular" | custom-call | tf_op jit(solution)/shard_map/jit(cholesky)/cholesky | solution.py:111
  170.1 11.7 %cholesky.265 = f32[128,128]{1,0:T(8,128)S(1)} custom-call(f32[128,128]{1,0:T(8,128)S(1)} %cholesky.658), custom_call_target="Cholesky" | custom-call | tf_op jit(solution)/shard_map/jit(cholesky)/cholesky | solution.py:111
  182.5 10.2 %custom-call.65 = f32[1,128,128]{1,2,0:T(8,128)S(1)} custom-call(f32[1,128,128]{2,1,0:T(8,128)S(1)} %get-tuple-element.32), custom_call_target="InvertDiagBlocksLowerTriangular" | custom-call | tf_op jit(solution)/shard_map/jit(cholesky)/cholesky | solution.py:111
  196.0 11.7 %cholesky.506 = f32[128,128]{1,0:T(8,128)S(1)} custom-call(f32[128,128]{1,0:T(8,128)S(1)} %cholesky.663), custom_call_target="Cholesky" | custom-call | tf_op jit(solution)/shard_map/jit(cholesky)/cholesky | solution.py:111
  209.0 9.8 %custom-call.66 = f32[1,128,128]{1,2,0:T(8,128)S(1)} custom-call(f32[1,128,128]{2,1,0:T(8,128)S(1)} %get-tuple-element.29), custom_call_target="InvertDiagBlocksLowerTriangular" | custom-call | tf_op jit(solution)/shard_map/jit(cholesky)/cholesky | solution.py:111
  222.4 11.9 %cholesky.525 = f32[128,128]{1,0:T(8,128)S(1)} custom-call(f32[128,128]{1,0:T(8,128)S(1)} %cholesky.668), custom_call_target="Cholesky" | custom-call | tf_op jit(solution)/shard_map/jit(cholesky)/cholesky | solution.py:111
  235.6 9.8 %custom-call.67 = f32[1,128,128]{1,2,0:T(8,128)S(1)} custom-call(f32[1,128,128]{2,1,0:T(8,128)S(1)} %get-tuple-element.26), custom_call_target="InvertDiagBlocksLowerTriangular" | custom-call | tf_op jit(solution)/shard_map/jit(cholesky)/cholesky | solution.py:111
  248.8 11.7 %cholesky.544 = f32[128,128]{1,0:T(8,128)S(1)} custom-call(f32[128,128]{1,0:T(8,128)S(1)} %cholesky.673), custom_call_target="Cholesky" | custom-call | tf_op jit(solution)/shard_map/jit(cholesky)/cholesky | solution.py:111
  261.9 9.8 %custom-call.68 = f32[1,128,128]{1,2,0:T(8,128)S(1)} custom-call(f32[1,128,128]{2,1,0:T(8,128)S(1)} %get-tuple-element.23), custom_call_target="InvertDiagBlocksLowerTriangular" | custom-call | tf_op jit(solution)/shard_map/jit(cholesky)/cholesky | solution.py:111
  275.3 11.7 %cholesky.564 = f32[128,128]{1,0:T(8,128)S(1)} custom-call(f32[128,128]{1,0:T(8,128)S(1)} %cholesky.678), custom_call_target="Cholesky" | custom-call | tf_op jit(solution)/shard_map/jit(cholesky)/cholesky | solution.py:111
  288.3 9.8 %custom-call.69 = f32[1,128,128]{1,2,0:T(8,128)S(1)} custom-call(f32[1,128,128]{2,1,0:T(8,128)S(1)} %get-tuple-element.20), custom_call_target="InvertDiagBlocksLowerTriangular" | custom-call | tf_op jit(solution)/shard_map/jit(cholesky)/cholesky | solution.py:111
  301.1 11.7 %cholesky.584 = f32[128,128]{1,0:T(8,128)S(1)} custom-call(f32[128,128]{1,0:T(8,128)S(1)} %cholesky.683), custom_call_target="Cholesky" | custom-call | tf_op jit(solution)/shard_map/jit(cholesky)/cholesky | solution.py:111
  314.1 10.2 %custom-call.70 = f32[1,128,128]{1,2,0:T(8,128)S(1)} custom-call(f32[1,128,128]{2,1,0:T(8,128)S(1)} %get-tuple-element.17), custom_call_target="InvertDiagBlocksLowerTriangular" | custom-call | tf_op jit(solution)/shard_map/jit(cholesky)/cholesky | solution.py:111
  326.9 11.7 %cholesky.602 = f32[128,128]{1,0:T(8,128)S(1)} custom-call(f32[128,128]{1,0:T(8,128)S(1)} %slice_subtract_fusion.7), custom_call_target="Cholesky" | custom-call | tf_op jit(solution)/shard_map/jit(cholesky)/cholesky | solution.py:111
  352.3 5.9 %convolution_bitcast_fusion.1 = f32[2,2,2,2,2,2,2,28,128]{8,7,0,3,1,4,2,5,6:T(8,128)S(1)} fusion(bf16[2,2,2,2,2,2,2,28,1024]{8,7,6,5,4,3,2,1,0:T(8,128)(2,1)} %dot_general.51, bf16[1024,256]{1,0:T(8,128)(2,1)S(1)} %convolution_convert_fusion), kind=kOutput, calls=%fused_computation.14 | convolution fusion | flops 939524096 | bytes 9437184 | tf_op jit(solution)/shard_map/dot_general | solution.py:13
  366.4 15.6 %collective-permute-done.1 = f32[64,28,128]{2,0,1:T(8,128)} collective-permute-done((f32[64,28,128]{2,0,1:T(8,128)S(1)}, f32[64,28,128]{2,0,1:T(8,128)}, u32[]{:S(2)}, u32[]{:S(2)}) %collective-permute-start.1) | collective-permute-done | bytes 917536 | tf_op jit(solution)/shard_map/ppermute | solution.py:38
  391.7 5.8 %collective-permute-done.2 = f32[32,28,128]{2,0,1:T(8,128)} collective-permute-done((f32[32,28,128]{2,0,1:T(8,128)S(1)}, f32[32,28,128]{2,0,1:T(8,128)}, u32[]{:S(2)}, u32[]{:S(2)}) %collective-permute-start.2) | collective-permute-done | bytes 458784 | tf_op jit(solution)/shard_map/ppermute | solution.py:38
  460.4 6.8 %collective-permute-done.20 = f32[384,128]{1,0:T(8,128)S(1)} collective-permute-done((f32[384,128]{1,0:T(8,128)S(1)}, f32[384,128]{1,0:T(8,128)S(1)}, u32[]{:S(2)}, u32[]{:S(2)}) %collective-permute-start.20) | collective-permute-done | bytes 196640 | tf_op jit(solution)/shard_map/ppermute | solution.py:46
  469.1 7.8 %collective-permute-done.21 = f32[384,128]{1,0:T(8,128)S(1)} collective-permute-done((f32[384,128]{1,0:T(8,128)S(1)}, f32[384,128]{1,0:T(8,128)S(1)}, u32[]{:S(2)}, u32[]{:S(2)}) %collective-permute-start.21) | collective-permute-done | bytes 196640 | tf_op jit(solution)/shard_map/ppermute | solution.py:46
  476.9 16.1 %collective-permute-start.22 = (f32[384,128]{1,0:T(8,128)S(1)}, f32[384,128]{1,0:T(8,128)S(1)}, u32[]{:S(2)}, u32[]{:S(2)}) collective-permute-start(f32[384,128]{1,0:T(8,128)S(1)} %add.293), channel_id=1, source_target_pairs={{0,1},{1,0},{2,3},{3,2},{4,5},{5,4},{6,7},{7,6},{8,9},{9,8},{10,11... | collective-permute-start | bytes 589832 | tf_op jit(solution)/shard_map/ppermute | solution.py:47
  496.2 11.7 %cholesky.634 = f32[128,128]{1,0:T(8,128)S(1)} custom-call(f32[128,128]{1,0:T(8,128)S(1)} %slice.207), custom_call_target="Cholesky" | custom-call | tf_op jit(solution)/shard_map/jit(cholesky)/cholesky | solution.py:79
  509.3 9.8 %custom-call.72 = f32[1,128,128]{1,2,0:T(8,128)S(1)} custom-call(f32[1,128,128]{2,1,0:T(8,128)S(1)} %fusion.42), custom_call_target="InvertDiagBlocksLowerTriangular" | custom-call | tf_op jit(solution)/shard_map/jit(_solve_triangular)/triangular_solve | solution.py:80
  520.4 11.7 %cholesky.645 = f32[128,128]{1,0:T(8,128)S(1)} custom-call(f32[128,128]{1,0:T(8,128)S(1)} %slice_subtract_fusion.6), custom_call_target="Cholesky" | custom-call | tf_op jit(solution)/shard_map/jit(cholesky)/cholesky | solution.py:82
  533.5 9.8 %custom-call.73 = f32[1,128,128]{1,2,0:T(8,128)S(1)} custom-call(f32[1,128,128]{2,1,0:T(8,128)S(1)} %fusion.43), custom_call_target="InvertDiagBlocksLowerTriangular" | custom-call | tf_op jit(solution)/shard_map/jit(_solve_triangular)/triangular_solve | solution.py:83
  (161 shorter events, 141.9 us)
Async XLA Ops:
  0.6 1.6 copy-start
  8.6 110.2 %all-to-all-start = ((bf16[128,16,1024]{2,1,0:T(8,128)(2,1)}), bf16[128,16,1024]{2,1,0:T(8,128)(2,1)}, u32[]{:S(2)}, u32[]{:S(2)}) async-start(bf16[128,16,1024]{2,1,0:T(8,128)(2,1)} %bitcast.118), calls=%async_computation | async-start | bytes 8388608 | tf_op jit(solution)/shard_map/all_to_all | solution.py:101
  118.7 10.7 %collective-permute-start = (bf16[2048,1024]{1,0:T(8,128)(2,1)}, bf16[2048,1024]{1,0:T(8,128)(2,1)S(1)}, u32[]{:S(2)}, u32[]{:S(2)}) collective-permute-start(bf16[2048,1024]{1,0:T(8,128)(2,1)} %bitcast.3), channel_id=1, source_target_pairs={{0,1},{1,0},{2,3},{3,2},{4,5},{5,4},{6,7},{7,6},{8,9},{9,8},{10,11... | collective-permute-start | bytes 12582920 | tf_op jit(solution)/shard_map/ppermute | solution.py:104
  140.1 2.0 copy-start.3
  345.5 4.7 copy-start.5
  348.3 2.0 copy-start.2
  350.3 10.1 %slice-start = ((s8[8388608]{0:T(1024)(128)(4,1)}), s8[4194304]{0:T(1024)(128)(4,1)S(1)}, s32[]{:S(2)}) async-start(s8[8388608]{0:T(1024)(128)(4,1)} %bitcast.112), calls=%async_computation.1 | async-start | bytes 8388608
  352.3 8.1 %slice-start.1 = ((s8[8388608]{0:T(1024)(128)(4,1)}), s8[4194304]{0:T(1024)(128)(4,1)S(1)}, s32[]{:S(2)}) async-start(s8[8388608]{0:T(1024)(128)(4,1)} %bitcast.112), calls=%async_computation.2 | async-start | bytes 8388608
  359.9 22.1 %collective-permute-start.1 = (f32[64,28,128]{2,0,1:T(8,128)S(1)}, f32[64,28,128]{2,0,1:T(8,128)}, u32[]{:S(2)}, u32[]{:S(2)}) collective-permute-start(f32[64,28,128]{2,0,1:T(8,128)S(1)} %constant_dynamic-slice_fusion.14), channel_id=1, source_target_pairs={{0,2},{2,0},{4,6},{6,4},{8,10},{10,8},{12,14},{14,12},{16,18},{18,... | collective-permute-start | bytes 2752520 | tf_op jit(solution)/shard_map/ppermute | solution.py:38
  365.7 21.9 %collective-permute-start.8 = (f32[64,28,128]{2,0,1:T(8,128)}, f32[64,28,128]{2,0,1:T(8,128)}, u32[]{:S(2)}, u32[]{:S(2)}) collective-permute-start(f32[64,28,128]{2,0,1:T(8,128)} %get-tuple-element.12), channel_id=1, source_target_pairs={{0,8},{2,10},{4,12},{6,14},{8,0},{10,2},{12,4},{14,6},{16,24},{18,... | collective-permute-start | bytes 2752520 | tf_op jit(solution)/shard_map/ppermute | solution.py:38
  366.4 21.3 %copy-start.4 = (f32[64,28,128]{2,0,1:T(8,128)S(1)}, f32[64,28,128]{2,0,1:T(8,128)}, u32[]{:S(2)}) copy-start(f32[64,28,128]{2,0,1:T(8,128)} %get-tuple-element.13) | copy-start | bytes 2752516
  383.3 14.2 %collective-permute-start.2 = (f32[32,28,128]{2,0,1:T(8,128)S(1)}, f32[32,28,128]{2,0,1:T(8,128)}, u32[]{:S(2)}, u32[]{:S(2)}) collective-permute-start(f32[32,28,128]{2,0,1:T(8,128)S(1)} %constant_dynamic-slice_fusion.13), channel_id=1, source_target_pairs={{0,8},{2,10},{4,12},{6,14},{8,0},{10,2},{12,4},{14,6},{16,24},{18,... | collective-permute-start | bytes 1376264 | tf_op jit(solution)/shard_map/ppermute | solution.py:38
  389.9 12.1 %collective-permute-start.9 = (f32[32,28,128]{2,1,0:T(8,128)S(1)}, f32[32,28,128]{2,1,0:T(8,128)S(1)}, u32[]{:S(2)}, u32[]{:S(2)}) collective-permute-start(f32[32,28,128]{2,1,0:T(8,128)S(1)} %constant_dynamic-slice_fusion.5), channel_id=1, source_target_pairs={{0,32},{2,34},{4,36},{6,38},{8,40},{10,42},{12,44},{14,46},{16,48}... | collective-permute-start | bytes 1376264 | tf_op jit(solution)/shard_map/ppermute | solution.py:38
  398.6 8.3 %collective-permute-start.3 = (f32[16,28,128]{2,0,1:T(8,128)S(1)}, f32[16,28,128]{2,0,1:T(8,128)S(1)}, u32[]{:S(2)}, u32[]{:S(2)}) collective-permute-start(f32[16,28,128]{2,0,1:T(8,128)S(1)} %constant_dynamic-slice_fusion.12), channel_id=1, source_target_pairs={{0,32},{2,34},{4,36},{6,38},{8,40},{10,42},{12,44},{14,46},{16,48}... | collective-permute-start | bytes 688136 | tf_op jit(solution)/shard_map/ppermute | solution.py:38
  402.1 7.4 %collective-permute-start.10 = (f32[16,28,128]{2,1,0:T(8,128)S(1)}, f32[16,28,128]{2,1,0:T(8,128)S(1)}, u32[]{:S(2)}, u32[]{:S(2)}) collective-permute-start(f32[16,28,128]{2,1,0:T(8,128)S(1)} %constant_dynamic-slice_fusion.4), channel_id=1, source_target_pairs={{0,2},{2,0},{4,6},{6,4},{8,10},{10,8},{12,14},{14,12},{16,18},{18,... | collective-permute-start | bytes 688136 | tf_op jit(solution)/shard_map/ppermute | solution.py:38
  407.0 6.1 %collective-permute-start.4 = (f32[8,28,128]{2,0,1:T(8,128)S(1)}, f32[8,28,128]{2,0,1:T(8,128)S(1)}, u32[]{:S(2)}, u32[]{:S(2)}) collective-permute-start(f32[8,28,128]{2,0,1:T(8,128)S(1)} %constant_dynamic-slice_fusion.11), channel_id=1, source_target_pairs={{0,4},{2,6},{4,0},{6,2},{8,12},{10,14},{12,8},{14,10},{16,20},{18,... | collective-permute-start | bytes 344072 | tf_op jit(solution)/shard_map/ppermute | solution.py:38
  409.6 5.8 %collective-permute-start.11 = (f32[8,28,128]{2,1,0:T(8,128)S(1)}, f32[8,28,128]{2,1,0:T(8,128)S(1)}, u32[]{:S(2)}, u32[]{:S(2)}) collective-permute-start(f32[8,28,128]{2,1,0:T(8,128)S(1)} %constant_dynamic-slice_fusion.3), channel_id=1, source_target_pairs={{0,16},{2,18},{4,20},{6,22},{8,24},{10,26},{12,28},{14,30},{16,0},... | collective-permute-start | bytes 344072 | tf_op jit(solution)/shard_map/ppermute | solution.py:38
  413.1 4.6 collective-permute-start.5
  415.4 4.4 collective-permute-start.12
  417.8 4.7 collective-permute-start.6
  419.9 6.0 %collective-permute-start.13 = (f32[2,28,128]{2,1,0:T(8,128)S(1)}, f32[2,28,128]{2,1,0:T(8,128)S(1)}, u32[]{:S(2)}, u32[]{:S(2)}) collective-permute-start(f32[2,28,128]{2,1,0:T(8,128)S(1)} %constant_dynamic-slice_fusion.1), channel_id=1, source_target_pairs={{0,4},{2,6},{4,0},{6,2},{8,12},{10,14},{12,8},{14,10},{16,20},{18,... | collective-permute-start | bytes 86024 | tf_op jit(solution)/shard_map/ppermute | solution.py:38
  422.5 6.7 %collective-permute-start.7 = (f32[1,28,128]{2,0,1:T(1,128)S(1)}, f32[1,28,128]{2,0,1:T(1,128)S(1)}, u32[]{:S(2)}, u32[]{:S(2)}) collective-permute-start(f32[1,28,128]{2,0,1:T(1,128)S(1)} %constant_dynamic-slice_fusion.8), channel_id=1, source_target_pairs={{0,128},{2,130},{4,132},{6,134},{8,136},{10,138},{12,140},{14,142}... | collective-permute-start | bytes 43016 | tf_op jit(solution)/shard_map/ppermute | solution.py:38
  425.9 6.6 %collective-permute-start.14 = (f32[1,28,128]{2,1,0:T(8,128)S(1)}, f32[1,28,128]{2,1,0:T(8,128)S(1)}, u32[]{:S(2)}, u32[]{:S(2)}) collective-permute-start(f32[1,28,128]{2,1,0:T(8,128)S(1)} %constant_dynamic-slice_fusion), channel_id=1, source_target_pairs={{0,128},{2,130},{4,132},{6,134},{8,136},{10,138},{12,140},{14,142}... | collective-permute-start | bytes 43016 | tf_op jit(solution)/shard_map/ppermute | solution.py:38
  433.1 4.9 collective-permute-start.15
  438.1 4.6 collective-permute-start.16
  442.7 4.6 collective-permute-start.17
  447.3 6.1 %collective-permute-start.18 = (f32[384,128]{1,0:T(8,128)S(1)}, f32[384,128]{1,0:T(8,128)S(1)}, u32[]{:S(2)}, u32[]{:S(2)}) collective-permute-start(f32[384,128]{1,0:T(8,128)S(1)} %add.289), channel_id=1, source_target_pairs={{0,4},{2,6},{4,0},{6,2},{8,12},{10,14},{12,8},{14,10},{16,20},{18,... | collective-permute-start | bytes 589832 | tf_op jit(solution)/shard_map/ppermute | solution.py:46
  453.4 91.0 %copy-start.1 = (bf16[128,8,1024]{2,1,0:T(8,128)(2,1)S(1)}, bf16[128,8,1024]{2,1,0:T(8,128)(2,1)}, u32[]{:S(2)}) copy-start(bf16[128,8,1024]{2,1,0:T(8,128)(2,1)} %param.8) | copy-start | bytes 6291460
  453.5 6.1 %collective-permute-start.19 = (f32[384,128]{1,0:T(8,128)S(1)}, f32[384,128]{1,0:T(8,128)S(1)}, u32[]{:S(2)}, u32[]{:S(2)}) collective-permute-start(f32[384,128]{1,0:T(8,128)S(1)} %add.290), channel_id=1, source_target_pairs={{0,16},{2,18},{4,20},{6,22},{8,24},{10,26},{12,28},{14,30},{16,0},... | collective-permute-start | bytes 589832 | tf_op jit(solution)/shard_map/ppermute | solution.py:46
  459.6 7.6 %collective-permute-start.20 = (f32[384,128]{1,0:T(8,128)S(1)}, f32[384,128]{1,0:T(8,128)S(1)}, u32[]{:S(2)}, u32[]{:S(2)}) collective-permute-start(f32[384,128]{1,0:T(8,128)S(1)} %add.291), channel_id=1, source_target_pairs={{0,64},{2,66},{4,68},{6,70},{8,72},{10,74},{12,76},{14,78},{16,80}... | collective-permute-start | bytes 589832 | tf_op jit(solution)/shard_map/ppermute | solution.py:46
  467.2 9.7 %collective-permute-start.21 = (f32[384,128]{1,0:T(8,128)S(1)}, f32[384,128]{1,0:T(8,128)S(1)}, u32[]{:S(2)}, u32[]{:S(2)}) collective-permute-start(f32[384,128]{1,0:T(8,128)S(1)} %add.292), channel_id=1, source_target_pairs={{0,128},{2,130},{4,132},{6,134},{8,136},{10,138},{12,140},{14,142}... | collective-permute-start | bytes 589832 | tf_op jit(solution)/shard_map/ppermute | solution.py:46
  476.9 19.3 %collective-permute-start.22 = (f32[384,128]{1,0:T(8,128)S(1)}, f32[384,128]{1,0:T(8,128)S(1)}, u32[]{:S(2)}, u32[]{:S(2)}) collective-permute-start(f32[384,128]{1,0:T(8,128)S(1)} %add.293), channel_id=1, source_target_pairs={{0,1},{1,0},{2,3},{3,2},{4,5},{5,4},{6,7},{7,6},{8,9},{9,8},{10,11... | collective-permute-start | bytes 589832 | tf_op jit(solution)/shard_map/ppermute | solution.py:47

commit v10 on v9

--- a/solution.py
+++ b/solution.py
@@ -109,16 +109,17 @@
     diag_mean = jnp.sum(jnp.where(on_diag, gram_mat, 0.0)) / hid_width
     damped = jnp.where(on_diag, gram_mat + (damping * diag_mean + jitter), gram_mat)
     whitening = jnp.linalg.cholesky(damped, symmetrize_input=False)
-    test_mat = jnp.dot(
-        whitening, omega[0].astype(jnp.float32), precision=lax.Precision.HIGHEST
-    ).astype(jnp.bfloat16)
     down_half = down_weight[0]
     half_cols = down_half.shape[1]
     def term(start, width):
-        return contract(test_mat[:, start:start + width], down_half)
+        test_part = jnp.dot(
+            whitening, omega[0, :, start:start + width].astype(jnp.float32),
+            precision=lax.Precision.HIGHEST,
+        ).astype(jnp.bfloat16)
+        return contract(test_part, down_half)
 
     orders = bit_orders(n_exp, 2)
-    sketch = scatter_sum(term, test_mat.shape[1], half_cols, orders)
+    sketch = scatter_sum(term, omega.shape[2], half_cols, orders)
     small_gram = all_sum(lower_blocks(sketch), orders[0])
     basis_rows = right_solve_chol(small_gram, sketch) * math.sqrt(half_cols * n_dp)
     own_rows = lax.dynamic_slice_in_dim(

time: 553 us -> 550 us (level)
  transfers between devices with their start and end apart: 24 -> 24, of which waited for: 17 -> 18; matrix products, arithmetic and copies ran while one was open for 8% -> 8% of each run, Pallas kernels for 0% -> 0%
where the time goes in v10:
time: 550 us; the launch traced here: 542 us
  other arithmetic  229 us (42%)
  waiting for transfers between devices  144 us (26%)
  starting transfers between devices  69.5 us (13%)
  matrix products  56.3 us (10%)
  local copies, waits for them, and re-layouts  35.1 us (6%)
  between operations  7.36 us (1%)
    another operation x30, other arithmetic, local(): whitening = jnp.linalg.cholesky(damped, symmetrize_input=False)  172 us
    all_to_all x1, waiting for transfers between devices, local(): lax.all_to_all(outgoing, 'expert', split_axis=0, concat_axis=0, tiled=True)  72 us
    ppermute x14, waiting for transfers between devices, scatter_sum(): part = keep + lax.ppermute(send, 'expert', xor_pairs(n_exp, 1 << b))  37.7 us
    ppermute x7, waiting for transfers between devices, all_sum(): x = x + lax.ppermute(x, 'expert', xor_pairs(n_exp, 1 << b))  34.7 us
    dot_general x5, matrix products, contract(): lax.dot_general(left, right, (((0,), (0,)), ((), ())), preferred_element_...  26.5 us
    ppermute x14, starting transfers between devices, scatter_sum(): part = keep + lax.ppermute(send, 'expert', xor_pairs(n_exp, 1 << b))  23.9 us
    another operation x14, matrix products, local(): whitening = jnp.linalg.cholesky(damped, symmetrize_input=False)  23.3 us
    dot_general x2, local copies, waits for them, and re-layouts, contract(): lax.dot_general(left, right, (((0,), (0,)), ((), ())), preferred_element_...  21.3 us
  transfers between devices with their start and end apart: 24, of which 18 were waited for; matrix products, arithmetic and copies ran while one was open for 8% of the time, Pallas kernels for 0%

profile of v10, /device:TPU:1, one launch (start us, length us, event | category | flops | bytes accessed | tf_op | source)
XLA Modules:
  0.0 542.2 jit_solution(11669465483150114776)
XLA Ops:
  2.3 6.3 %fusion.3 = bf16[2048,1024]{1,0:T(8,128)(2,1)} fusion(s32[1024]{0:T(1024)S(1)} %eq.22, bf16[128,8,1024]{2,1,0:T(8,128)(2,1)S(1)} %copy-done), kind=kOutput, calls=%fused_computation.10 | convolution fusion | flops 4299161600 | bytes 6295552 | tf_op jit(solution)/shard_map/dot_general | solution.py:13
  8.6 16.9 %all-to-all-start = ((bf16[128,16,1024]{2,1,0:T(8,128)(2,1)}), bf16[128,16,1024]{2,1,0:T(8,128)(2,1)}, u32[]{:S(2)}, u32[]{:S(2)}) async-start(bf16[128,16,1024]{2,1,0:T(8,128)(2,1)} %bitcast.122), calls=%async_computation | async-start | bytes 8388608 | tf_op jit(solution)/shard_map/all_to_all | solution.py:101
  25.4 10.4 %copy.30 = bf16[3584,1024]{1,0:T(8,128)(2,1)} copy(bf16[3584,1024]{0,1:T(8,128)(2,1)} %bitcast.118) | data formatting | bytes 14680064 | tf_op jit(solution)/shard_map/dot_general | solution.py:13
  35.8 10.9 %dot_general.54 = bf16[2,2,2,2,2,2,2,28,1024]{8,7,6,5,4,3,2,1,0:T(8,128)(2,1)} reshape(bf16[3584,1024]{1,0:T(8,128)(2,1)} %copy.30) | data formatting | bytes 14680064 | tf_op jit(solution)/shard_map/dot_general | solution.py:13
  46.7 72.0 %all-to-all-done = bf16[128,16,1024]{2,1,0:T(8,128)(2,1)} async-done(((bf16[128,16,1024]{2,1,0:T(8,128)(2,1)}), bf16[128,16,1024]{2,1,0:T(8,128)(2,1)}, u32[]{:S(2)}, u32[]{:S(2)}) %all-to-all-start) | async-done | bytes 4194336 | tf_op jit(solution)/shard_map/all_to_all | solution.py:101
  121.9 7.6 %fusion.78 = f32[1024,1024,1]{1,0,2:T(8,128)S(1)} fusion(bf16[128,16,1024]{2,1,0:T(8,128)(2,1)} %all-to-all-done), kind=kOutput, calls=%fused_computation.167 | convolution fusion | flops 4294967296 | bytes 8388608 | tf_op jit(solution)/shard_map/dot_general | solution.py:13
  129.5 7.4 %select_reduce_fusion = (f32[]{:T(128)}, f32[1024,1024]{1,0:T(8,128)}) fusion(bf16[2048,1024]{1,0:T(8,128)(2,1)S(1)} %collective-permute-done, f32[1024,1024,1]{1,0,2:T(8,128)S(1)} %fusion.78), kind=kOutput, calls=%fused_computation.6 | convolution fusion | flops 4300210176 | bytes 12582916 | tf_op jit(solution)/shard_map/dot_general | solution.py:13
  142.1 11.7 %cholesky.242 = f32[128,128]{1,0:T(8,128)S(1)} custom-call(f32[128,128]{1,0:T(8,128)S(1)} %cholesky.654), custom_call_target="Cholesky" | custom-call | tf_op jit(solution)/shard_map/jit(cholesky)/cholesky | solution.py:111
  153.8 9.8 %custom-call.64 = f32[1,128,128]{1,2,0:T(8,128)S(1)} custom-call(f32[1,128,128]{2,1,0:T(8,128)S(1)} %get-tuple-element.35), custom_call_target="InvertDiagBlocksLowerTriangular" | custom-call | tf_op jit(solution)/shard_map/jit(cholesky)/cholesky | solution.py:111
  170.1 11.7 %cholesky.265 = f32[128,128]{1,0:T(8,128)S(1)} custom-call(f32[128,128]{1,0:T(8,128)S(1)} %cholesky.658), custom_call_target="Cholesky" | custom-call | tf_op jit(solution)/shard_map/jit(cholesky)/cholesky | solution.py:111
  182.5 10.2 %custom-call.65 = f32[1,128,128]{1,2,0:T(8,128)S(1)} custom-call(f32[1,128,128]{2,1,0:T(8,128)S(1)} %get-tuple-element.32), custom_call_target="InvertDiagBlocksLowerTriangular" | custom-call | tf_op jit(solution)/shard_map/jit(cholesky)/cholesky | solution.py:111
  196.0 11.7 %cholesky.506 = f32[128,128]{1,0:T(8,128)S(1)} custom-call(f32[128,128]{1,0:T(8,128)S(1)} %cholesky.663), custom_call_target="Cholesky" | custom-call | tf_op jit(solution)/shard_map/jit(cholesky)/cholesky | solution.py:111
  209.0 9.8 %custom-call.66 = f32[1,128,128]{1,2,0:T(8,128)S(1)} custom-call(f32[1,128,128]{2,1,0:T(8,128)S(1)} %get-tuple-element.29), custom_call_target="InvertDiagBlocksLowerTriangular" | custom-call | tf_op jit(solution)/shard_map/jit(cholesky)/cholesky | solution.py:111
  222.4 11.9 %cholesky.525 = f32[128,128]{1,0:T(8,128)S(1)} custom-call(f32[128,128]{1,0:T(8,128)S(1)} %cholesky.668), custom_call_target="Cholesky" | custom-call | tf_op jit(solution)/shard_map/jit(cholesky)/cholesky | solution.py:111
  235.6 9.8 %custom-call.67 = f32[1,128,128]{1,2,0:T(8,128)S(1)} custom-call(f32[1,128,128]{2,1,0:T(8,128)S(1)} %get-tuple-element.26), custom_call_target="InvertDiagBlocksLowerTriangular" | custom-call | tf_op jit(solution)/shard_map/jit(cholesky)/cholesky | solution.py:111
  248.8 11.7 %cholesky.544 = f32[128,128]{1,0:T(8,128)S(1)} custom-call(f32[128,128]{1,0:T(8,128)S(1)} %cholesky.673), custom_call_target="Cholesky" | custom-call | tf_op jit(solution)/shard_map/jit(cholesky)/cholesky | solution.py:111
  261.9 9.8 %custom-call.68 = f32[1,128,128]{1,2,0:T(8,128)S(1)} custom-call(f32[1,128,128]{2,1,0:T(8,128)S(1)} %get-tuple-element.23), custom_call_target="InvertDiagBlocksLowerTriangular" | custom-call | tf_op jit(solution)/shard_map/jit(cholesky)/cholesky | solution.py:111
  275.3 11.7 %cholesky.564 = f32[128,128]{1,0:T(8,128)S(1)} custom-call(f32[128,128]{1,0:T(8,128)S(1)} %cholesky.678), custom_call_target="Cholesky" | custom-call | tf_op jit(solution)/shard_map/jit(cholesky)/cholesky | solution.py:111
  288.3 9.8 %custom-call.69 = f32[1,128,128]{1,2,0:T(8,128)S(1)} custom-call(f32[1,128,128]{2,1,0:T(8,128)S(1)} %get-tuple-element.20), custom_call_target="InvertDiagBlocksLowerTriangular" | custom-call | tf_op jit(solution)/shard_map/jit(cholesky)/cholesky | solution.py:111
  301.1 11.7 %cholesky.584 = f32[128,128]{1,0:T(8,128)S(1)} custom-call(f32[128,128]{1,0:T(8,128)S(1)} %cholesky.683), custom_call_target="Cholesky" | custom-call | tf_op jit(solution)/shard_map/jit(cholesky)/cholesky | solution.py:111
  314.1 10.2 %custom-call.70 = f32[1,128,128]{1,2,0:T(8,128)S(1)} custom-call(f32[1,128,128]{2,1,0:T(8,128)S(1)} %get-tuple-element.17), custom_call_target="InvertDiagBlocksLowerTriangular" | custom-call | tf_op jit(solution)/shard_map/jit(cholesky)/cholesky | solution.py:111
  326.9 11.7 %cholesky.602 = f32[128,128]{1,0:T(8,128)S(1)} custom-call(f32[128,128]{1,0:T(8,128)S(1)} %slice_subtract_fusion.7), custom_call_target="Cholesky" | custom-call | tf_op jit(solution)/shard_map/jit(cholesky)/cholesky | solution.py:111
  363.3 15.6 %collective-permute-done.1 = f32[64,28,128]{2,0,1:T(8,128)} collective-permute-done((f32[64,28,128]{2,0,1:T(8,128)S(1)}, f32[64,28,128]{2,0,1:T(8,128)}, u32[]{:S(2)}, u32[]{:S(2)}) %collective-permute-start.1) | collective-permute-done | bytes 917536 | tf_op jit(solution)/shard_map/ppermute | solution.py:38
  388.5 5.9 %collective-permute-done.2 = f32[32,28,128]{2,0,1:T(8,128)} collective-permute-done((f32[32,28,128]{2,0,1:T(8,128)S(1)}, f32[32,28,128]{2,0,1:T(8,128)}, u32[]{:S(2)}, u32[]{:S(2)}) %collective-permute-start.2) | collective-permute-done | bytes 458784 | tf_op jit(solution)/shard_map/ppermute | solution.py:38
  445.5 4.7 collective-permute-done.18
  457.5 6.5 %collective-permute-done.20 = f32[384,128]{1,0:T(8,128)S(1)} collective-permute-done((f32[384,128]{1,0:T(8,128)S(1)}, f32[384,128]{1,0:T(8,128)S(1)}, u32[]{:S(2)}, u32[]{:S(2)}) %collective-permute-start.20) | collective-permute-done | bytes 196640 | tf_op jit(solution)/shard_map/ppermute | solution.py:46
  466.2 7.7 %collective-permute-done.21 = f32[384,128]{1,0:T(8,128)S(1)} collective-permute-done((f32[384,128]{1,0:T(8,128)S(1)}, f32[384,128]{1,0:T(8,128)S(1)}, u32[]{:S(2)}, u32[]{:S(2)}) %collective-permute-start.21) | collective-permute-done | bytes 196640 | tf_op jit(solution)/shard_map/ppermute | solution.py:46
  473.9 16.4 %collective-permute-start.22 = (f32[384,128]{1,0:T(8,128)S(1)}, f32[384,128]{1,0:T(8,128)S(1)}, u32[]{:S(2)}, u32[]{:S(2)}) collective-permute-start(f32[384,128]{1,0:T(8,128)S(1)} %add.293), channel_id=1, source_target_pairs={{0,1},{1,0},{2,3},{3,2},{4,5},{5,4},{6,7},{7,6},{8,9},{9,8},{10,11... | collective-permute-start | bytes 589832 | tf_op jit(solution)/shard_map/ppermute | solution.py:47
  493.6 11.7 %cholesky.634 = f32[128,128]{1,0:T(8,128)S(1)} custom-call(f32[128,128]{1,0:T(8,128)S(1)} %slice.205), custom_call_target="Cholesky" | custom-call | tf_op jit(solution)/shard_map/jit(cholesky)/cholesky | solution.py:79
  506.6 9.8 %custom-call.72 = f32[1,128,128]{1,2,0:T(8,128)S(1)} custom-call(f32[1,128,128]{2,1,0:T(8,128)S(1)} %fusion.47), custom_call_target="InvertDiagBlocksLowerTriangular" | custom-call | tf_op jit(solution)/shard_map/jit(_solve_triangular)/triangular_solve | solution.py:80
  517.7 11.7 %cholesky.645 = f32[128,128]{1,0:T(8,128)S(1)} custom-call(f32[128,128]{1,0:T(8,128)S(1)} %slice_subtract_fusion.6), custom_call_target="Cholesky" | custom-call | tf_op jit(solution)/shard_map/jit(cholesky)/cholesky | solution.py:82
  530.8 9.8 %custom-call.73 = f32[1,128,128]{1,2,0:T(8,128)S(1)} custom-call(f32[1,128,128]{2,1,0:T(8,128)S(1)} %fusion.48), custom_call_target="InvertDiagBlocksLowerTriangular" | custom-call | tf_op jit(solution)/shard_map/jit(_solve_triangular)/triangular_solve | solution.py:83
  (162 shorter events, 140.3 us)
Async XLA Ops:
  0.6 1.6 copy-start
  8.6 110.2 %all-to-all-start = ((bf16[128,16,1024]{2,1,0:T(8,128)(2,1)}), bf16[128,16,1024]{2,1,0:T(8,128)(2,1)}, u32[]{:S(2)}, u32[]{:S(2)}) async-start(bf16[128,16,1024]{2,1,0:T(8,128)(2,1)} %bitcast.122), calls=%async_computation | async-start | bytes 8388608 | tf_op jit(solution)/shard_map/all_to_all | solution.py:101
  118.7 10.7 %collective-permute-start = (bf16[2048,1024]{1,0:T(8,128)(2,1)}, bf16[2048,1024]{1,0:T(8,128)(2,1)S(1)}, u32[]{:S(2)}, u32[]{:S(2)}) collective-permute-start(bf16[2048,1024]{1,0:T(8,128)(2,1)} %bitcast.3), channel_id=1, source_target_pairs={{0,1},{1,0},{2,3},{3,2},{4,5},{5,4},{6,7},{7,6},{8,9},{9,8},{10,11... | collective-permute-start | bytes 12582920 | tf_op jit(solution)/shard_map/ppermute | solution.py:104
  140.1 2.0 copy-start.3
  345.5 2.9 copy-start.5
  345.5 7.0 %slice-start = ((s8[8388608]{0:T(1024)(128)(4,1)}), s8[4194304]{0:T(1024)(128)(4,1)S(1)}, s32[]{:S(2)}) async-start(s8[8388608]{0:T(1024)(128)(4,1)} %bitcast.116), calls=%async_computation.1 | async-start | bytes 8388608
  348.4 2.1 copy-start.2
  348.4 4.1 slice-start.1
  356.7 22.1 %collective-permute-start.1 = (f32[64,28,128]{2,0,1:T(8,128)S(1)}, f32[64,28,128]{2,0,1:T(8,128)}, u32[]{:S(2)}, u32[]{:S(2)}) collective-permute-start(f32[64,28,128]{2,0,1:T(8,128)S(1)} %constant_dynamic-slice_fusion.14), channel_id=1, source_target_pairs={{0,2},{2,0},{4,6},{6,4},{8,10},{10,8},{12,14},{14,12},{16,18},{18,... | collective-permute-start | bytes 2752520 | tf_op jit(solution)/shard_map/ppermute | solution.py:38
  362.6 21.9 %collective-permute-start.8 = (f32[64,28,128]{2,0,1:T(8,128)}, f32[64,28,128]{2,0,1:T(8,128)}, u32[]{:S(2)}, u32[]{:S(2)}) collective-permute-start(f32[64,28,128]{2,0,1:T(8,128)} %get-tuple-element.12), channel_id=1, source_target_pairs={{0,8},{2,10},{4,12},{6,14},{8,0},{10,2},{12,4},{14,6},{16,24},{18,... | collective-permute-start | bytes 2752520 | tf_op jit(solution)/shard_map/ppermute | solution.py:38
  363.3 21.3 %copy-start.4 = (f32[64,28,128]{2,0,1:T(8,128)S(1)}, f32[64,28,128]{2,0,1:T(8,128)}, u32[]{:S(2)}) copy-start(f32[64,28,128]{2,0,1:T(8,128)} %get-tuple-element.13) | copy-start | bytes 2752516
  380.2 14.2 %collective-permute-start.2 = (f32[32,28,128]{2,0,1:T(8,128)S(1)}, f32[32,28,128]{2,0,1:T(8,128)}, u32[]{:S(2)}, u32[]{:S(2)}) collective-permute-start(f32[32,28,128]{2,0,1:T(8,128)S(1)} %constant_dynamic-slice_fusion.13), channel_id=1, source_target_pairs={{0,8},{2,10},{4,12},{6,14},{8,0},{10,2},{12,4},{14,6},{16,24},{18,... | collective-permute-start | bytes 1376264 | tf_op jit(solution)/shard_map/ppermute | solution.py:38
  386.8 12.0 %collective-permute-start.9 = (f32[32,28,128]{2,1,0:T(8,128)S(1)}, f32[32,28,128]{2,1,0:T(8,128)S(1)}, u32[]{:S(2)}, u32[]{:S(2)}) collective-permute-start(f32[32,28,128]{2,1,0:T(8,128)S(1)} %constant_dynamic-slice_fusion.5), channel_id=1, source_target_pairs={{0,32},{2,34},{4,36},{6,38},{8,40},{10,42},{12,44},{14,46},{16,48}... | collective-permute-start | bytes 1376264 | tf_op jit(solution)/shard_map/ppermute | solution.py:38
  395.5 8.2 %collective-permute-start.3 = (f32[16,28,128]{2,0,1:T(8,128)S(1)}, f32[16,28,128]{2,0,1:T(8,128)S(1)}, u32[]{:S(2)}, u32[]{:S(2)}) collective-permute-start(f32[16,28,128]{2,0,1:T(8,128)S(1)} %constant_dynamic-slice_fusion.12), channel_id=1, source_target_pairs={{0,32},{2,34},{4,36},{6,38},{8,40},{10,42},{12,44},{14,46},{16,48}... | collective-permute-start | bytes 688136 | tf_op jit(solution)/shard_map/ppermute | solution.py:38
  398.9 7.6 %collective-permute-start.10 = (f32[16,28,128]{2,1,0:T(8,128)S(1)}, f32[16,28,128]{2,1,0:T(8,128)S(1)}, u32[]{:S(2)}, u32[]{:S(2)}) collective-permute-start(f32[16,28,128]{2,1,0:T(8,128)S(1)} %constant_dynamic-slice_fusion.4), channel_id=1, source_target_pairs={{0,2},{2,0},{4,6},{6,4},{8,10},{10,8},{12,14},{14,12},{16,18},{18,... | collective-permute-start | bytes 688136 | tf_op jit(solution)/shard_map/ppermute | solution.py:38
  403.8 6.5 %collective-permute-start.4 = (f32[8,28,128]{2,0,1:T(8,128)S(1)}, f32[8,28,128]{2,0,1:T(8,128)S(1)}, u32[]{:S(2)}, u32[]{:S(2)}) collective-permute-start(f32[8,28,128]{2,0,1:T(8,128)S(1)} %constant_dynamic-slice_fusion.11), channel_id=1, source_target_pairs={{0,4},{2,6},{4,0},{6,2},{8,12},{10,14},{12,8},{14,10},{16,20},{18,... | collective-permute-start | bytes 344072 | tf_op jit(solution)/shard_map/ppermute | solution.py:38
  406.6 5.8 %collective-permute-start.11 = (f32[8,28,128]{2,1,0:T(8,128)S(1)}, f32[8,28,128]{2,1,0:T(8,128)S(1)}, u32[]{:S(2)}, u32[]{:S(2)}) collective-permute-start(f32[8,28,128]{2,1,0:T(8,128)S(1)} %constant_dynamic-slice_fusion.3), channel_id=1, source_target_pairs={{0,16},{2,18},{4,20},{6,22},{8,24},{10,26},{12,28},{14,30},{16,0},... | collective-permute-start | bytes 344072 | tf_op jit(solution)/shard_map/ppermute | solution.py:38
  410.4 4.6 collective-permute-start.5
  412.5 4.4 collective-permute-start.12
  415.0 4.5 collective-permute-start.6
  416.9 5.7 %collective-permute-start.13 = (f32[2,28,128]{2,1,0:T(8,128)S(1)}, f32[2,28,128]{2,1,0:T(8,128)S(1)}, u32[]{:S(2)}, u32[]{:S(2)}) collective-permute-start(f32[2,28,128]{2,1,0:T(8,128)S(1)} %constant_dynamic-slice_fusion.1), channel_id=1, source_target_pairs={{0,4},{2,6},{4,0},{6,2},{8,12},{10,14},{12,8},{14,10},{16,20},{18,... | collective-permute-start | bytes 86024 | tf_op jit(solution)/shard_map/ppermute | solution.py:38
  419.6 6.6 %collective-permute-start.7 = (f32[1,28,128]{2,0,1:T(1,128)S(1)}, f32[1,28,128]{2,0,1:T(1,128)S(1)}, u32[]{:S(2)}, u32[]{:S(2)}) collective-permute-start(f32[1,28,128]{2,0,1:T(1,128)S(1)} %constant_dynamic-slice_fusion.8), channel_id=1, source_target_pairs={{0,128},{2,130},{4,132},{6,134},{8,136},{10,138},{12,140},{14,142}... | collective-permute-start | bytes 43016 | tf_op jit(solution)/shard_map/ppermute | solution.py:38
  422.7 6.6 %collective-permute-start.14 = (f32[1,28,128]{2,1,0:T(8,128)S(1)}, f32[1,28,128]{2,1,0:T(8,128)S(1)}, u32[]{:S(2)}, u32[]{:S(2)}) collective-permute-start(f32[1,28,128]{2,1,0:T(8,128)S(1)} %constant_dynamic-slice_fusion), channel_id=1, source_target_pairs={{0,128},{2,130},{4,132},{6,134},{8,136},{10,138},{12,140},{14,142}... | collective-permute-start | bytes 43016 | tf_op jit(solution)/shard_map/ppermute | solution.py:38
  429.9 4.9 collective-permute-start.15
  434.8 4.6 collective-permute-start.16
  439.5 4.6 collective-permute-start.17
  444.1 6.1 %collective-permute-start.18 = (f32[384,128]{1,0:T(8,128)S(1)}, f32[384,128]{1,0:T(8,128)S(1)}, u32[]{:S(2)}, u32[]{:S(2)}) collective-permute-start(f32[384,128]{1,0:T(8,128)S(1)} %add.289), channel_id=1, source_target_pairs={{0,4},{2,6},{4,0},{6,2},{8,12},{10,14},{12,8},{14,10},{16,20},{18,... | collective-permute-start | bytes 589832 | tf_op jit(solution)/shard_map/ppermute | solution.py:46
  450.2 91.6 %copy-start.1 = (bf16[128,8,1024]{2,1,0:T(8,128)(2,1)S(1)}, bf16[128,8,1024]{2,1,0:T(8,128)(2,1)}, u32[]{:S(2)}) copy-start(bf16[128,8,1024]{2,1,0:T(8,128)(2,1)} %param.8) | copy-start | bytes 6291460
  450.2 6.1 %collective-permute-start.19 = (f32[384,128]{1,0:T(8,128)S(1)}, f32[384,128]{1,0:T(8,128)S(1)}, u32[]{:S(2)}, u32[]{:S(2)}) collective-permute-start(f32[384,128]{1,0:T(8,128)S(1)} %add.290), channel_id=1, source_target_pairs={{0,16},{2,18},{4,20},{6,22},{8,24},{10,26},{12,28},{14,30},{16,0},... | collective-permute-start | bytes 589832 | tf_op jit(solution)/shard_map/ppermute | solution.py:46
  456.4 7.6 %collective-permute-start.20 = (f32[384,128]{1,0:T(8,128)S(1)}, f32[384,128]{1,0:T(8,128)S(1)}, u32[]{:S(2)}, u32[]{:S(2)}) collective-permute-start(f32[384,128]{1,0:T(8,128)S(1)} %add.291), channel_id=1, source_target_pairs={{0,64},{2,66},{4,68},{6,70},{8,72},{10,74},{12,76},{14,78},{16,80}... | collective-permute-start | bytes 589832 | tf_op jit(solution)/shard_map/ppermute | solution.py:46
  464.0 9.9 %collective-permute-start.21 = (f32[384,128]{1,0:T(8,128)S(1)}, f32[384,128]{1,0:T(8,128)S(1)}, u32[]{:S(2)}, u32[]{:S(2)}) collective-permute-start(f32[384,128]{1,0:T(8,128)S(1)} %add.292), channel_id=1, source_target_pairs={{0,128},{2,130},{4,132},{6,134},{8,136},{10,138},{12,140},{14,142}... | collective-permute-start | bytes 589832 | tf_op jit(solution)/shard_map/ppermute | solution.py:46
  473.9 19.6 %collective-permute-start.22 = (f32[384,128]{1,0:T(8,128)S(1)}, f32[384,128]{1,0:T(8,128)S(1)}, u32[]{:S(2)}, u32[]{:S(2)}) collective-permute-start(f32[384,128]{1,0:T(8,128)S(1)} %add.293), channel_id=1, source_target_pairs={{0,1},{1,0},{2,3},{3,2},{4,5},{5,4},{6,7},{7,6},{8,9},{9,8},{10,11... | collective-permute-start | bytes 589832 | tf_op jit(solution)/shard_map/ppermute | solution.py:47
